TPU v7x, 256 devices: a whole 4x4x8 slice. The times are simulated.
256 devices in a mesh: tile: 16 (over z, core), tensor: 16 (over y, x).
Axes of the slice: x: 4, y: 4, z: 8, core: 2. Of those that a mesh axis runs over, the one named last changes fastest.
Arguments:
- image_hidden: bfloat16 [8, 32, 32, 3072], P(None, 'tile', 'tensor'), may hold values from -6 to 6
- text_hidden: bfloat16 [8, 512, 3072], P(None, ('tile', 'tensor')), may hold values from -6 to 6
- latents: float32 [8, 32, 2048], P(None, 'tile', 'tensor'), may hold values from -6 to 6
- step_index: int32 [8], replicated, may hold values from 0 to 27
- anchor: int32 [8, 2], replicated, may hold values from 0 to 63
- text_len: int32 [8], replicated, may hold values from 64 to 512
- mod_image: float32 [8, 3, 3072], replicated, may hold values from -3 to 3
- mod_text: float32 [8, 3, 3072], replicated, may hold values from -3 to 3
- mod_mlp: float32 [8, 3, 3072], replicated, may hold values from -3 to 3
- mod_final: float32 [8, 2, 3072], replicated, may hold values from -3 to 3
- qkv_image: bfloat16 [3072, 3, 2048], P(None, None, 'tensor'), may hold values from -0.109375 to 0.109375
- qkv_text: bfloat16 [3072, 3, 2048], P(None, None, 'tensor'), may hold values from -0.109375 to 0.109375
- proj_image: bfloat16 [2048, 3072], P('tensor'), may hold values from -0.125 to 0.125
- proj_text: bfloat16 [2048, 3072], P('tensor'), may hold values from -0.125 to 0.125
- qk_gain: float32 [2, 2, 128], replicated, may hold values from 0.5 to 10
- mlp_expand: bfloat16 [3072, 6144], P(None, 'tensor'), may hold values from -0.109375 to 0.109375
- mlp_reduce: bfloat16 [6144, 3072], P('tensor'), may hold values from -0.078125 to 0.078125
- final_weight: bfloat16 [3072, 64], replicated, may hold values from -0.109375 to 0.109375
Outputs:
- image_out: bfloat16 [8, 32, 32, 3072], P(None, 'tile', 'tensor')
- text_out: bfloat16 [8, 512, 3072], P(None, ('tile', 'tensor'))
- latents_ext: float32 [8, 64, 2048], P(None, 'tile', 'tensor')
Inputs may be any that keep to these rules, and one draw needn't show every extreme that they name: text_len gives each request's live text tokens; slots at or past it take no part as keys. step_index is a step of the 28-step plan.
All inputs are finite; a program needn't handle non-finite values.
Results may differ from a plain program's by a relative error of at most 0.0085.
The roundings to bfloat16 on the way count: a program that leaves them out, or rounds other values in their place, can miss the bound.
Values may be sent and summed in bfloat16 or wider, within the bound.
No kernel may reach another device: no remote copies, remote signals or barrier semaphores. Data moves between devices by JAX's collectives and lax.ppermute only.
A program may use at most 128 MiB of HBM per device.

v0:
```python
import math

import jax
import jax.numpy as jnp
from jax import lax
from jax.sharding import PartitionSpec as P

HEAD_DIM = 128
GRID = 32
NSTEPS = 28


norm_eps = 1e-06
time_shift = 3.0


def padded(value, sides, width):
    for axis, dim in sides:
        size, length = (lax.axis_size(axis), value.shape[dim])
        up = [(i, (i + 1) % size) for i in range(size - 1)]
        down = [(j, i) for i, j in up]
        last = lax.slice_in_dim(value, length - width, length, axis=dim)
        leading = lax.slice_in_dim(value, 0, width, axis=dim)
        before = lax.ppermute(last, axis, up)
        after = lax.ppermute(leading, axis, down)
        value = jnp.concatenate([before, value, after], axis=dim)
    return value


def layer_norm(values):
    average = jnp.mean(values, -1, keepdims=True)
    centred = values - average
    spread = jnp.mean(centred * centred, -1, keepdims=True)
    return centred * lax.rsqrt(spread + norm_eps)


def modulate(hidden, shift, stretch):
    normed = layer_norm(hidden.astype(jnp.float32))
    return ((1.0 + stretch) * normed + shift).astype(jnp.bfloat16)


def rope_tables(row_ids, col_ids):
    pair_index = jnp.arange(64, dtype=jnp.int32)
    row_rank = (pair_index - 8).astype(jnp.float32)
    col_rank = (pair_index - 36).astype(jnp.float32)
    log_base = math.log(10000.0)
    row_freq = jnp.where(
        (pair_index >= 8) & (pair_index < 36), jnp.exp(-2.0 * row_rank / 56.0 * log_base), 0.0
    )
    col_freq = jnp.where(pair_index >= 36, jnp.exp(-2.0 * col_rank / 56.0 * log_base), 0.0)
    angles = row_ids[..., None] * row_freq + col_ids[..., None] * col_freq
    angles = jnp.repeat(angles, 2, axis=-1)
    sign_table = jnp.where(jnp.arange(128, dtype=jnp.int32) % 2 == 0, -1.0, 1.0).astype(jnp.float32)
    return (jnp.cos(angles), jnp.sin(angles) * sign_table)


def rotate(values, cos_table, sin_table):
    paired = values.reshape(values.shape[:-1] + (values.shape[-1] // 2, 2))
    swapped = jnp.flip(paired, -1).reshape(values.shape)
    return values * cos_table + swapped * sin_table


def head_norm(projected, head_gain):
    squares = jnp.mean(projected * projected, -1, keepdims=True)
    return projected * lax.rsqrt(squares + norm_eps) * head_gain


def sigma_of(step_float):
    level = 1.0 - step_float / NSTEPS
    return time_shift * level / (1.0 + (time_shift - 1.0) * level)


def key_usable(text_len, key_count, text_tile, block_len):
    key_pos = jnp.arange(key_count, dtype=jnp.int32)
    owner_tile = key_pos // block_len
    offset = key_pos % block_len
    text_pos = owner_tile * text_tile + offset
    return jnp.logical_or(offset[None, :] >= text_tile, text_pos[None, :] < text_len[:, None])


def per_device(
    image_hidden,
    text_hidden,
    latents,
    step_index,
    anchor,
    text_len,
    mod_image,
    mod_text,
    mod_mlp,
    mod_final,
    qkv_image,
    qkv_text,
    proj_image,
    proj_text,
    qk_gain,
    mlp_expand,
    mlp_reduce,
    final_weight,
):
    requests, tile_rows, tile_cols, model_width = image_hidden.shape
    local_cols = qkv_image.shape[2]
    local_heads = local_cols // HEAD_DIM
    local_units = mlp_expand.shape[1]
    image_all, text_all = (
        lax.all_gather(image_hidden, "tensor", axis=2, tiled=True),
        lax.all_gather(text_hidden, "tensor", axis=1, tiled=True),
    )
    image_mod = modulate(image_all, mod_image[:, 0, None, None, :], mod_image[:, 1, None, None, :])
    text_mod = modulate(text_all, mod_text[:, 0, None, :], mod_text[:, 1, None, :])
    text_tile = text_mod.shape[1]
    image_count = tile_rows * GRID
    block_len = text_tile + image_count
    tile_index = lax.axis_index("tile")
    token_index = jnp.arange(image_count, dtype=jnp.int32)
    row_ids = (anchor[:, 0:1] + tile_index * tile_rows + token_index[None, :] // GRID).astype(
        jnp.float32
    )
    col_ids = (anchor[:, 1:2] + token_index[None, :] % GRID).astype(jnp.float32)
    cos_table, sin_table = rope_tables(row_ids, col_ids)
    cos_table = cos_table[:, :, None, :]
    sin_table = sin_table[:, :, None, :]
    image_qkv = jnp.dot(
        image_mod.reshape(requests * image_count, model_width),
        qkv_image.reshape(model_width, 3 * local_cols),
        preferred_element_type=jnp.float32,
    ).reshape(requests, image_count, 3, local_heads, HEAD_DIM)
    text_qkv = jnp.dot(
        text_mod.reshape(requests * text_tile, model_width),
        qkv_text.reshape(model_width, 3 * local_cols),
        preferred_element_type=jnp.float32,
    ).reshape(requests, text_tile, 3, local_heads, HEAD_DIM)
    query = jnp.concatenate(
        [
            head_norm(text_qkv[:, :, 0], qk_gain[1, 0]).astype(jnp.bfloat16),
            rotate(head_norm(image_qkv[:, :, 0], qk_gain[0, 0]), cos_table, sin_table).astype(
                jnp.bfloat16
            ),
        ],
        1,
    )
    keys = jnp.concatenate(
        [
            head_norm(text_qkv[:, :, 1], qk_gain[1, 1]).astype(jnp.bfloat16),
            rotate(head_norm(image_qkv[:, :, 1], qk_gain[0, 1]), cos_table, sin_table).astype(
                jnp.bfloat16
            ),
        ],
        1,
    )
    values = jnp.concatenate([text_qkv[:, :, 2], image_qkv[:, :, 2]], 1).astype(jnp.bfloat16)
    score_scale = 1.0 / math.sqrt(HEAD_DIM)
    keys_all, values_all = (
        lax.all_gather(keys, "tile", axis=1, tiled=True),
        lax.all_gather(values, "tile", axis=1, tiled=True),
    )
    usable = key_usable(text_len, keys_all.shape[1], text_tile, block_len)[:, None, None, :]
    scores = (
        jnp.einsum("rqhd,rkhd->rhqk", query, keys_all, preferred_element_type=jnp.float32)
        * score_scale
    )
    row_top = jnp.max(jnp.where(usable, scores, -jnp.inf), -1, keepdims=True)
    weights_raw = jnp.where(usable, jnp.exp(scores - row_top), 0.0)
    weight_sum = jnp.sum(weights_raw, -1, keepdims=True)
    accum = jnp.einsum(
        "rhqk,rkhd->rhqd",
        weights_raw.astype(jnp.bfloat16),
        values_all,
        preferred_element_type=jnp.float32,
    )
    attended = (accum / weight_sum).transpose(0, 2, 1, 3).astype(jnp.bfloat16)
    text_term = jnp.dot(
        attended[:, :text_tile].reshape(requests * text_tile, local_cols),
        proj_text,
        preferred_element_type=jnp.float32,
    ).reshape(requests, text_tile, model_width)
    image_term = jnp.dot(
        attended[:, text_tile:].reshape(requests * image_count, local_cols),
        proj_image,
        preferred_element_type=jnp.float32,
    ).reshape(requests, tile_rows, GRID, model_width)
    image_gate = mod_image[:, 2, None, None, :]
    image_sum, text_sum = (
        lax.psum_scatter(image_term, "tensor", scatter_dimension=2, tiled=True),
        lax.psum_scatter(text_term, "tensor", scatter_dimension=1, tiled=True),
    )
    image_mid = (image_hidden.astype(jnp.float32) + image_gate * image_sum).astype(jnp.bfloat16)
    mlp_mod = modulate(image_mid, mod_mlp[:, 0, None, None, :], mod_mlp[:, 1, None, None, :])
    piece = lax.all_gather(mlp_mod, "tensor", axis=2, tiled=True)
    grown = jnp.dot(piece.reshape(-1, model_width), mlp_expand, preferred_element_type=jnp.float32)
    activated = (
        jax.nn.gelu(grown, approximate=True)
        .astype(jnp.bfloat16)
        .reshape(piece.shape[:-1] + (local_units,))
    )
    text_out = (text_hidden.astype(jnp.float32) + mod_text[:, 2, None, :] * text_sum).astype(
        jnp.bfloat16
    )
    mlp_term = jnp.dot(
        activated.reshape(requests * image_count, local_units),
        mlp_reduce,
        preferred_element_type=jnp.float32,
    ).reshape(requests, tile_rows, GRID, model_width)
    mlp_sum = lax.psum_scatter(mlp_term, "tensor", scatter_dimension=2, tiled=True)
    image_out = (image_mid.astype(jnp.float32) + mod_mlp[:, 2, None, None, :] * mlp_sum).astype(
        jnp.bfloat16
    )
    final_in = modulate(image_out, mod_final[:, 0, None, None, :], mod_final[:, 1, None, None, :])
    velocity = jnp.dot(
        final_in.reshape(requests * tile_rows * tile_cols, model_width),
        final_weight,
        preferred_element_type=jnp.float32,
    ).reshape(requests, tile_rows, tile_cols * final_weight.shape[1])
    step_float = step_index.astype(jnp.float32)
    time_delta = sigma_of(step_float + 1.0) - sigma_of(step_float)
    latents_next = latents + time_delta[:, None, None] * velocity
    latents_ext = padded(latents_next, (("tile", 1),), 1)
    return (image_out, text_out, latents_ext)


def solution(mesh):
    return jax.shard_map(
        per_device,
        mesh=mesh,
        in_specs=(
            P(None, "tile", "tensor", None),
            P(None, ("tile", "tensor"), None),
            P(None, "tile", "tensor"),
            P(),
            P(),
            P(),
            P(),
            P(),
            P(),
            P(),
            P(None, None, "tensor"),
            P(None, None, "tensor"),
            P("tensor", None),
            P("tensor", None),
            P(),
            P(None, "tensor"),
            P("tensor", None),
            P(),
        ),
        out_specs=(
            P(None, "tile", "tensor", None),
            P(None, ("tile", "tensor"), None),
            P(None, "tile", "tensor"),
        ),
        check_vma=False,
    )
```

profile of v0, /device:TPU:32, one launch (start us, length us, event | category | flops | bytes accessed | tf_op | source)
XLA Modules:
  0.0 585.7 jit_solution(4433946694455913558)
XLA Ops:
  7.2 1.7 copy.62
  9.0 1.7 copy.61
  10.8 4.3 copy.66
  15.5 1.0 fusion.99
  16.6 0.9 copy.68
  17.5 0.9 copy.70
  18.5 4.3 copy.63
  22.7 0.5 compare_select_fusion
  23.3 0.7 slice_bitcast_fusion.8
  23.9 1.7 slice_bitcast_fusion.3
  25.6 36.5 %all-gather.6.cloned.1.call-done = bf16[8,32,3072]{2,0,1:T(8,128)(2,1)} async-done(((bf16[8,2,3072]{2,0,1:T(8,128)(2,1)}), bf16[8,32,3072]{2,0,1:T(8,128)(2,1)}) %all-gather.6.cloned.1.call-update) | async-done | bytes 1572880 | tf_op jit(solution)/shard_map/all_gather | solution.py:107
  62.1 1.8 convert_reduce_fusion.1
  63.9 2.0 fusion.13
  65.9 2.8 fusion.38
  68.8 0.6 copy-done.4
  69.4 0.7 multiply_convert_fusion.1
  70.1 0.6 copy.76
  70.8 46.7 %all-gather.8.cloned.1.call-done = bf16[8,2,32,3072]{3,0,1,2:T(8,128)(2,1)} async-done(((bf16[8,2,2,3072]{3,0,1,2:T(8,128)(2,1)}), bf16[8,2,32,3072]{3,0,1,2:T(8,128)(2,1)}) %all-gather.8.cloned.1.call-update) | async-done | bytes 3145744 | tf_op jit(solution)/shard_map/all_gather | solution.py:106
  117.5 5.4 convert_reduce_fusion
  122.9 3.2 fusion.3
  126.1 7.0 %fusion.6 = bf16[8,2,32,3072]{3,2,1,0:T(8,128)(2,1)S(1)} fusion(f32[8,3072]{1,0:T(8,128)S(1)} %get-tuple-element.32, f32[8,2,32]{2,1,0:T(2,128)S(1)} %add_rsqrt_fusion.3, f32[8,2,32]{2,1,0:T(2,128)S(1)} %broadcast_multiply_fusion.1, f32[8,3072]{1,0:T(8,128)S(1)} %get-tuple-element.33, bf16[8,2,32,3072]{3,0,1,2:T(8,128)(2,1)S(1)} %copy-done.1), kind=kLoop, calls=%fused_computation.8 | loop fusion | flops 9437184 | bytes 6492160 | tf_op jit(solution)/shard_map/convert_element_type | solution.py:39
  133.1 1.8 fusion.35
  135.1 0.8 slice_bitcast_fusion
  135.9 2.0 copy.74
  137.9 2.0 multiply_multiply_fusion.1
  139.9 1.9 rev.8
  141.8 1.9 copy.75
  143.7 1.0 copy.69
  144.7 2.0 multiply_multiply_fusion.2
  146.7 1.9 rev.7
  148.6 1.2 copy.71
  149.8 1.3 fusion.93
  151.2 1.5 pad_maximum_fusion
  152.8 0.9 fusion.106
  153.7 0.7 pad_maximum_fusion.1
  154.5 0.7 compare_or_fusion
  155.3 0.9 copy.72
  156.1 36.4 %all-gather.10.cloned.1.call-done = bf16[8,1536,1,128]{3,1,0,2:T(8,128)(2,1)} async-done(((bf16[8,96,1,128]{3,1,0,2:T(8,128)(2,1)}), bf16[8,1536,1,128]{3,1,0,2:T(8,128)(2,1)}) %all-gather.10.cloned.1.call-update) | async-done | bytes 3145744 | tf_op jit(solution)/shard_map/all_gather | solution.py:154
  192.5 3.0 fusion.19
  195.6 3.0 fusion.132
  198.5 36.0 %all-gather.12.cloned.1.call-done = bf16[8,1536,1,128]{3,1,0,2:T(8,128)(2,1)} async-done(((bf16[8,96,1,128]{3,1,0,2:T(8,128)(2,1)}), bf16[8,1536,1,128]{3,1,0,2:T(8,128)(2,1)}) %all-gather.12.cloned.1.call-update) | async-done | bytes 3145744 | tf_op jit(solution)/shard_map/all_gather | solution.py:155
  234.5 3.5 fusion.53
  238.0 0.7 copy-done.14
  238.7 3.6 fusion.68
  242.4 0.9 copy-done.12
  243.3 84.6 %reduce-scatter.4.cloned.1.call-done = f32[8,2,2,3072]{3,0,1,2:T(8,128)} async-done(((f32[8,2,32,3072]{3,0,1,2:T(8,128)}), f32[8,2,2,3072]{3,0,1,2:T(8,128)}) %reduce-scatter.4.cloned.1.call-update) | async-done | bytes 393232 | tf_op jit(solution)/shard_map/reduce_scatter | solution.py:184
  327.9 1.2 convert_reduce_fusion.2
  329.3 0.8 fusion.77
  330.5 52.7 %all-gather.14.cloned.1.call-done = bf16[8,2,32,3072]{3,0,1,2:T(8,128)(2,1)} async-done(((bf16[8,2,2,3072]{3,0,1,2:T(8,128)(2,1)}), bf16[8,2,32,3072]{3,0,1,2:T(8,128)(2,1)}) %all-gather.14.cloned.1.call-update) | async-done | bytes 3145744 | tf_op jit(solution)/shard_map/all_gather | solution.py:189
  383.2 5.3 copy.79
  388.4 8.8 %fusion.83 = f32[512,3072]{1,0:T(8,128)} fusion(bf16[384,3072]{1,0:T(8,128)(2,1)S(1)} %copy-done, bf16[512,3072]{1,0:T(8,128)(2,1)} %bitcast.160, bf16[3072,384]{1,0:T(8,128)(2,1)} %param.33), kind=kOutput, calls=%fused_computation.76 | convolution fusion | flops 2417688576 | bytes 14155776 | tf_op jit(solution)/shard_map/dot_general | solution.py:199
  397.2 9.1 %copy.80 = f32[8,2,32,3072]{3,0,1,2:T(8,128)} copy(f32[8,2,32,3072]{3,2,1,0:T(8,128)} %bitcast.158) | data formatting | bytes 12582912 | tf_op jit(solution)/shard_map/reshape | solution.py:203
  406.4 0.9 slice_bitcast_fusion.9
  407.5 2.3 fusion.66
  409.8 0.9 copy-done.13
  410.9 80.8 %reduce-scatter.6.cloned.1.call-done = f32[8,2,2,3072]{3,0,1,2:T(8,128)} async-done(((f32[8,2,32,3072]{3,0,1,2:T(8,128)}), f32[8,2,2,3072]{3,0,1,2:T(8,128)}) %reduce-scatter.6.cloned.1.call-update) | async-done | bytes 393232 | tf_op jit(solution)/shard_map/reduce_scatter | solution.py:204
  491.7 1.1 convert_reduce_fusion.3
  494.0 1.9 collective-permute-start
  495.9 3.6 collective-permute-start.1
  499.5 76.0 %reduce-scatter.8.cloned.1.call-done = f32[8,2,3072]{2,0,1:T(8,128)} async-done(((f32[8,32,3072]{2,0,1:T(8,128)}), f32[8,2,3072]{2,0,1:T(8,128)}) %reduce-scatter.8.cloned.1.call-update) | async-done | bytes 196624 | tf_op jit(solution)/shard_map/reduce_scatter | solution.py:185
  575.6 1.0 add_convert_fusion.1
  576.6 0.7 copy.87
  577.3 0.9 copy.86
  578.2 0.6 pad_maximum_fusion.2
  (92 shorter events, 3.4 us)
Async XLA Ops:
  7.2 381.3 %copy-start = (bf16[384,3072]{1,0:T(8,128)(2,1)S(1)}, bf16[384,3072]{1,0:T(8,128)(2,1)}, u32[]{:S(2)}) copy-start(bf16[384,3072]{1,0:T(8,128)(2,1)} %param.34) | copy-start | bytes 7077892
  7.2 7.9 %copy-start.16 = (f32[2,2,128]{2,1,0:T(2,128)S(1)}, f32[2,2,128]{2,1,0:T(2,128)}, u32[]{:S(2)}) copy-start(f32[2,2,128]{2,1,0:T(2,128)} %param.32) | copy-start | bytes 6148
  7.2 8.2 %copy-start.17 = (s32[8,2]{0,1:T(2,128)S(1)}, s32[8,2]{0,1:T(2,128)}, u32[]{:S(2)}) copy-start(s32[8,2]{0,1:T(2,128)} %param.22) | copy-start | bytes 196
  7.2 54.9 %all-gather.6.cloned.1.call-start = ((), (), s32[]{:S(2)}) async-start(), calls=%async_computation.3 | async-start | bytes 1671168 | tf_op jit(solution)/shard_map/all_gather | solution.py:107
  9.0 108.5 %all-gather.8.cloned.1.call-start = ((), (), s32[]{:S(2)}) async-start(), calls=%async_computation.4 | async-start | bytes 3342336 | tf_op jit(solution)/shard_map/all_gather | solution.py:106
  10.7 181.8 %all-gather.10.cloned.1.call-start = ((), (), s32[]{:S(2)}) async-start(), calls=%async_computation.5 | async-start | bytes 3342336 | tf_op jit(solution)/shard_map/all_gather | solution.py:154
  17.5 5.7 copy-start.11
  62.1 3.8 copy-start.2
  68.7 0.8 copy-start.4
  117.5 5.4 copy-start.1
  126.0 7.1 %copy-start.3 = (bf16[3072,3,128]{0,2,1:T(8,128)(2,1)S(1)}, bf16[3072,3,128]{0,2,1:T(8,128)(2,1)}, u32[]{:S(2)}) copy-start(bf16[3072,3,128]{0,2,1:T(8,128)(2,1)} %copy.66) | copy-start | bytes 7077892
  152.7 81.8 %all-gather.12.cloned.1.call-start = ((), (), s32[]{:S(2)}) async-start(), calls=%async_computation.6 | async-start | bytes 3342336 | tf_op jit(solution)/shard_map/all_gather | solution.py:155
  154.4 173.5 %reduce-scatter.4.cloned.1.call-start = ((), (), s32[]{:S(2)}) async-start(), calls=%async_computation.7 | async-start | bytes 6684672 | tf_op jit(solution)/shard_map/reduce_scatter | solution.py:184
  234.5 4.2 copy-start.5
  238.0 0.7 copy-start.14
  242.3 1.0 copy-start.12
  242.3 85.6 %copy-start.6 = (bf16[8,2,2,3072]{3,2,1,0:T(2,128)(2,1)S(1)}, bf16[8,2,2,3072]{3,2,1,0:T(2,128)(2,1)}, u32[]{:S(2)}) copy-start(bf16[8,2,2,3072]{3,2,1,0:T(2,128)(2,1)} %param.18) | copy-start | bytes 589828
  242.3 85.6 %copy-start.8 = (f32[8,3072]{1,0:T(8,128)S(1)}, f32[8,3072]{1,0:T(8,128)}, u32[]{:S(2)}) copy-start(f32[8,3072]{1,0:T(8,128)} %get-tuple-element.31) | copy-start | bytes 294916
  242.4 140.8 %all-gather.14.cloned.1.call-start = ((), (), s32[]{:S(2)}) async-start(), calls=%async_computation.8 | async-start | bytes 3342336 | tf_op jit(solution)/shard_map/all_gather | solution.py:189
  330.2 161.5 %reduce-scatter.6.cloned.1.call-start = ((), (), s32[]{:S(2)}) async-start(), calls=%async_computation.9 | async-start | bytes 6684672 | tf_op jit(solution)/shard_map/reduce_scatter | solution.py:204
  406.3 1.2 copy-start.7
  406.3 169.2 %reduce-scatter.8.cloned.1.call-start = ((), (), s32[]{:S(2)}) async-start(), calls=%async_computation.10 | async-start | bytes 3342336 | tf_op jit(solution)/shard_map/reduce_scatter | solution.py:185
  407.5 2.3 copy-start.18
  409.7 0.9 copy-start.13
  409.7 83.8 %copy-start.9 = (bf16[3072,64]{0,1:T(8,128)(2,1)S(1)}, bf16[3072,64]{0,1:T(8,128)(2,1)}, u32[]{:S(2)}) copy-start(bf16[3072,64]{0,1:T(8,128)(2,1)} %param.35) | copy-start | bytes 1179652
  409.8 84.1 %copy-start.15 = (f32[8,2,128]{2,1,0:T(2,128)S(1)}, f32[8,2,128]{2,1,0:T(2,128)}, u32[]{:S(2)}) copy-start(f32[8,2,128]{2,1,0:T(2,128)} %param.20) | copy-start | bytes 24580
  409.8 165.8 %copy-start.10 = (f32[8,3072]{1,0:T(8,128)S(1)}, f32[8,3072]{1,0:T(8,128)}, u32[]{:S(2)}) copy-start(f32[8,3072]{1,0:T(8,128)} %get-tuple-element.25) | copy-start | bytes 294916
  494.0 84.2 %collective-permute-start = (f32[8,1,128]{2,1,0:T(1,128)S(1)}, f32[8,1,128]{2,1,0:T(1,128)S(1)}, u32[]{:S(2)}, u32[]{:S(2)}) collective-permute-start(f32[8,1,128]{2,1,0:T(1,128)S(1)} %get-tuple-element.38), channel_id=1, source_target_pairs={{0,16},{16,32},{32,48},{48,64},{64,80},{80,96},{96,112},{112,128},... | collective-permute-start | bytes 12296 | tf_op jit(solution)/shard_map/ppermute | solution.py:24
  495.9 82.3 %collective-permute-start.1 = (f32[8,1,128]{2,1,0:T(1,128)S(1)}, f32[8,1,128]{2,1,0:T(1,128)S(1)}, u32[]{:S(2)}, u32[]{:S(2)}) collective-permute-start(f32[8,1,128]{2,1,0:T(1,128)S(1)} %get-tuple-element.39), channel_id=1, source_target_pairs={{16,0},{32,16},{48,32},{64,48},{80,64},{96,80},{112,96},{128,112},... | collective-permute-start | bytes 12296 | tf_op jit(solution)/shard_map/ppermute | solution.py:25
Sparse Core Ops, SparseCore 0:
  10.5 51.5 all-gather.5
  65.1 52.3 all-gather.7
  152.8 39.6 all-gather.9
  194.8 39.6 all-gather.11
  242.5 85.3 reduce-scatter.3
  330.8 52.3 all-gather.13
  406.5 85.2 reduce-scatter.5
  495.3 80.1 reduce-scatter.7
where the time goes:
time: 587 us; the launch traced here: 586 us
  waiting for transfers between devices  450 us (77%)
  local copies, waits for them, and re-layouts  47.8 us (8%)
  other arithmetic  41.3 us (7%)
  matrix products  26 us (4%)
  between operations  14.5 us (2%)
  starting transfers between devices  6.11 us (1%)
    reduce_scatter x1, waiting for transfers between devices, per_device(): lax.psum_scatter(image_term, 'tensor', scatter_dimension=2, tiled=True)  84.6 us
    reduce_scatter x1, waiting for transfers between devices, per_device(): lax.psum_scatter(mlp_term, 'tensor', scatter_dimension=2, tiled=True)  80.8 us
    reduce_scatter x1, waiting for transfers between devices, per_device(): lax.psum_scatter(text_term, 'tensor', scatter_dimension=1, tiled=True)  76 us
    all_gather x1, waiting for transfers between devices, per_device(): piece = lax.all_gather(mlp_mod, 'tensor', axis=2, tiled=True)  52.7 us
    all_gather x1, waiting for transfers between devices, per_device(): lax.all_gather(image_hidden, 'tensor', axis=2, tiled=True)  46.7 us
    all_gather x1, waiting for transfers between devices, per_device(): lax.all_gather(text_hidden, 'tensor', axis=1, tiled=True)  36.5 us
    all_gather x1, waiting for transfers between devices, per_device(): lax.all_gather(keys, 'tile', axis=1, tiled=True)  36.4 us
    all_gather x1, waiting for transfers between devices, per_device(): lax.all_gather(values, 'tile', axis=1, tiled=True)  36 us
  transfers between devices with their start and end apart: 10, of which 8 were waited for; matrix products, arithmetic and copies ran while one was open for 7% of the time, Pallas kernels for 0%

commit v1 on v0

--- a/solution.py
+++ b/solution.py
@@ -102,21 +102,32 @@
     local_cols = qkv_image.shape[2]
     local_heads = local_cols // HEAD_DIM
     local_units = mlp_expand.shape[1]
-    image_all, text_all = (
-        lax.all_gather(image_hidden, "tensor", axis=2, tiled=True),
-        lax.all_gather(text_hidden, "tensor", axis=1, tiled=True),
-    )
-    image_mod = modulate(image_all, mod_image[:, 0, None, None, :], mod_image[:, 1, None, None, :])
+    owners = lax.axis_size("tensor")
+    own_image = tile_rows * tile_cols
+    own_text = text_hidden.shape[1]
+    joined = jnp.concatenate(
+        [image_hidden.reshape(requests, own_image, model_width), text_hidden], 1
+    )
+    gathered = lax.all_gather(joined, "tensor", axis=1, tiled=True).reshape(
+        requests, owners, own_image + own_text, model_width
+    )
+    image_all = gathered[:, :, :own_image].reshape(requests, owners * own_image, model_width)
+    text_all = gathered[:, :, own_image:].reshape(requests, owners * own_text, model_width)
+    image_mod = modulate(image_all, mod_image[:, 0, None, :], mod_image[:, 1, None, :])
     text_mod = modulate(text_all, mod_text[:, 0, None, :], mod_text[:, 1, None, :])
     text_tile = text_mod.shape[1]
-    image_count = tile_rows * GRID
+    image_count = image_mod.shape[1]
     block_len = text_tile + image_count
     tile_index = lax.axis_index("tile")
     token_index = jnp.arange(image_count, dtype=jnp.int32)
-    row_ids = (anchor[:, 0:1] + tile_index * tile_rows + token_index[None, :] // GRID).astype(
+    owner = token_index // own_image
+    within = token_index % own_image
+    row_ids = (anchor[:, 0:1] + tile_index * tile_rows + within[None, :] // tile_cols).astype(
         jnp.float32
     )
-    col_ids = (anchor[:, 1:2] + token_index[None, :] % GRID).astype(jnp.float32)
+    col_ids = (anchor[:, 1:2] + owner[None, :] * tile_cols + within[None, :] % tile_cols).astype(
+        jnp.float32
+    )
     cos_table, sin_table = rope_tables(row_ids, col_ids)
     cos_table = cos_table[:, :, None, :]
     sin_table = sin_table[:, :, None, :]
@@ -150,10 +161,8 @@
     )
     values = jnp.concatenate([text_qkv[:, :, 2], image_qkv[:, :, 2]], 1).astype(jnp.bfloat16)
     score_scale = 1.0 / math.sqrt(HEAD_DIM)
-    keys_all, values_all = (
-        lax.all_gather(keys, "tile", axis=1, tiled=True),
-        lax.all_gather(values, "tile", axis=1, tiled=True),
-    )
+    kv_all = lax.all_gather(jnp.stack([keys, values], 2), "tile", axis=1, tiled=True)
+    keys_all, values_all = kv_all[:, :, 0], kv_all[:, :, 1]
     usable = key_usable(text_len, keys_all.shape[1], text_tile, block_len)[:, None, None, :]
     scores = (
         jnp.einsum("rqhd,rkhd->rhqk", query, keys_all, preferred_element_type=jnp.float32)
@@ -173,35 +182,33 @@
         attended[:, :text_tile].reshape(requests * text_tile, local_cols),
         proj_text,
         preferred_element_type=jnp.float32,
-    ).reshape(requests, text_tile, model_width)
+    ).reshape(requests, owners, own_text, model_width)
     image_term = jnp.dot(
         attended[:, text_tile:].reshape(requests * image_count, local_cols),
         proj_image,
         preferred_element_type=jnp.float32,
-    ).reshape(requests, tile_rows, GRID, model_width)
+    ).reshape(requests, owners, own_image, model_width)
+    both_term = jnp.concatenate([image_term, text_term], 2).reshape(
+        requests, owners * (own_image + own_text), model_width
+    )
+    both_sum = lax.psum_scatter(both_term, "tensor", scatter_dimension=1, tiled=True)
+    image_sum = both_sum[:, :own_image].reshape(requests, tile_rows, tile_cols, model_width)
+    text_sum = both_sum[:, own_image:]
     image_gate = mod_image[:, 2, None, None, :]
-    image_sum, text_sum = (
-        lax.psum_scatter(image_term, "tensor", scatter_dimension=2, tiled=True),
-        lax.psum_scatter(text_term, "tensor", scatter_dimension=1, tiled=True),
-    )
     image_mid = (image_hidden.astype(jnp.float32) + image_gate * image_sum).astype(jnp.bfloat16)
     mlp_mod = modulate(image_mid, mod_mlp[:, 0, None, None, :], mod_mlp[:, 1, None, None, :])
-    piece = lax.all_gather(mlp_mod, "tensor", axis=2, tiled=True)
+    piece = lax.all_gather(mlp_mod, "tensor", axis=1, tiled=True)
     grown = jnp.dot(piece.reshape(-1, model_width), mlp_expand, preferred_element_type=jnp.float32)
-    activated = (
-        jax.nn.gelu(grown, approximate=True)
-        .astype(jnp.bfloat16)
-        .reshape(piece.shape[:-1] + (local_units,))
-    )
+    activated = jax.nn.gelu(grown, approximate=True).astype(jnp.bfloat16)
     text_out = (text_hidden.astype(jnp.float32) + mod_text[:, 2, None, :] * text_sum).astype(
         jnp.bfloat16
     )
     mlp_term = jnp.dot(
-        activated.reshape(requests * image_count, local_units),
+        activated,
         mlp_reduce,
         preferred_element_type=jnp.float32,
-    ).reshape(requests, tile_rows, GRID, model_width)
-    mlp_sum = lax.psum_scatter(mlp_term, "tensor", scatter_dimension=2, tiled=True)
+    ).reshape(requests, owners * tile_rows, tile_cols, model_width)
+    mlp_sum = lax.psum_scatter(mlp_term, "tensor", scatter_dimension=1, tiled=True)
     image_out = (image_mid.astype(jnp.float32) + mod_mlp[:, 2, None, None, :] * mlp_sum).astype(
         jnp.bfloat16
     )

time: 587 us -> 492 us (0.84)
  waiting for transfers between devices: 450 us -> 317 us
  local copies, waits for them, and re-layouts: 47.8 us -> 86.2 us
  matrix products: 26 us -> 18.3 us
    reduce_scatter x3 -> x2, waiting for transfers between devices: 241 us -> 174 us  [the longest x1 90.7 us: per_device(): lax.psum_scatter(both_term, 'tensor', scatter_dimension=1, tiled=True)]
    all_gather x5 -> x3, waiting for transfers between devices: 208 us -> 142 us  [the longest x1 52.9 us: per_device(): piece = lax.all_gather(mlp_mod, 'tensor', axis=1, tiled=True)]
    reshape x1 -> x3, local copies, waits for them, and re-layouts: 9.09 us -> 24.7 us  [the longest x2 17.2 us: per_device(): mlp_term = jnp.dot(activated, mlp_reduce, preferred_element_type=jnp.floa...]
    concatenate x3 -> x1, local copies, waits for them, and re-layouts: 0.95 us -> 12.8 us  [per_device(): jnp.concatenate([image_term, text_term], 2)]
    concatenate x2, other arithmetic: 2.21 us -> 8.23 us  [the longest x1 7.47 us: per_device(): jnp.concatenate([image_term, text_term], 2)]
  transfers between devices with their start and end apart: 10 -> 7, of which waited for: 8 -> 5; matrix products, arithmetic and copies ran while one was open for 7% -> 5% of each run, Pallas kernels for 0% -> 0%
where the time goes in v1:
time: 492 us; the launch traced here: 485 us
  waiting for transfers between devices  317 us (64%)
  local copies, waits for them, and re-layouts  86.2 us (18%)
  other arithmetic  43.9 us (9%)
  matrix products  18.3 us (4%)
  between operations  14.4 us (3%)
  starting transfers between devices  5.94 us (1%)
    reduce_scatter x1, waiting for transfers between devices, per_device(): lax.psum_scatter(both_term, 'tensor', scatter_dimension=1, tiled=True)  90.7 us
    reduce_scatter x1, waiting for transfers between devices, per_device(): lax.psum_scatter(mlp_term, 'tensor', scatter_dimension=1, tiled=True)  83.5 us
    all_gather x1, waiting for transfers between devices, per_device(): piece = lax.all_gather(mlp_mod, 'tensor', axis=1, tiled=True)  52.9 us
    all_gather x1, waiting for transfers between devices, per_device(): lax.all_gather(joined, 'tensor', axis=1, tiled=True)  44.9 us
    all_gather x1, waiting for transfers between devices, per_device(): lax.all_gather(jnp.stack([keys, values], 2), 'tile', axis=1, tiled=True)  44.5 us
    reshape x2, local copies, waits for them, and re-layouts, per_device(): mlp_term = jnp.dot(activated, mlp_reduce, preferred_element_type=jnp.floa...  17.2 us
    unnamed x45, local copies, waits for them, and re-layouts  14.7 us
    concatenate x1, local copies, waits for them, and re-layouts, per_device(): jnp.concatenate([image_term, text_term], 2)  12.8 us
  transfers between devices with their start and end apart: 7, of which 5 were waited for; matrix products, arithmetic and copies ran while one was open for 5% of the time, Pallas kernels for 0%

profile of v1, /device:TPU:32, one launch (start us, length us, event | category | flops | bytes accessed | tf_op | source)
XLA Modules:
  0.0 485.3 jit_solution(10807011997168839072)
XLA Ops:
  7.2 1.1 copy.171
  8.4 0.9 copy.173
  9.3 0.8 pad_maximum_fusion.1
  10.1 4.3 copy.175
  15.0 0.7 mul.611
  15.8 0.8 mul.590
  16.6 1.0 fusion.83
  18.0 0.9 copy.181
  18.9 4.4 copy.174
  23.9 1.7 slice_bitcast_fusion.9
  25.5 1.7 slice_bitcast_fusion.4
  27.3 44.9 %all-gather.4.cloned.1.call-done = bf16[8,96,3072]{2,0,1:T(8,128)(2,1)} async-done(((bf16[8,6,3072]{2,0,1:T(8,128)(2,1)}), bf16[8,96,3072]{2,0,1:T(8,128)(2,1)}) %all-gather.4.cloned.1.call-update) | async-done | bytes 4718608 | tf_op jit(solution)/shard_map/all_gather | solution.py:111
  72.1 2.5 convert_reduce_fusion
  74.7 2.9 fusion.3
  77.6 1.8 fusion.6
  79.4 1.8 fusion.27
  81.3 0.8 fusion.73
  82.1 0.9 slice_bitcast_fusion.1
  83.9 0.8 fusion.16
  84.7 1.0 fusion.30
  85.7 0.8 multiply_reduce_fusion.1
  87.1 1.4 copy.184
  88.5 1.3 add_rsqrt_fusion.4
  89.8 2.0 copy.187
  91.8 1.4 copy.185
  93.2 2.1 multiply_multiply_fusion.1
  95.2 1.9 rev.8
  97.1 1.9 copy.188
  99.1 1.4 copy.177
  100.5 1.3 add_rsqrt_fusion.5
  101.8 2.0 copy.180
  103.8 1.4 copy.178
  105.1 2.1 multiply_multiply_fusion.2
  107.2 1.9 rev.7
  109.1 1.9 copy.182
  111.8 1.7 multiply_convert_fusion.1
  113.5 2.0 fusion.77
  115.5 1.7 maximum_bitcast_fusion
  117.3 0.9 maximum_bitcast_fusion.1
  118.3 44.5 %all-gather.6.cloned.1.call-done = bf16[8,1536,2,1,128]{4,0,3,2,1:T(8,128)(2,1)} async-done(((bf16[8,96,2,1,128]{4,0,3,2,1:T(8,128)(2,1)}), bf16[8,1536,2,1,128]{4,0,3,2,1:T(8,128)(2,1)}) %all-gather.6.cloned.1.call-update) | async-done | bytes 6291472 | tf_op jit(solution)/shard_map/all_gather | solution.py:164
  162.7 3.4 fusion.113
  166.2 1.2 fusion.18
  167.3 1.6 fusion.116
  169.0 1.1 fusion.39
  170.1 3.7 fusion.52
  174.3 7.5 %pad_maximum_fusion = f32[8,16,6,3072]{3,1,2,0:T(8,128)} fusion(f32[8,16,2,3072]{3,1,2,0:T(8,128)S(1)} %fusion.50, f32[8,16,4,3072]{3,1,2,0:T(8,128)} %fusion.52), kind=kLoop, calls=%fused_computation.1 | loop fusion | flops 2359296 | bytes 18874368 | tf_op jit(solution)/shard_map/concatenate | solution.py:191
  181.8 12.8 %copy.195 = f32[8,16,6,3072]{3,0,2,1:T(8,128)} copy(f32[8,16,6,3072]{3,1,2,0:T(8,128)} %pad_maximum_fusion) | data formatting | bytes 18874368 | tf_op jit(solution)/shard_map/concatenate | solution.py:191
  195.6 90.7 %reduce-scatter.3.cloned.1.call-done = f32[8,6,3072]{2,0,1:T(8,128)} async-done(((f32[8,96,3072]{2,0,1:T(8,128)}), f32[8,6,3072]{2,0,1:T(8,128)}) %reduce-scatter.3.cloned.1.call-update) | async-done | bytes 589840 | tf_op jit(solution)/shard_map/reduce_scatter | solution.py:194
  286.3 1.0 slice.149
  287.8 0.8 fusion.61
  288.7 52.9 %all-gather.8.cloned.1.call-done = bf16[8,32,2,3072]{3,0,2,1:T(8,128)(2,1)} async-done(((bf16[8,2,2,3072]{3,0,2,1:T(8,128)(2,1)}), bf16[8,32,2,3072]{3,0,2,1:T(8,128)(2,1)}) %all-gather.8.cloned.1.call-update) | async-done | bytes 3145744 | tf_op jit(solution)/shard_map/all_gather | solution.py:200
  341.7 6.8 %copy.196 = bf16[8,32,2,3072]{3,2,1,0:T(2,128)(2,1)} copy(bf16[8,32,2,3072]{3,0,2,1:T(8,128)(2,1)} %all-gather.8.cloned.1.call-done) | data formatting | bytes 6291456 | tf_op jit(solution)/shard_map/all_gather | solution.py:200
  348.4 7.5 %reshape.851 = bf16[512,3072]{1,0:T(8,128)(2,1)} reshape(bf16[8,32,2,3072]{3,2,1,0:T(2,128)(2,1)} %copy.196) | data formatting | bytes 6291456 | tf_op jit(solution)/shard_map/reshape | solution.py:201
  355.9 8.8 %fusion.67 = f32[512,3072]{1,0:T(8,128)} fusion(bf16[384,3072]{1,0:T(8,128)(2,1)S(1)} %copy-done, bf16[512,3072]{1,0:T(8,128)(2,1)} %reshape.851, bf16[3072,384]{1,0:T(8,128)(2,1)} %param.33), kind=kOutput, calls=%fused_computation.72 | convolution fusion | flops 2417688576 | bytes 14155776 | tf_op jit(solution)/shard_map/dot_general | solution.py:206
  364.8 8.1 %reshape.852 = f32[8,32,2,3072]{3,2,1,0:T(2,128)} reshape(f32[512,3072]{1,0:T(8,128)} %fusion.67) | data formatting | bytes 12582912 | tf_op jit(solution)/shard_map/reshape | solution.py:210
  372.9 9.1 %copy.197 = f32[8,32,2,3072]{3,0,2,1:T(8,128)} copy(f32[8,32,2,3072]{3,2,1,0:T(2,128)} %reshape.852) | data formatting | bytes 12582912 | tf_op jit(solution)/shard_map/reshape | solution.py:210
  382.7 1.2 fusion.114
  384.0 83.5 %reduce-scatter.5.cloned.1.call-done = f32[8,2,2,3072]{3,0,2,1:T(8,128)} async-done(((f32[8,32,2,3072]{3,0,2,1:T(8,128)}), f32[8,2,2,3072]{3,0,2,1:T(8,128)}) %reduce-scatter.5.cloned.1.call-update) | async-done | bytes 393232 | tf_op jit(solution)/shard_map/reduce_scatter | solution.py:211
  467.5 1.1 convert_reduce_fusion.3
  469.7 1.9 collective-permute-start
  471.6 3.6 collective-permute-start.1
  475.3 1.0 fusion.86
  476.3 0.7 copy.203
  477.1 0.9 copy.202
  (95 shorter events, 8.7 us)
Async XLA Ops:
  7.2 348.8 %copy-start = (bf16[384,3072]{1,0:T(8,128)(2,1)S(1)}, bf16[384,3072]{1,0:T(8,128)(2,1)}, u32[]{:S(2)}) copy-start(bf16[384,3072]{1,0:T(8,128)(2,1)} %param.34) | copy-start | bytes 7077892
  7.2 7.2 %copy-start.15 = (f32[2,2,128]{2,1,0:T(2,128)S(1)}, f32[2,2,128]{2,1,0:T(2,128)}, u32[]{:S(2)}) copy-start(f32[2,2,128]{2,1,0:T(2,128)} %param.32) | copy-start | bytes 6148
  7.2 9.4 %copy-start.16 = (s32[8,2]{0,1:T(2,128)S(1)}, s32[8,2]{0,1:T(2,128)}, u32[]{:S(2)}) copy-start(s32[8,2]{0,1:T(2,128)} %param.22) | copy-start | bytes 196
  7.2 64.9 %all-gather.4.cloned.1.call-start = ((), (), s32[]{:S(2)}) async-start(), calls=%async_computation.2 | async-start | bytes 5013504 | tf_op jit(solution)/shard_map/all_gather | solution.py:111
  10.1 152.6 %all-gather.6.cloned.1.call-start = ((), (), s32[]{:S(2)}) async-start(), calls=%async_computation.3 | async-start | bytes 6684672 | tf_op jit(solution)/shard_map/all_gather | solution.py:164
  72.1 5.4 %copy-start.1 = (bf16[8,96,3072]{2,0,1:T(8,128)(2,1)S(1)}, bf16[8,96,3072]{2,0,1:T(8,128)(2,1)}, u32[]{:S(2)}) copy-start(bf16[8,96,3072]{2,0,1:T(8,128)(2,1)} %all-gather.4.cloned.1.call-done) | copy-start | bytes 14155780
  77.6 1.8 copy-start.2
  81.2 2.6 copy-start.8
  81.3 2.6 copy-start.9
  82.9 1.7 copy-start.3
  85.7 0.8 copy-start.4
  111.7 5.5 %copy-start.17 = (s32[8]{0:T(128)S(1)}, s32[8]{0:T(128)}, u32[]{:S(2)}) copy-start(s32[8]{0:T(128)} %param.23) | copy-start | bytes 100
  117.1 169.1 %reduce-scatter.3.cloned.1.call-start = ((), (), s32[]{:S(2)}) async-start(), calls=%async_computation.4 | async-start | bytes 10027008 | tf_op jit(solution)/shard_map/reduce_scatter | solution.py:194
  169.0 1.1 copy-start.5
  170.1 3.7 copy-start.7
  194.6 1.0 copy-start.13
  194.6 92.7 %copy-start.6 = (bf16[8,2,2,3072]{3,2,1,0:T(2,128)(2,1)S(1)}, bf16[8,2,2,3072]{3,2,1,0:T(2,128)(2,1)}, u32[]{:S(2)}) copy-start(bf16[8,2,2,3072]{3,2,1,0:T(2,128)(2,1)} %param.18) | copy-start | bytes 589828
  194.6 92.7 %copy-start.10 = (f32[8,3072]{1,0:T(8,128)S(1)}, f32[8,3072]{1,0:T(8,128)}, u32[]{:S(2)}) copy-start(f32[8,3072]{1,0:T(8,128)} %get-tuple-element.45) | copy-start | bytes 294916
  194.6 147.0 %all-gather.8.cloned.1.call-start = ((), (), s32[]{:S(2)}) async-start(), calls=%async_computation.5 | async-start | bytes 3342336 | tf_op jit(solution)/shard_map/all_gather | solution.py:200
  288.7 178.8 %reduce-scatter.5.cloned.1.call-start = ((), (), s32[]{:S(2)}) async-start(), calls=%async_computation.6 | async-start | bytes 6684672 | tf_op jit(solution)/shard_map/reduce_scatter | solution.py:211
  382.0 0.7 copy-start.18
  382.6 86.6 %copy-start.11 = (bf16[3072,64]{0,1:T(8,128)(2,1)S(1)}, bf16[3072,64]{0,1:T(8,128)(2,1)}, u32[]{:S(2)}) copy-start(bf16[3072,64]{0,1:T(8,128)(2,1)} %param.35) | copy-start | bytes 1179652
  382.6 87.0 %copy-start.14 = (f32[8,2,128]{2,1,0:T(2,128)S(1)}, f32[8,2,128]{2,1,0:T(2,128)}, u32[]{:S(2)}) copy-start(f32[8,2,128]{2,1,0:T(2,128)} %param.20) | copy-start | bytes 24580
  382.6 92.6 %copy-start.12 = (f32[8,3072]{1,0:T(8,128)S(1)}, f32[8,3072]{1,0:T(8,128)}, u32[]{:S(2)}) copy-start(f32[8,3072]{1,0:T(8,128)} %get-tuple-element.39) | copy-start | bytes 294916
  469.7 8.2 %collective-permute-start = (f32[8,1,128]{2,1,0:T(1,128)S(1)}, f32[8,1,128]{2,1,0:T(1,128)S(1)}, u32[]{:S(2)}, u32[]{:S(2)}) collective-permute-start(f32[8,1,128]{2,1,0:T(1,128)S(1)} %get-tuple-element.52), channel_id=1, source_target_pairs={{0,16},{16,32},{32,48},{48,64},{64,80},{80,96},{96,112},{112,128},... | collective-permute-start | bytes 12296 | tf_op jit(solution)/shard_map/ppermute | solution.py:24
  471.6 6.3 %collective-permute-start.1 = (f32[8,1,128]{2,1,0:T(1,128)S(1)}, f32[8,1,128]{2,1,0:T(1,128)S(1)}, u32[]{:S(2)}, u32[]{:S(2)}) collective-permute-start(f32[8,1,128]{2,1,0:T(1,128)S(1)} %get-tuple-element.53), channel_id=1, source_target_pairs={{16,0},{32,16},{48,32},{64,48},{80,64},{96,80},{112,96},{128,112},... | collective-permute-start | bytes 12296 | tf_op jit(solution)/shard_map/ppermute | solution.py:25
Sparse Core Ops, SparseCore 0:
  10.5 61.6 all-gather.3
  117.3 45.4 all-gather.5
  194.8 91.4 reduce-scatter.2
  289.4 52.1 all-gather.7
  382.1 85.2 reduce-scatter.4

commit v2 on v1

--- a/solution.py
+++ b/solution.py
@@ -40,7 +40,8 @@
 
 
 def rope_tables(row_ids, col_ids):
-    pair_index = jnp.arange(64, dtype=jnp.int32)
+    lane = jnp.arange(2 * 64, dtype=jnp.int32)
+    pair_index = lane // 2
     row_rank = (pair_index - 8).astype(jnp.float32)
     col_rank = (pair_index - 36).astype(jnp.float32)
     log_base = math.log(10000.0)
@@ -49,14 +50,15 @@
     )
     col_freq = jnp.where(pair_index >= 36, jnp.exp(-2.0 * col_rank / 56.0 * log_base), 0.0)
     angles = row_ids[..., None] * row_freq + col_ids[..., None] * col_freq
-    angles = jnp.repeat(angles, 2, axis=-1)
-    sign_table = jnp.where(jnp.arange(128, dtype=jnp.int32) % 2 == 0, -1.0, 1.0).astype(jnp.float32)
+    sign_table = jnp.where(lane % 2 == 0, -1.0, 1.0).astype(jnp.float32)
     return (jnp.cos(angles), jnp.sin(angles) * sign_table)
 
 
 def rotate(values, cos_table, sin_table):
-    paired = values.reshape(values.shape[:-1] + (values.shape[-1] // 2, 2))
-    swapped = jnp.flip(paired, -1).reshape(values.shape)
+    lane = lax.broadcasted_iota(jnp.int32, values.shape, values.ndim - 1)
+    swapped = jnp.where(
+        lane % 2 == 0, jnp.roll(values, -1, axis=-1), jnp.roll(values, 1, axis=-1)
+    )
     return values * cos_table + swapped * sin_table
 
 
@@ -105,16 +107,18 @@
     owners = lax.axis_size("tensor")
     own_image = tile_rows * tile_cols
     own_text = text_hidden.shape[1]
-    joined = jnp.concatenate(
-        [image_hidden.reshape(requests, own_image, model_width), text_hidden], 1
-    )
+    image_mod_own = modulate(
+        image_hidden.reshape(requests, own_image, model_width),
+        mod_image[:, 0, None, :],
+        mod_image[:, 1, None, :],
+    )
+    text_mod_own = modulate(text_hidden, mod_text[:, 0, None, :], mod_text[:, 1, None, :])
+    joined = jnp.concatenate([image_mod_own, text_mod_own], 1)
     gathered = lax.all_gather(joined, "tensor", axis=1, tiled=True).reshape(
         requests, owners, own_image + own_text, model_width
     )
-    image_all = gathered[:, :, :own_image].reshape(requests, owners * own_image, model_width)
-    text_all = gathered[:, :, own_image:].reshape(requests, owners * own_text, model_width)
-    image_mod = modulate(image_all, mod_image[:, 0, None, :], mod_image[:, 1, None, :])
-    text_mod = modulate(text_all, mod_text[:, 0, None, :], mod_text[:, 1, None, :])
+    image_mod = gathered[:, :, :own_image].reshape(requests, owners * own_image, model_width)
+    text_mod = gathered[:, :, own_image:].reshape(requests, owners * own_text, model_width)
     text_tile = text_mod.shape[1]
     image_count = image_mod.shape[1]
     block_len = text_tile + image_count
@@ -178,17 +182,19 @@
         preferred_element_type=jnp.float32,
     )
     attended = (accum / weight_sum).transpose(0, 2, 1, 3).astype(jnp.bfloat16)
-    text_term = jnp.dot(
-        attended[:, :text_tile].reshape(requests * text_tile, local_cols),
-        proj_text,
-        preferred_element_type=jnp.float32,
-    ).reshape(requests, owners, own_text, model_width)
-    image_term = jnp.dot(
-        attended[:, text_tile:].reshape(requests * image_count, local_cols),
-        proj_image,
-        preferred_element_type=jnp.float32,
-    ).reshape(requests, owners, own_image, model_width)
-    both_term = jnp.concatenate([image_term, text_term], 2).reshape(
+    text_att = attended[:, :text_tile].reshape(requests, owners, own_text, local_cols)
+    image_att = attended[:, text_tile:].reshape(requests, owners, own_image, local_cols)
+    zeros_t = jnp.zeros_like(text_att)
+    zeros_i = jnp.zeros_like(image_att)
+    stacked = jnp.concatenate(
+        [
+            jnp.concatenate([image_att, zeros_i], 3),
+            jnp.concatenate([zeros_t, text_att], 3),
+        ],
+        2,
+    ).reshape(requests * owners * (own_image + own_text), 2 * local_cols)
+    both_proj = jnp.concatenate([proj_image, proj_text], 0)
+    both_term = jnp.dot(stacked, both_proj, preferred_element_type=jnp.float32).reshape(
         requests, owners * (own_image + own_text), model_width
     )
     both_sum = lax.psum_scatter(both_term, "tensor", scatter_dimension=1, tiled=True)
@@ -197,7 +203,9 @@
     image_gate = mod_image[:, 2, None, None, :]
     image_mid = (image_hidden.astype(jnp.float32) + image_gate * image_sum).astype(jnp.bfloat16)
     mlp_mod = modulate(image_mid, mod_mlp[:, 0, None, None, :], mod_mlp[:, 1, None, None, :])
-    piece = lax.all_gather(mlp_mod, "tensor", axis=1, tiled=True)
+    piece = lax.all_gather(
+        mlp_mod.reshape(requests, own_image, model_width), "tensor", axis=1, tiled=True
+    )
     grown = jnp.dot(piece.reshape(-1, model_width), mlp_expand, preferred_element_type=jnp.float32)
     activated = jax.nn.gelu(grown, approximate=True).astype(jnp.bfloat16)
     text_out = (text_hidden.astype(jnp.float32) + mod_text[:, 2, None, :] * text_sum).astype(
@@ -207,8 +215,10 @@
         activated,
         mlp_reduce,
         preferred_element_type=jnp.float32,
-    ).reshape(requests, owners * tile_rows, tile_cols, model_width)
-    mlp_sum = lax.psum_scatter(mlp_term, "tensor", scatter_dimension=1, tiled=True)
+    ).reshape(requests, owners * own_image, model_width)
+    mlp_sum = lax.psum_scatter(mlp_term, "tensor", scatter_dimension=1, tiled=True).reshape(
+        requests, tile_rows, tile_cols, model_width
+    )
     image_out = (image_mid.astype(jnp.float32) + mod_mlp[:, 2, None, None, :] * mlp_sum).astype(
         jnp.bfloat16
     )

time: 492 us -> 425 us (0.86)
  local copies, waits for them, and re-layouts: 86.2 us -> 34.3 us
  other arithmetic: 43.9 us -> 19.6 us
  waiting for transfers between devices: 317 us -> 325 us
    concatenate x1 -> x0, local copies, waits for them, and re-layouts: 12.8 us -> none  [per_device(): jnp.concatenate([image_term, text_term], 2)]
    reshape x3 -> x2, local copies, waits for them, and re-layouts: 11.4 us -> 0.12 us  [the longest x1 0.09 us: per_device(): attended[:, text_tile:].reshape(requests, owners, own_image, local_cols)]
    reshape x2 -> x1, local copies, waits for them, and re-layouts: 17.2 us -> 9.07 us  [per_device(): mlp_term = jnp.dot(activated, mlp_reduce, preferred_element_type=jnp.floa...]
    all_gather x1, waiting for transfers between devices: 44.9 us -> 52.9 us  [per_device(): lax.all_gather(joined, 'tensor', axis=1, tiled=True)]
    concatenate x2, other arithmetic: 8.23 us -> 0.78 us  [the longest x1 0.75 us: per_device(): joined = jnp.concatenate([image_mod_own, text_mod_own], 1)]
    unnamed x45 -> x39, local copies, waits for them, and re-layouts: 14.7 us -> 11.8 us
  transfers between devices with their start and end apart: 7 -> 7, of which waited for: 5 -> 5; matrix products, arithmetic and copies ran while one was open for 5% -> 3% of each run, Pallas kernels for 0% -> 0%
where the time goes in v2:
time: 425 us; the launch traced here: 421 us
  waiting for transfers between devices  325 us (76%)
  local copies, waits for them, and re-layouts  34.3 us (8%)
  matrix products  21.6 us (5%)
  other arithmetic  19.6 us (5%)
  between operations  14.3 us (3%)
  starting transfers between devices  6.17 us (1%)
    reduce_scatter x1, waiting for transfers between devices, per_device(): lax.psum_scatter(both_term, 'tensor', scatter_dimension=1, tiled=True)  90.9 us
    reduce_scatter x1, waiting for transfers between devices, per_device(): lax.psum_scatter(mlp_term, 'tensor', scatter_dimension=1, tiled=True)  84.3 us
    all_gather x1, waiting for transfers between devices, per_device(): lax.all_gather(joined, 'tensor', axis=1, tiled=True)  52.9 us
    all_gather x1, waiting for transfers between devices, per_device(): lax.all_gather(mlp_mod.reshape(requests, own_image, model_width), 'tensor...  52.1 us
    all_gather x1, waiting for transfers between devices, per_device(): lax.all_gather(jnp.stack([keys, values], 2), 'tile', axis=1, tiled=True)  45.2 us
    unnamed x39, local copies, waits for them, and re-layouts  11.8 us
    reshape x1, local copies, waits for them, and re-layouts, per_device(): mlp_term = jnp.dot(activated, mlp_reduce, preferred_element_type=jnp.floa...  9.07 us
    dot_general x1, matrix products, per_device(): jnp.dot(activated, mlp_reduce, preferred_element_type=jnp.float32)  8.79 us
  transfers between devices with their start and end apart: 7, of which 5 were waited for; matrix products, arithmetic and copies ran while one was open for 3% of the time, Pallas kernels for 0%

profile of v2, /device:TPU:32, one launch (start us, length us, event | category | flops | bytes accessed | tf_op | source)
XLA Modules:
  0.0 421.3 jit_solution(15517366317401850293)
XLA Ops:
  7.2 1.3 convert_reduce_fusion.3
  8.6 1.3 multiply_reduce_fusion
  9.9 0.1 copy.73
  10.0 1.0 copy.72
  11.0 1.0 slice_bitcast_fusion.19
  12.0 0.1 copy.74
  12.1 1.6 slice_bitcast_fusion.14
  13.8 1.0 convert_reduce_fusion.2
  14.8 1.1 fusion.84
  15.8 1.0 fusion.87
  16.8 0.1 fusion.68
  17.0 0.7 pad_maximum_fusion
  17.8 4.4 %copy.79 = bf16[3072,3,128]{0,2,1:T(8,128)(2,1)} copy(bf16[3072,3,128]{2,0,1:T(8,128)(2,1)} %param.28) | data formatting | bytes 4718592 | tf_op args[10]
  22.2 4.3 %copy.77 = bf16[3072,3,128]{0,2,1:T(8,128)(2,1)} copy(bf16[3072,3,128]{2,0,1:T(8,128)(2,1)} %param.29) | data formatting | bytes 4718592 | tf_op args[11]
  26.7 52.9 %all-gather.4.cloned.1.call-done = bf16[8,96,3072]{2,0,1:T(8,128)(2,1)} async-done(((bf16[8,6,3072]{2,0,1:T(8,128)(2,1)}), bf16[8,96,3072]{2,0,1:T(8,128)(2,1)}) %all-gather.4.cloned.1.call-update) | async-done | bytes 4718608 | tf_op jit(solution)/shard_map/all_gather | solution.py:117
  79.6 2.3 slice.175
  81.9 0.3 copy-done.3
  82.2 2.2 fusion.20
  84.3 0.2 multiply_reduce_fusion.2
  84.6 0.2 multiply_multiply_fusion.2
  84.8 0.1 fusion.111
  84.9 0.1 fusion.112
  85.1 0.1 fusion.113
  85.2 0.1 fusion.114
  85.3 1.7 slice.173
  87.1 1.3 fusion.25
  88.5 0.1 multiply_reduce_fusion.4
  88.6 0.1 multiply_convert_fusion.1
  88.8 1.4 fusion.77
  90.2 0.8 maximum_maximum_fusion
  91.0 0.2 reduce-scatter.3.cloned.1.call-start
  91.4 45.2 %all-gather.6.cloned.1.call-done = bf16[8,1536,2,1,128]{4,1,2,0,3:T(8,128)(2,1)} async-done(((bf16[8,96,2,1,128]{4,1,2,0,3:T(8,128)(2,1)}), bf16[8,1536,2,1,128]{4,1,2,0,3:T(8,128)(2,1)}) %all-gather.6.cloned.1.call-update) | async-done | bytes 6291472 | tf_op jit(solution)/shard_map/all_gather | solution.py:168
  136.6 3.2 fusion.6
  139.8 1.6 fusion.117
  141.4 0.9 fusion.36
  142.3 0.1 copy.82
  142.6 0.2 copy-done.7
  142.8 5.1 %fusion.16 = f32[8,96,3072]{2,0,1:T(8,128)} fusion(bf16[8,96,256]{2,0,1:T(8,128)(2,1)S(1)} %bitcast.149, bf16[128,3072]{1,0:T(8,128)(2,1)S(1)} %copy-done.6, bf16[128,3072]{1,0:T(8,128)(2,1)S(1)} %copy-done.7), kind=kOutput, calls=%fused_computation.19 | convolution fusion | flops 1211105280 | bytes 11403264 | tf_op jit(solution)/shard_map/dot_general | solution.py:197
  147.9 0.9 copy-done.9
  148.8 90.9 %reduce-scatter.3.cloned.1.call-done = f32[8,6,3072]{2,0,1:T(8,128)} async-done(((f32[8,96,3072]{2,0,1:T(8,128)}), f32[8,6,3072]{2,0,1:T(8,128)}) %reduce-scatter.3.cloned.1.call-update) | async-done | bytes 589840 | tf_op jit(solution)/shard_map/reduce_scatter | solution.py:200
  239.7 1.0 slice.193
  240.8 0.5 convert_reduce_fusion
  241.3 0.4 fusion.53
  241.7 0.4 fusion.56
  242.1 0.7 copy.87
  242.9 0.3 reduce-scatter.5.cloned.1.call-start
  243.2 52.1 %all-gather.8.cloned.1.call-done = bf16[8,64,3072]{2,0,1:T(8,128)(2,1)} async-done(((bf16[8,4,3072]{2,0,1:T(8,128)(2,1)}), bf16[8,64,3072]{2,0,1:T(8,128)(2,1)}) %all-gather.8.cloned.1.call-update) | async-done | bytes 3145744 | tf_op jit(solution)/shard_map/all_gather | solution.py:206
  295.2 5.3 %copy.88 = bf16[8,64,3072]{2,1,0:T(8,128)(2,1)} copy(bf16[8,64,3072]{2,0,1:T(8,128)(2,1)} %all-gather.8.cloned.1.call-done) | data formatting | bytes 6291456 | tf_op jit(solution)/shard_map/all_gather | solution.py:206
  300.6 8.8 %fusion.63 = f32[512,3072]{1,0:T(8,128)} fusion(bf16[384,3072]{1,0:T(8,128)(2,1)S(1)} %copy-done, bf16[512,3072]{1,0:T(8,128)(2,1)} %bitcast.148, bf16[3072,384]{1,0:T(8,128)(2,1)} %param.33), kind=kOutput, calls=%fused_computation.60 | convolution fusion | flops 2417688576 | bytes 14155776 | tf_op jit(solution)/shard_map/dot_general | solution.py:214
  309.3 9.1 %copy.89 = f32[8,64,3072]{2,0,1:T(8,128)} copy(f32[8,64,3072]{2,1,0:T(8,128)} %bitcast.144) | data formatting | bytes 12582912 | tf_op jit(solution)/shard_map/reshape | solution.py:218
  318.5 0.6 copy-done.15
  319.1 0.3 copy-done.10
  319.4 0.2 fusion.115
  319.6 84.3 %reduce-scatter.5.cloned.1.call-done = f32[8,4,3072]{2,0,1:T(8,128)} async-done(((f32[8,64,3072]{2,0,1:T(8,128)}), f32[8,4,3072]{2,0,1:T(8,128)}) %reduce-scatter.5.cloned.1.call-update) | async-done | bytes 393232 | tf_op jit(solution)/shard_map/reduce_scatter | solution.py:219
  403.9 1.5 convert_reduce_fusion.1
  405.4 0.4 fusion.57
  405.8 0.4 fusion.60
  406.3 0.2 fusion.120
  406.6 0.1 reshape.847
  406.7 1.9 collective-permute-start
  408.7 3.6 collective-permute-start.1
  412.3 1.0 fusion.88
  413.4 0.7 copy.93
  414.1 0.6 pad_maximum_fusion.1
  (78 shorter events, 1.0 us)
Async XLA Ops:
  7.2 293.4 %copy-start = (bf16[384,3072]{1,0:T(8,128)(2,1)S(1)}, bf16[384,3072]{1,0:T(8,128)(2,1)}, u32[]{:S(2)}) copy-start(bf16[384,3072]{1,0:T(8,128)(2,1)} %param.34) | copy-start | bytes 7077892
  7.2 72.4 %all-gather.4.cloned.1.call-start = ((), (), s32[]{:S(2)}) async-start(), calls=%async_computation.2 | async-start | bytes 5013504 | tf_op jit(solution)/shard_map/all_gather | solution.py:117
  17.8 118.8 %all-gather.6.cloned.1.call-start = ((), (), s32[]{:S(2)}) async-start(), calls=%async_computation.3 | async-start | bytes 6684672 | tf_op jit(solution)/shard_map/all_gather | solution.py:168
  22.2 4.4 %copy-start.13 = (s32[8,2]{0,1:T(2,128)S(1)}, s32[8,2]{0,1:T(2,128)}, u32[]{:S(2)}) copy-start(s32[8,2]{0,1:T(2,128)} %param.22) | copy-start | bytes 196
  22.2 4.4 %copy-start.12 = (f32[2,2,128]{2,1,0:T(2,128)S(1)}, f32[2,2,128]{2,1,0:T(2,128)}, u32[]{:S(2)}) copy-start(f32[2,2,128]{2,1,0:T(2,128)} %param.32) | copy-start | bytes 6148
  79.6 2.6 copy-start.3
  84.9 2.2 copy-start.2
  88.4 2.8 copy-start.14
  91.0 148.7 %reduce-scatter.3.cloned.1.call-start = ((), (), s32[]{:S(2)}) async-start(), calls=%async_computation.4 | async-start | bytes 10027008 | tf_op jit(solution)/shard_map/reduce_scatter | solution.py:200
  136.6 4.8 %slice-start = ((s8[6291456]{0:T(1024)(128)(4,1)}), s8[4194304]{0:T(1024)(128)(4,1)S(1)}, s32[]{:S(2)}) async-start(s8[6291456]{0:T(1024)(128)(4,1)} %bitcast.152), calls=%async_computation.7 | async-start | bytes 8388608
  139.7 1.7 slice-start.1
  141.4 1.1 copy-start.6
  141.4 1.4 copy-start.7
  147.9 1.0 copy-start.9
  147.9 92.9 %copy-start.1 = (bf16[8,2,2,3072]{3,2,1,0:T(2,128)(2,1)S(1)}, bf16[8,2,2,3072]{3,2,1,0:T(2,128)(2,1)}, u32[]{:S(2)}) copy-start(bf16[8,2,2,3072]{3,2,1,0:T(2,128)(2,1)} %param.18) | copy-start | bytes 589828
  147.9 147.3 %all-gather.8.cloned.1.call-start = ((), (), s32[]{:S(2)}) async-start(), calls=%async_computation.5 | async-start | bytes 3342336 | tf_op jit(solution)/shard_map/all_gather | solution.py:206
  242.9 161.0 %reduce-scatter.5.cloned.1.call-start = ((), (), s32[]{:S(2)}) async-start(), calls=%async_computation.6 | async-start | bytes 6684672 | tf_op jit(solution)/shard_map/reduce_scatter | solution.py:219
  318.4 0.7 copy-start.15
  318.4 0.9 copy-start.10
  318.4 87.9 %copy-start.8 = (bf16[3072,64]{0,1:T(8,128)(2,1)S(1)}, bf16[3072,64]{0,1:T(8,128)(2,1)}, u32[]{:S(2)}) copy-start(bf16[3072,64]{0,1:T(8,128)(2,1)} %param.35) | copy-start | bytes 1179652
  319.1 87.6 %copy-start.11 = (f32[8,2,128]{2,1,0:T(2,128)S(1)}, f32[8,2,128]{2,1,0:T(2,128)}, u32[]{:S(2)}) copy-start(f32[8,2,128]{2,1,0:T(2,128)} %param.20) | copy-start | bytes 24580
  319.1 93.3 %copy-start.5 = (bf16[8,2,3072]{2,1,0:T(2,128)(2,1)S(1)}, bf16[8,2,3072]{2,1,0:T(2,128)(2,1)}, u32[]{:S(2)}) copy-start(bf16[8,2,3072]{2,1,0:T(2,128)(2,1)} %param.19) | copy-start | bytes 294916
  405.4 9.3 %copy-start.4 = (bf16[8,2,2,3072]{3,2,1,0:T(2,128)(2,1)}, bf16[8,2,2,3072]{3,2,1,0:T(2,128)(2,1)S(1)}, u32[]{:S(2)}) copy-start(bf16[8,2,2,3072]{3,2,1,0:T(2,128)(2,1)S(1)} %get-tuple-element.14) | copy-start | bytes 589828
  406.7 7.4 %collective-permute-start = (f32[8,1,128]{2,1,0:T(1,128)S(1)}, f32[8,1,128]{2,1,0:T(1,128)S(1)}, u32[]{:S(2)}, u32[]{:S(2)}) collective-permute-start(f32[8,1,128]{2,1,0:T(1,128)S(1)} %get-tuple-element.42), channel_id=1, source_target_pairs={{0,16},{16,32},{32,48},{48,64},{64,80},{80,96},{96,112},{112,128},... | collective-permute-start | bytes 12296 | tf_op jit(solution)/shard_map/ppermute | solution.py:24
  408.7 5.4 %collective-permute-start.1 = (f32[8,1,128]{2,1,0:T(1,128)S(1)}, f32[8,1,128]{2,1,0:T(1,128)S(1)}, u32[]{:S(2)}, u32[]{:S(2)}) collective-permute-start(f32[8,1,128]{2,1,0:T(1,128)S(1)} %get-tuple-element.43), channel_id=1, source_target_pairs={{16,0},{32,16},{48,32},{64,48},{80,64},{96,80},{112,96},{128,112},... | collective-permute-start | bytes 12296 | tf_op jit(solution)/shard_map/ppermute | solution.py:25
Sparse Core Ops, SparseCore 0:
  17.9 61.6 all-gather.3
  91.1 45.4 all-gather.5
  148.0 91.6 reduce-scatter.2
  243.0 52.1 all-gather.7
  318.6 85.2 reduce-scatter.4

commit v3 on v2

v3 whole, which is shorter than its diff:
```python
import math

import jax
import jax.numpy as jnp
from jax import lax
from jax.sharding import PartitionSpec as P

HEAD_DIM = 128
GRID = 32
NSTEPS = 28


norm_eps = 1e-06
time_shift = 3.0


def padded(value, sides, width):
    for axis, dim in sides:
        size, length = (lax.axis_size(axis), value.shape[dim])
        up = [(i, (i + 1) % size) for i in range(size - 1)]
        down = [(j, i) for i, j in up]
        last = lax.slice_in_dim(value, length - width, length, axis=dim)
        leading = lax.slice_in_dim(value, 0, width, axis=dim)
        before = lax.ppermute(last, axis, up)
        after = lax.ppermute(leading, axis, down)
        value = jnp.concatenate([before, value, after], axis=dim)
    return value


def layer_norm(values):
    average = jnp.mean(values, -1, keepdims=True)
    centred = values - average
    spread = jnp.mean(centred * centred, -1, keepdims=True)
    return centred * lax.rsqrt(spread + norm_eps)


def modulate(hidden, shift, stretch):
    normed = layer_norm(hidden.astype(jnp.float32))
    return ((1.0 + stretch) * normed + shift).astype(jnp.bfloat16)


def rope_tables(row_ids, col_ids):
    lane = jnp.arange(2 * 64, dtype=jnp.int32)
    pair_index = lane // 2
    row_rank = (pair_index - 8).astype(jnp.float32)
    col_rank = (pair_index - 36).astype(jnp.float32)
    log_base = math.log(10000.0)
    row_freq = jnp.where(
        (pair_index >= 8) & (pair_index < 36), jnp.exp(-2.0 * row_rank / 56.0 * log_base), 0.0
    )
    col_freq = jnp.where(pair_index >= 36, jnp.exp(-2.0 * col_rank / 56.0 * log_base), 0.0)
    angles = row_ids[..., None] * row_freq + col_ids[..., None] * col_freq
    sign_table = jnp.where(lane % 2 == 0, -1.0, 1.0).astype(jnp.float32)
    return (jnp.cos(angles), jnp.sin(angles) * sign_table)


def rotate(values, cos_table, sin_table):
    lane = lax.broadcasted_iota(jnp.int32, values.shape, values.ndim - 1)
    swapped = jnp.where(
        lane % 2 == 0, jnp.roll(values, -1, axis=-1), jnp.roll(values, 1, axis=-1)
    )
    return values * cos_table + swapped * sin_table


def head_norm(projected, head_gain):
    squares = jnp.mean(projected * projected, -1, keepdims=True)
    return projected * lax.rsqrt(squares + norm_eps) * head_gain


def sigma_of(step_float):
    level = 1.0 - step_float / NSTEPS
    return time_shift * level / (1.0 + (time_shift - 1.0) * level)


def key_usable(text_len, key_count, text_tile, block_len):
    key_pos = jnp.arange(key_count, dtype=jnp.int32)
    owner_tile = key_pos // block_len
    offset = key_pos % block_len
    text_pos = owner_tile * text_tile + offset
    return jnp.logical_or(offset[None, :] >= text_tile, text_pos[None, :] < text_len[:, None])


def sum_over_tensor(term, owners, narrow):
    if not narrow:
        return lax.psum_scatter(term, "tensor", scatter_dimension=0, tiled=True)
    parts = term.astype(jnp.bfloat16).reshape((owners, -1) + term.shape[1:])
    parts = lax.all_to_all(parts, "tensor", 0, 0, tiled=True)
    return jnp.sum(parts.astype(jnp.float32), 0)


NARROW_SUMS = True


def per_device(
    image_hidden,
    text_hidden,
    latents,
    step_index,
    anchor,
    text_len,
    mod_image,
    mod_text,
    mod_mlp,
    mod_final,
    qkv_image,
    qkv_text,
    proj_image,
    proj_text,
    qk_gain,
    mlp_expand,
    mlp_reduce,
    final_weight,
):
    requests, tile_rows, tile_cols, model_width = image_hidden.shape
    local_cols = qkv_image.shape[2]
    local_heads = local_cols // HEAD_DIM
    owners = lax.axis_size("tensor")
    own_image = tile_rows * tile_cols
    own_text = text_hidden.shape[1]
    slots = own_image + own_text
    image_own = image_hidden.reshape(requests, own_image, model_width).transpose(1, 0, 2)
    text_own = text_hidden.transpose(1, 0, 2)
    image_mod_own = modulate(image_own, mod_image[None, :, 0, :], mod_image[None, :, 1, :])
    text_mod_own = modulate(text_own, mod_text[None, :, 0, :], mod_text[None, :, 1, :])
    joined = jnp.concatenate([image_mod_own, text_mod_own], 0)
    gathered = lax.all_gather(joined, "tensor", axis=0, tiled=True).reshape(
        owners, slots, requests, model_width
    )
    image_count = owners * own_image
    text_tile = owners * own_text
    block_len = text_tile + image_count
    image_mod = gathered[:, :own_image].reshape(image_count * requests, model_width)
    text_mod = gathered[:, own_image:].reshape(text_tile * requests, model_width)
    tile_index = lax.axis_index("tile")
    token_index = jnp.arange(image_count, dtype=jnp.int32)
    owner = token_index // own_image
    within = token_index % own_image
    row_ids = (anchor[None, :, 0] + tile_index * tile_rows + (within // tile_cols)[:, None]).astype(
        jnp.float32
    )
    col_ids = (anchor[None, :, 1] + (owner * tile_cols + within % tile_cols)[:, None]).astype(
        jnp.float32
    )
    cos_table, sin_table = rope_tables(row_ids, col_ids)
    cos_table = cos_table[:, :, None, :]
    sin_table = sin_table[:, :, None, :]
    image_qkv = jnp.dot(
        image_mod, qkv_image.reshape(model_width, 3 * local_cols), preferred_element_type=jnp.float32
    ).reshape(image_count, requests, 3, local_heads, HEAD_DIM)
    text_qkv = jnp.dot(
        text_mod, qkv_text.reshape(model_width, 3 * local_cols), preferred_element_type=jnp.float32
    ).reshape(text_tile, requests, 3, local_heads, HEAD_DIM)
    query = jnp.concatenate(
        [
            head_norm(text_qkv[:, :, 0], qk_gain[1, 0]).astype(jnp.bfloat16),
            rotate(head_norm(image_qkv[:, :, 0], qk_gain[0, 0]), cos_table, sin_table).astype(
                jnp.bfloat16
            ),
        ],
        0,
    )
    keys = jnp.concatenate(
        [
            head_norm(text_qkv[:, :, 1], qk_gain[1, 1]).astype(jnp.bfloat16),
            rotate(head_norm(image_qkv[:, :, 1], qk_gain[0, 1]), cos_table, sin_table).astype(
                jnp.bfloat16
            ),
        ],
        0,
    )
    values = jnp.concatenate([text_qkv[:, :, 2], image_qkv[:, :, 2]], 0).astype(jnp.bfloat16)
    score_scale = 1.0 / math.sqrt(HEAD_DIM)
    kv_all = lax.all_gather(jnp.stack([keys, values], 1), "tile", axis=0, tiled=True)
    keys_all, values_all = kv_all[:, 0], kv_all[:, 1]
    usable = key_usable(text_len, keys_all.shape[0], text_tile, block_len)[:, None, None, :]
    scores = (
        jnp.einsum("qrhd,krhd->rhqk", query, keys_all, preferred_element_type=jnp.float32)
        * score_scale
    )
    row_top = jnp.max(jnp.where(usable, scores, -jnp.inf), -1, keepdims=True)
    weights_raw = jnp.where(usable, jnp.exp(scores - row_top), 0.0)
    weight_sum = jnp.sum(weights_raw, -1, keepdims=True)
    accum = jnp.einsum(
        "rhqk,krhd->rhqd",
        weights_raw.astype(jnp.bfloat16),
        values_all,
        preferred_element_type=jnp.float32,
    )
    attended = (
        (accum / weight_sum).astype(jnp.bfloat16).transpose(2, 0, 1, 3).reshape(
            block_len, requests, local_cols
        )
    )
    text_att = attended[:text_tile].reshape(owners, own_text, requests, local_cols)
    image_att = attended[text_tile:].reshape(owners, own_image, requests, local_cols)
    stacked = jnp.concatenate(
        [
            jnp.concatenate([image_att, jnp.zeros_like(image_att)], 3),
            jnp.concatenate([jnp.zeros_like(text_att), text_att], 3),
        ],
        1,
    ).reshape(owners * slots * requests, 2 * local_cols)
    both_proj = jnp.concatenate([proj_image, proj_text], 0)
    both_term = jnp.dot(stacked, both_proj, preferred_element_type=jnp.float32).reshape(
        owners * slots, requests, model_width
    )
    both_sum = sum_over_tensor(both_term, owners, NARROW_SUMS)
    image_sum = both_sum[:own_image]
    text_sum = both_sum[own_image:]
    image_mid = (image_own.astype(jnp.float32) + mod_image[None, :, 2, :] * image_sum).astype(
        jnp.bfloat16
    )
    mlp_mod = modulate(image_mid, mod_mlp[None, :, 0, :], mod_mlp[None, :, 1, :])
    piece = lax.all_gather(mlp_mod, "tensor", axis=0, tiled=True)
    grown = jnp.dot(piece.reshape(-1, model_width), mlp_expand, preferred_element_type=jnp.float32)
    activated = jax.nn.gelu(grown, approximate=True).astype(jnp.bfloat16)
    text_out = (text_own.astype(jnp.float32) + mod_text[None, :, 2, :] * text_sum).astype(
        jnp.bfloat16
    )
    mlp_term = jnp.dot(activated, mlp_reduce, preferred_element_type=jnp.float32).reshape(
        image_count, requests, model_width
    )
    mlp_sum = sum_over_tensor(mlp_term, owners, NARROW_SUMS)
    image_out = (image_mid.astype(jnp.float32) + mod_mlp[None, :, 2, :] * mlp_sum).astype(
        jnp.bfloat16
    )
    final_in = modulate(image_out, mod_final[None, :, 0, :], mod_final[None, :, 1, :])
    velocity = jnp.dot(
        final_in.reshape(own_image * requests, model_width),
        final_weight,
        preferred_element_type=jnp.float32,
    ).reshape(own_image, requests, final_weight.shape[1])
    velocity = velocity.transpose(1, 0, 2).reshape(
        requests, tile_rows, tile_cols * final_weight.shape[1]
    )
    step_float = step_index.astype(jnp.float32)
    time_delta = sigma_of(step_float + 1.0) - sigma_of(step_float)
    latents_next = latents + time_delta[:, None, None] * velocity
    latents_ext = padded(latents_next, (("tile", 1),), 1)
    image_out = image_out.transpose(1, 0, 2).reshape(requests, tile_rows, tile_cols, model_width)
    return (image_out, text_out.transpose(1, 0, 2), latents_ext)


def solution(mesh):
    return jax.shard_map(
        per_device,
        mesh=mesh,
        in_specs=(
            P(None, "tile", "tensor", None),
            P(None, ("tile", "tensor"), None),
            P(None, "tile", "tensor"),
            P(),
            P(),
            P(),
            P(),
            P(),
            P(),
            P(),
            P(None, None, "tensor"),
            P(None, None, "tensor"),
            P("tensor", None),
            P("tensor", None),
            P(),
            P(None, "tensor"),
            P("tensor", None),
            P(),
        ),
        out_specs=(
            P(None, "tile", "tensor", None),
            P(None, ("tile", "tensor"), None),
            P(None, "tile", "tensor"),
        ),
        check_vma=False,
    )
```

time: 425 us -> 365 us (0.86)
  waiting for transfers between devices: 325 us -> 261 us
  starting transfers between devices: 6.17 us -> 17.5 us
  local copies, waits for them, and re-layouts: 34.3 us -> 25 us
  other arithmetic: 19.6 us -> 26.8 us
  matrix products: 21.6 us -> 16.7 us
    reduce_scatter x2 -> x0, waiting for transfers between devices: 175 us -> none  [the longest x1 90.9 us: per_device(): lax.psum_scatter(both_term, 'tensor', scatter_dimension=1, tiled=True)]
    all_to_all x0 -> x2, waiting for transfers between devices: none -> 117 us  [sum_over_tensor(): parts = lax.all_to_all(parts, 'tensor', 0, 0, tiled=True)]
    all_to_all x0 -> x2, starting transfers between devices: none -> 11.7 us  [sum_over_tensor(): parts = lax.all_to_all(parts, 'tensor', 0, 0, tiled=True)]
    reshape x5 -> x1, local copies, waits for them, and re-layouts: 9.36 us -> 0.09 us  [per_device(): velocity.transpose(1, 0, 2)]
    reduce_sum x0 -> x2, other arithmetic: none -> 5.89 us  [sum_over_tensor(): return jnp.sum(parts.astype(jnp.float32), 0)]
    all_gather x3, waiting for transfers between devices: 150 us -> 145 us  [the longest x1 50.5 us: per_device(): piece = lax.all_gather(mlp_mod, 'tensor', axis=0, tiled=True)]
    all_gather x1 -> x0, local copies, waits for them, and re-layouts: 5.33 us -> none  [per_device(): lax.all_gather(mlp_mod.reshape(requests, own_image, model_width), 'tensor...]
    unnamed x39 -> x64, local copies, waits for them, and re-layouts: 11.8 us -> 11 us
  transfers between devices with their start and end apart: 7 -> 7, of which waited for: 5 -> 5; matrix products, arithmetic and copies ran while one was open for 3% -> 5% of each run, Pallas kernels for 0% -> 0%
where the time goes in v3:
time: 365 us; the launch traced here: 362 us
  waiting for transfers between devices  261 us (72%)
  other arithmetic  26.8 us (7%)
  local copies, waits for them, and re-layouts  25 us (7%)
  starting transfers between devices  17.5 us (5%)
  matrix products  16.7 us (5%)
  between operations  14.3 us (4%)
    all_to_all x2, waiting for transfers between devices, sum_over_tensor(): parts = lax.all_to_all(parts, 'tensor', 0, 0, tiled=True)  117 us
    all_gather x1, waiting for transfers between devices, per_device(): piece = lax.all_gather(mlp_mod, 'tensor', axis=0, tiled=True)  50.5 us
    all_gather x1, waiting for transfers between devices, per_device(): lax.all_gather(joined, 'tensor', axis=0, tiled=True)  48.7 us
    all_gather x1, waiting for transfers between devices, per_device(): lax.all_gather(jnp.stack([keys, values], 1), 'tile', axis=0, tiled=True)  45.4 us
    all_to_all x2, starting transfers between devices, sum_over_tensor(): parts = lax.all_to_all(parts, 'tensor', 0, 0, tiled=True)  11.7 us
    unnamed x64, local copies, waits for them, and re-layouts  11 us
    dot_general x1, matrix products, per_device(): jnp.dot(activated, mlp_reduce, preferred_element_type=jnp.float32)  7.79 us
  transfers between devices with their start and end apart: 7, of which 5 were waited for; matrix products, arithmetic and copies ran while one was open for 5% of the time, Pallas kernels for 0%

profile of v3, /device:TPU:32, one launch (start us, length us, event | category | flops | bytes accessed | tf_op | source)
XLA Modules:
  0.0 361.6 jit_solution(4454665537678521913)
XLA Ops:
  7.2 1.1 copy.82
  8.5 0.2 multiply_reduce_fusion
  8.7 1.7 slice_bitcast_fusion.11
  10.4 1.6 slice_bitcast_fusion.6
  12.0 1.0 bitcast_reduce_fusion
  13.0 1.1 fusion.91
  14.4 0.7 pad_maximum_fusion
  15.2 4.3 %copy.85 = bf16[3072,3,128]{0,2,1:T(8,128)(2,1)} copy(bf16[3072,3,128]{2,0,1:T(8,128)(2,1)} %param.28) | data formatting | bytes 4718592 | tf_op args[10]
  19.6 0.7 copy.89
  20.3 0.7 copy.90
  21.0 4.3 %copy.84 = bf16[3072,3,128]{0,2,1:T(8,128)(2,1)} copy(bf16[3072,3,128]{2,0,1:T(8,128)(2,1)} %param.29) | data formatting | bytes 4718592 | tf_op args[11]
  25.3 0.6 and_select_fusion.2
  25.9 0.6 compare_and_fusion
  26.5 0.6 compare_select_fusion
  27.1 0.6 iota_and_fusion
  27.7 0.6 slice_bitcast_fusion.16
  28.2 48.7 %all-gather.4.cloned.1.call-done = bf16[96,8,3072]{2,1,0:T(8,128)(2,1)} async-done(((bf16[6,8,3072]{2,1,0:T(8,128)(2,1)}), bf16[96,8,3072]{2,1,0:T(8,128)(2,1)}) %all-gather.4.cloned.1.call-update) | async-done | bytes 4718608 | tf_op jit(solution)/shard_map/all_gather | solution.py:126
  76.9 2.3 slice.174
  79.3 0.3 copy-done.2
  79.6 1.8 fusion.21
  81.4 0.8 multiply_reduce_fusion.2
  82.2 0.8 copy.87
  83.0 0.7 copy.88
  83.7 0.8 copy.92
  84.5 0.7 copy.93
  85.2 1.0 multiply_multiply_fusion.2
  86.2 0.2 fusion.123
  86.4 0.2 fusion.122
  86.6 1.6 slice.172
  88.3 0.3 copy-done.1
  88.6 1.0 fusion.24
  90.1 1.4 fusion.81
  91.4 0.8 maximum_maximum_fusion
  92.4 45.4 %all-gather.6.cloned.1.call-done = bf16[1536,2,8,1,128]{4,2,0,3,1:T(8,128)(2,1)} async-done(((bf16[96,2,8,1,128]{4,2,0,3,1:T(8,128)(2,1)}), bf16[1536,2,8,1,128]{4,2,0,3,1:T(8,128)(2,1)}) %all-gather.6.cloned.1.call-update) | async-done | bytes 6291472 | tf_op jit(solution)/shard_map/all_gather | solution.py:173
  137.8 3.1 slice_bitcast_fusion.1
  140.9 1.2 fusion.9
  142.1 1.6 fusion.128
  143.7 1.1 fusion.39
  144.9 0.2 fusion.58
  145.1 0.2 copy.97
  145.3 3.6 convolution_convert_fusion
  148.9 7.0 %all-to-all-start = ((bf16[16,6,8,3072]{3,2,1,0:T(8,128)(2,1)}), bf16[16,6,8,3072]{3,2,1,0:T(8,128)(2,1)}, u32[]{:S(2)}, u32[]{:S(2)}) async-start(bf16[16,6,8,3072]{3,2,1,0:T(8,128)(2,1)} %bitcast.171), calls=%async_computation | async-start | bytes 9437184 | tf_op jit(solution)/shard_map/all_to_all | solution.py:87
  155.9 0.2 all-gather.8.cloned.1.call-start
  156.2 0.7 slice_bitcast_fusion.8
  156.9 70.3 %all-to-all-done = bf16[16,6,8,3072]{3,2,1,0:T(8,128)(2,1)} async-done(((bf16[16,6,8,3072]{3,2,1,0:T(8,128)(2,1)}), bf16[16,6,8,3072]{3,2,1,0:T(8,128)(2,1)}, u32[]{:S(2)}, u32[]{:S(2)}) %all-to-all-start) | async-done | bytes 4718624 | tf_op jit(solution)/shard_map/all_to_all | solution.py:87
  227.2 3.3 convert_reduce_fusion
  230.5 0.9 fusion.73
  231.6 0.2 fusion.63
  231.8 0.8 fusion.66
  232.7 50.5 %all-gather.8.cloned.1.call-done = bf16[64,8,3072]{2,1,0:T(8,128)(2,1)} async-done(((bf16[4,8,3072]{2,1,0:T(8,128)(2,1)}), bf16[64,8,3072]{2,1,0:T(8,128)(2,1)}) %all-gather.8.cloned.1.call-update) | async-done | bytes 3145744 | tf_op jit(solution)/shard_map/all_gather | solution.py:214
  283.2 7.8 %convolution_convert_fusion.1 = bf16[512,3072]{1,0:T(8,128)(2,1)} fusion(bf16[384,3072]{1,0:T(8,128)(2,1)S(1)} %copy-done, bf16[3072,384]{1,0:T(8,128)(2,1)} %param.33, bf16[64,8,3072]{2,1,0:T(8,128)(2,1)} %all-gather.8.cloned.1.call-done), kind=kOutput, calls=%fused_computation.7 | convolution fusion | flops 2419261440 | bytes 11010048 | tf_op jit(solution)/shard_map/dot_general | solution.py:220
  291.0 4.7 %all-to-all-start.1 = ((bf16[16,4,8,3072]{3,2,1,0:T(8,128)(2,1)}), bf16[16,4,8,3072]{3,2,1,0:T(8,128)(2,1)}, u32[]{:S(2)}, u32[]{:S(2)}) async-start(bf16[16,4,8,3072]{3,2,1,0:T(8,128)(2,1)} %bitcast.176), calls=%async_computation.1 | async-start | bytes 6291456 | tf_op jit(solution)/shard_map/all_to_all | solution.py:87
  295.9 0.7 copy_bitcast_fusion
  296.6 46.2 %all-to-all-done.1 = bf16[16,4,8,3072]{3,2,1,0:T(8,128)(2,1)} async-done(((bf16[16,4,8,3072]{3,2,1,0:T(8,128)(2,1)}), bf16[16,4,8,3072]{3,2,1,0:T(8,128)(2,1)}, u32[]{:S(2)}, u32[]{:S(2)}) %all-to-all-start.1) | async-done | bytes 3145760 | tf_op jit(solution)/shard_map/all_to_all | solution.py:87
  342.8 2.6 convert_reduce_fusion.1
  345.4 0.2 convert_reduce_fusion.3
  345.6 0.2 fusion.67
  345.8 0.3 convolution_bitcast_fusion
  346.3 1.9 collective-permute-start
  348.2 3.6 %collective-permute-start.1 = (f32[8,1,128]{2,1,0:T(1,128)S(1)}, f32[8,1,128]{2,1,0:T(1,128)S(1)}, u32[]{:S(2)}, u32[]{:S(2)}) collective-permute-start(f32[8,1,128]{2,1,0:T(1,128)S(1)} %get-tuple-element.49), channel_id=1, source_target_pairs={{16,0},{32,16},{48,32},{64,48},{80,64},{96,80},{112,96},{128,112},... | collective-permute-start | bytes 12296 | tf_op jit(solution)/shard_map/ppermute | solution.py:25
  351.9 0.9 fusion.101
  352.8 0.7 copy.102
  353.6 0.9 copy.101
  354.4 0.6 pad_maximum_fusion.1
  (101 shorter events, 1.7 us)
Async XLA Ops:
  7.2 276.1 %copy-start = (bf16[384,3072]{1,0:T(8,128)(2,1)S(1)}, bf16[384,3072]{1,0:T(8,128)(2,1)}, u32[]{:S(2)}) copy-start(bf16[384,3072]{1,0:T(8,128)(2,1)} %param.34) | copy-start | bytes 7077892
  7.2 7.1 %copy-start.3 = (bf16[8,2,3072]{2,1,0:T(2,128)(2,1)S(1)}, bf16[8,2,3072]{2,1,0:T(2,128)(2,1)}, u32[]{:S(2)}) copy-start(bf16[8,2,3072]{2,1,0:T(2,128)(2,1)} %param.19) | copy-start | bytes 294916
  7.2 69.7 %all-gather.4.cloned.1.call-start = ((), (), s32[]{:S(2)}) async-start(), calls=%async_computation.2 | async-start | bytes 5013504 | tf_op jit(solution)/shard_map/all_gather | solution.py:126
  14.3 5.3 %copy-start.21 = (s32[8,2]{0,1:T(2,128)S(1)}, s32[8,2]{0,1:T(2,128)}, u32[]{:S(2)}) copy-start(s32[8,2]{0,1:T(2,128)} %param.22) | copy-start | bytes 196
  15.1 122.7 %all-gather.6.cloned.1.call-start = ((), (), s32[]{:S(2)}) async-start(), calls=%async_computation.3 | async-start | bytes 6684672 | tf_op jit(solution)/shard_map/all_gather | solution.py:173
  19.5 8.1 %copy-start.20 = (f32[2,2,128]{2,1,0:T(2,128)S(1)}, f32[2,2,128]{2,1,0:T(2,128)}, u32[]{:S(2)}) copy-start(f32[2,2,128]{2,1,0:T(2,128)} %param.32) | copy-start | bytes 6148
  76.9 2.6 copy-start.2
  86.4 2.1 copy-start.1
  88.5 1.3 copy-start.18
  88.6 1.3 copy-start.19
  88.6 1.4 copy-start.15
  88.6 1.4 copy-start.16
  88.6 1.4 copy-start.22
  88.6 1.4 copy-start.23
  88.6 1.4 copy-start.24
  88.6 1.4 copy-start.25
  88.6 1.4 copy-start.26
  88.6 1.4 copy-start.27
  89.6 2.7 copy-start.28
  143.7 1.6 copy-start.5
  143.7 1.6 copy-start.6
  148.9 7.2 %copy-start.13 = (f32[8,3,3072]{2,0,1:T(8,128)S(1)}, f32[8,3,3072]{2,0,1:T(8,128)}, u32[]{:S(2)}) copy-start(f32[8,3,3072]{2,0,1:T(8,128)} %param.26) | copy-start | bytes 884740
  148.9 78.3 %all-to-all-start = ((bf16[16,6,8,3072]{3,2,1,0:T(8,128)(2,1)}), bf16[16,6,8,3072]{3,2,1,0:T(8,128)(2,1)}, u32[]{:S(2)}, u32[]{:S(2)}) async-start(bf16[16,6,8,3072]{3,2,1,0:T(8,128)(2,1)} %bitcast.171), calls=%async_computation | async-start | bytes 9437184 | tf_op jit(solution)/shard_map/all_to_all | solution.py:87
  155.9 127.3 %all-gather.8.cloned.1.call-start = ((), (), s32[]{:S(2)}) async-start(), calls=%async_computation.4 | async-start | bytes 3342336 | tf_op jit(solution)/shard_map/all_gather | solution.py:214
  227.2 4.6 %copy-start.8 = (f32[8,3072]{1,0:T(8,128)S(1)}, f32[8,3072]{1,0:T(8,128)}, u32[]{:S(2)}) copy-start(f32[8,3072]{1,0:T(8,128)} %get-tuple-element.31) | copy-start | bytes 294916
  227.2 4.6 %copy-start.9 = (f32[8,3072]{1,0:T(8,128)S(1)}, f32[8,3072]{1,0:T(8,128)}, u32[]{:S(2)}) copy-start(f32[8,3072]{1,0:T(8,128)} %get-tuple-element.32) | copy-start | bytes 294916
  291.0 4.7 %copy-start.29 = (s32[8]{0:T(128)S(1)}, s32[8]{0:T(128)}, u32[]{:S(2)}) copy-start(s32[8]{0:T(128)} %param.21) | copy-start | bytes 100
  291.0 4.7 %copy-start.14 = (f32[8,2,3072]{2,1,0:T(2,128)S(1)}, f32[8,2,3072]{2,1,0:T(2,128)}, u32[]{:S(2)}) copy-start(f32[8,2,3072]{2,1,0:T(2,128)} %param.27) | copy-start | bytes 589828
  291.0 51.8 %all-to-all-start.1 = ((bf16[16,4,8,3072]{3,2,1,0:T(8,128)(2,1)}), bf16[16,4,8,3072]{3,2,1,0:T(8,128)(2,1)}, u32[]{:S(2)}, u32[]{:S(2)}) async-start(bf16[16,4,8,3072]{3,2,1,0:T(8,128)(2,1)} %bitcast.176), calls=%async_computation.1 | async-start | bytes 6291456 | tf_op jit(solution)/shard_map/all_to_all | solution.py:87
  295.7 49.7 %copy-start.7 = (f32[8,3072]{1,0:T(8,128)S(1)}, f32[8,3072]{1,0:T(8,128)}, u32[]{:S(2)}) copy-start(f32[8,3072]{1,0:T(8,128)} %get-tuple-element.30) | copy-start | bytes 294916
  295.7 50.5 %copy-start.17 = (f32[8,2,128]{2,1,0:T(2,128)S(1)}, f32[8,2,128]{2,1,0:T(2,128)}, u32[]{:S(2)}) copy-start(f32[8,2,128]{2,1,0:T(2,128)} %param.20) | copy-start | bytes 24580
  295.8 56.1 %copy-start.4 = (bf16[8,2,3072]{2,1,0:T(2,128)(2,1)S(1)}, bf16[8,2,3072]{2,1,0:T(2,128)(2,1)}, u32[]{:S(2)}) copy-start(bf16[8,2,3072]{2,1,0:T(2,128)(2,1)} %param.19) | copy-start | bytes 294916
  342.8 3.0 copy-start.10
  342.8 3.0 copy-start.11
  342.8 3.0 copy-start.12
  346.3 8.1 %collective-permute-start = (f32[8,1,128]{2,1,0:T(1,128)S(1)}, f32[8,1,128]{2,1,0:T(1,128)S(1)}, u32[]{:S(2)}, u32[]{:S(2)}) collective-permute-start(f32[8,1,128]{2,1,0:T(1,128)S(1)} %get-tuple-element.48), channel_id=1, source_target_pairs={{0,16},{16,32},{32,48},{48,64},{64,80},{80,96},{96,112},{112,128},... | collective-permute-start | bytes 12296 | tf_op jit(solution)/shard_map/ppermute | solution.py:24
  348.2 6.2 %collective-permute-start.1 = (f32[8,1,128]{2,1,0:T(1,128)S(1)}, f32[8,1,128]{2,1,0:T(1,128)S(1)}, u32[]{:S(2)}, u32[]{:S(2)}) collective-permute-start(f32[8,1,128]{2,1,0:T(1,128)S(1)} %get-tuple-element.49), channel_id=1, source_target_pairs={{16,0},{32,16},{48,32},{64,48},{80,64},{96,80},{112,96},{128,112},... | collective-permute-start | bytes 12296 | tf_op jit(solution)/shard_map/ppermute | solution.py:25
Sparse Core Ops, SparseCore 0:
  15.3 61.6 all-gather.3
  92.4 45.4 all-gather.5
  232.8 50.3 all-gather.7

commit v4 on v3

--- a/solution.py
+++ b/solution.py
@@ -122,15 +122,16 @@
     text_own = text_hidden.transpose(1, 0, 2)
     image_mod_own = modulate(image_own, mod_image[None, :, 0, :], mod_image[None, :, 1, :])
     text_mod_own = modulate(text_own, mod_text[None, :, 0, :], mod_text[None, :, 1, :])
-    joined = jnp.concatenate([image_mod_own, text_mod_own], 0)
-    gathered = lax.all_gather(joined, "tensor", axis=0, tiled=True).reshape(
-        owners, slots, requests, model_width
-    )
     image_count = owners * own_image
     text_tile = owners * own_text
     block_len = text_tile + image_count
-    image_mod = gathered[:, :own_image].reshape(image_count * requests, model_width)
-    text_mod = gathered[:, own_image:].reshape(text_tile * requests, model_width)
+    image_mod = lax.all_gather(image_mod_own, "tensor", axis=0, tiled=True).reshape(
+        image_count * requests, model_width
+    )
+    text_mod = lax.all_to_all(
+        jnp.broadcast_to(text_mod_own[None], (owners,) + text_mod_own.shape), "tensor", 0, 0,
+        tiled=True,
+    ).reshape(text_tile * requests, model_width)
     tile_index = lax.axis_index("tile")
     token_index = jnp.arange(image_count, dtype=jnp.int32)
     owner = token_index // own_image
@@ -191,22 +192,17 @@
             block_len, requests, local_cols
         )
     )
-    text_att = attended[:text_tile].reshape(owners, own_text, requests, local_cols)
-    image_att = attended[text_tile:].reshape(owners, own_image, requests, local_cols)
-    stacked = jnp.concatenate(
-        [
-            jnp.concatenate([image_att, jnp.zeros_like(image_att)], 3),
-            jnp.concatenate([jnp.zeros_like(text_att), text_att], 3),
-        ],
-        1,
-    ).reshape(owners * slots * requests, 2 * local_cols)
-    both_proj = jnp.concatenate([proj_image, proj_text], 0)
-    both_term = jnp.dot(stacked, both_proj, preferred_element_type=jnp.float32).reshape(
-        owners * slots, requests, model_width
-    )
-    both_sum = sum_over_tensor(both_term, owners, NARROW_SUMS)
-    image_sum = both_sum[:own_image]
-    text_sum = both_sum[own_image:]
+    text_att = attended[:text_tile].reshape(text_tile * requests, local_cols)
+    image_att = attended[text_tile:].reshape(image_count * requests, local_cols)
+    image_term = jnp.dot(image_att, proj_image, preferred_element_type=jnp.float32).reshape(
+        image_count, requests, model_width
+    )
+    image_sum = sum_over_tensor(image_term, owners, NARROW_SUMS)
+    text_term = jnp.dot(text_att, proj_text, preferred_element_type=jnp.float32).reshape(
+        text_tile, requests, model_width
+    )
+    after_image = (image_sum[0, 0, 0] * 0.0).astype(text_term.dtype)
+    text_sum = sum_over_tensor(text_term + after_image, owners, NARROW_SUMS)
     image_mid = (image_own.astype(jnp.float32) + mod_image[None, :, 2, :] * image_sum).astype(
         jnp.bfloat16
     )

time: 365 us -> 346 us (0.948)
  waiting for transfers between devices: 261 us -> 223 us
  starting transfers between devices: 17.5 us -> 28.9 us
  matrix products: 16.7 us -> 24.4 us
    all_to_all x2 -> x3, waiting for transfers between devices: 117 us -> 90.7 us  [sum_over_tensor(): parts = lax.all_to_all(parts, 'tensor', 0, 0, tiled=True)]
    all_gather x1, waiting for transfers between devices: 48.7 us -> 23.3 us  [per_device(): lax.all_gather(image_mod_own, 'tensor', axis=0, tiled=True)]
    all_to_all x0 -> x1, waiting for transfers between devices: none -> 14.9 us  [per_device(): lax.all_to_all(jnp.broadcast_to(text_mod_own[None], (owners,) + text_mod_...]
    all_to_all x0 -> x1, starting transfers between devices: none -> 7.08 us  [per_device(): lax.all_to_all(jnp.broadcast_to(text_mod_own[None], (owners,) + text_mod_...]
    all_to_all x2 -> x3, starting transfers between devices: 11.7 us -> 16.1 us  [sum_over_tensor(): parts = lax.all_to_all(parts, 'tensor', 0, 0, tiled=True)]
    unnamed x64 -> x50, local copies, waits for them, and re-layouts: 11 us -> 10.3 us
  transfers between devices with their start and end apart: 7 -> 9, of which waited for: 5 -> 6; matrix products, arithmetic and copies ran while one was open for 5% -> 12% of each run, Pallas kernels for 0% -> 0%
where the time goes in v4:
time: 346 us; the launch traced here: 342 us
  waiting for transfers between devices  223 us (64%)
  starting transfers between devices  28.9 us (8%)
  other arithmetic  26.9 us (8%)
  matrix products  24.4 us (7%)
  local copies, waits for them, and re-layouts  24 us (7%)
  between operations  14.8 us (4%)
    all_to_all x3, waiting for transfers between devices, sum_over_tensor(): parts = lax.all_to_all(parts, 'tensor', 0, 0, tiled=True)  90.7 us
    all_gather x1, waiting for transfers between devices, per_device(): piece = lax.all_gather(mlp_mod, 'tensor', axis=0, tiled=True)  50.5 us
    all_gather x1, waiting for transfers between devices, per_device(): lax.all_gather(jnp.stack([keys, values], 1), 'tile', axis=0, tiled=True)  43.8 us
    all_gather x1, waiting for transfers between devices, per_device(): lax.all_gather(image_mod_own, 'tensor', axis=0, tiled=True)  23.3 us
    all_to_all x3, starting transfers between devices, sum_over_tensor(): parts = lax.all_to_all(parts, 'tensor', 0, 0, tiled=True)  16.1 us
    all_to_all x1, waiting for transfers between devices, per_device(): lax.all_to_all(jnp.broadcast_to(text_mod_own[None], (owners,) + text_mod_...  14.9 us
    unnamed x50, local copies, waits for them, and re-layouts  10.3 us
    dot_general x1, matrix products, per_device(): jnp.dot(activated, mlp_reduce, preferred_element_type=jnp.float32)  7.78 us
  transfers between devices with their start and end apart: 9, of which 6 were waited for; matrix products, arithmetic and copies ran while one was open for 12% of the time, Pallas kernels for 0%

profile of v4, /device:TPU:32, one launch (start us, length us, event | category | flops | bytes accessed | tf_op | source)
XLA Modules:
  0.0 342.3 jit_solution(14958489612896935357)
XLA Ops:
  7.2 1.1 copy.85
  8.5 0.2 multiply_reduce_fusion
  8.7 1.7 slice_bitcast_fusion.12
  10.4 0.8 add_convert_fusion.1
  11.2 1.0 fusion.88
  12.4 0.6 slice_bitcast_fusion.7
  13.2 1.3 broadcast_in_dim.30
  14.5 7.1 %all-to-all-start = ((bf16[16,2,8,3072]{3,2,1,0:T(8,128)(2,1)}), bf16[16,2,8,3072]{3,2,1,0:T(8,128)(2,1)}, u32[]{:S(2)}, u32[]{:S(2)}) async-start(bf16[16,2,8,3072]{3,2,1,0:T(8,128)(2,1)} %broadcast_in_dim.30), calls=%async_computation | async-start | bytes 3145728 | tf_op jit(solution)/shard_map/all_to_all | solution.py:131
  21.7 4.3 %copy.88 = bf16[3072,3,128]{0,2,1:T(8,128)(2,1)} copy(bf16[3072,3,128]{2,0,1:T(8,128)(2,1)} %param.28) | data formatting | bytes 4718592 | tf_op args[10]
  26.1 0.7 copy.92
  26.8 0.7 copy.93
  27.5 4.3 %copy.87 = bf16[3072,3,128]{0,2,1:T(8,128)(2,1)} copy(bf16[3072,3,128]{2,0,1:T(8,128)(2,1)} %param.29) | data formatting | bytes 4718592 | tf_op args[11]
  31.7 0.6 and_select_fusion.2
  32.3 0.6 compare_and_fusion
  32.9 0.6 compare_select_fusion
  33.5 0.6 iota_and_fusion
  34.1 14.9 %all-to-all-done = bf16[16,2,8,3072]{3,2,1,0:T(8,128)(2,1)} async-done(((bf16[16,2,8,3072]{3,2,1,0:T(8,128)(2,1)}), bf16[16,2,8,3072]{3,2,1,0:T(8,128)(2,1)}, u32[]{:S(2)}, u32[]{:S(2)}) %all-to-all-start) | async-done | bytes 1572896 | tf_op jit(solution)/shard_map/all_to_all | solution.py:131
  48.9 3.1 fusion.26
  52.3 0.6 fusion.105
  52.9 0.8 multiply_convert_fusion.1
  53.7 23.3 %all-gather.4.cloned.1.call-done = bf16[64,8,3072]{2,1,0:T(8,128)(2,1)} async-done(((bf16[4,8,3072]{2,1,0:T(8,128)(2,1)}), bf16[64,8,3072]{2,1,0:T(8,128)(2,1)}) %all-gather.4.cloned.1.call-update) | async-done | bytes 3145744 | tf_op jit(solution)/shard_map/all_gather | solution.py:128
  76.9 4.4 %fusion.21 = f32[64,8,3,1,128]{4,1,2,0,3:T(8,128)S(1)} fusion(bf16[3072,3,128]{0,2,1:T(8,128)(2,1)} %copy.88, bf16[64,8,3072]{2,1,0:T(8,128)(2,1)} %all-gather.4.cloned.1.call-done), kind=kOutput, calls=%fused_computation.29 | convolution fusion | flops 1207959552 | bytes 6291456 | tf_op jit(solution)/shard_map/dot_general | solution.py:148
  81.3 0.8 multiply_reduce_fusion.2
  82.2 0.8 copy.90
  83.0 0.7 copy.91
  83.7 0.8 copy.95
  84.5 0.7 copy.96
  85.2 1.0 multiply_multiply_fusion.2
  86.4 0.2 fusion.124
  86.7 2.1 fusion.82
  88.8 0.8 maximum_maximum_fusion
  89.8 0.9 maximum_bitcast_fusion
  90.6 43.8 %all-gather.6.cloned.1.call-done = bf16[1536,2,8,1,128]{4,2,0,3,1:T(8,128)(2,1)} async-done(((bf16[96,2,8,1,128]{4,2,0,3,1:T(8,128)(2,1)}), bf16[1536,2,8,1,128]{4,2,0,3,1:T(8,128)(2,1)}) %all-gather.6.cloned.1.call-update) | async-done | bytes 6291472 | tf_op jit(solution)/shard_map/all_gather | solution.py:174
  134.5 3.1 slice_bitcast_fusion.1
  137.5 1.2 fusion.12
  138.7 1.6 fusion.130
  140.4 1.1 fusion.39
  141.5 2.6 convolution_convert_fusion.1
  144.1 7.0 %all-to-all-start.1 = ((bf16[16,4,8,3072]{3,2,1,0:T(8,128)(2,1)}), bf16[16,4,8,3072]{3,2,1,0:T(8,128)(2,1)}, u32[]{:S(2)}, u32[]{:S(2)}) async-start(bf16[16,4,8,3072]{3,2,1,0:T(8,128)(2,1)} %bitcast.189), calls=%async_computation.1 | async-start | bytes 6291456 | tf_op jit(solution)/shard_map/all_to_all | solution.py:87
  151.2 0.7 slice_bitcast_fusion.9
  151.9 47.9 %all-to-all-done.1 = bf16[16,4,8,3072]{3,2,1,0:T(8,128)(2,1)} async-done(((bf16[16,4,8,3072]{3,2,1,0:T(8,128)(2,1)}), bf16[16,4,8,3072]{3,2,1,0:T(8,128)(2,1)}, u32[]{:S(2)}, u32[]{:S(2)}) %all-to-all-start.1) | async-done | bytes 3145760 | tf_op jit(solution)/shard_map/all_to_all | solution.py:87
  199.8 2.5 convert_reduce_fusion.1
  202.5 0.2 fusion.64
  202.8 0.8 fusion.67
  203.6 0.8 slice_bitcast_fusion.13
  204.5 0.5 slice.178
  205.6 3.0 fusion.5
  208.6 4.5 %all-to-all-start.3 = ((bf16[16,2,8,3072]{3,2,1,0:T(8,128)(2,1)}), bf16[16,2,8,3072]{3,2,1,0:T(8,128)(2,1)}, u32[]{:S(2)}, u32[]{:S(2)}) async-start(bf16[16,2,8,3072]{3,2,1,0:T(8,128)(2,1)} %bitcast.190), calls=%async_computation.3 | async-start | bytes 3145728 | tf_op jit(solution)/shard_map/all_to_all | solution.py:87
  213.0 50.5 %all-gather.8.cloned.1.call-done = bf16[64,8,3072]{2,1,0:T(8,128)(2,1)} async-done(((bf16[4,8,3072]{2,1,0:T(8,128)(2,1)}), bf16[64,8,3072]{2,1,0:T(8,128)(2,1)}) %all-gather.8.cloned.1.call-update) | async-done | bytes 3145744 | tf_op jit(solution)/shard_map/all_gather | solution.py:210
  263.5 7.8 %convolution_convert_fusion = bf16[512,3072]{1,0:T(8,128)(2,1)} fusion(bf16[384,3072]{1,0:T(8,128)(2,1)S(1)} %copy-done, bf16[3072,384]{1,0:T(8,128)(2,1)} %param.33, bf16[64,8,3072]{2,1,0:T(8,128)(2,1)} %all-gather.8.cloned.1.call-done), kind=kOutput, calls=%fused_computation.6 | convolution fusion | flops 2419261440 | bytes 11010048 | tf_op jit(solution)/shard_map/dot_general | solution.py:216
  271.3 4.7 %all-to-all-start.2 = ((bf16[16,4,8,3072]{3,2,1,0:T(8,128)(2,1)}), bf16[16,4,8,3072]{3,2,1,0:T(8,128)(2,1)}, u32[]{:S(2)}, u32[]{:S(2)}) async-start(bf16[16,4,8,3072]{3,2,1,0:T(8,128)(2,1)} %bitcast.191), calls=%async_computation.2 | async-start | bytes 6291456 | tf_op jit(solution)/shard_map/all_to_all | solution.py:87
  276.0 1.2 fusion.128
  277.2 0.7 copy_bitcast_fusion
  277.9 1.6 convert_reduce_fusion.2
  279.6 0.7 copy.106
  280.4 42.8 %all-to-all-done.2 = bf16[16,4,8,3072]{3,2,1,0:T(8,128)(2,1)} async-done(((bf16[16,4,8,3072]{3,2,1,0:T(8,128)(2,1)}), bf16[16,4,8,3072]{3,2,1,0:T(8,128)(2,1)}, u32[]{:S(2)}, u32[]{:S(2)}) %all-to-all-start.2) | async-done | bytes 3145760 | tf_op jit(solution)/shard_map/all_to_all | solution.py:87
  323.2 2.5 convert_reduce_fusion
  325.8 0.2 fusion.68
  326.1 1.3 convolution_bitcast_fusion
  327.6 1.9 collective-permute-start
  329.5 3.6 %collective-permute-start.1 = (f32[8,1,128]{2,1,0:T(1,128)S(1)}, f32[8,1,128]{2,1,0:T(1,128)S(1)}, u32[]{:S(2)}, u32[]{:S(2)}) collective-permute-start(f32[8,1,128]{2,1,0:T(1,128)S(1)} %get-tuple-element.52), channel_id=1, source_target_pairs={{16,0},{32,16},{48,32},{64,48},{80,64},{96,80},{112,96},{128,112},... | collective-permute-start | bytes 12296 | tf_op jit(solution)/shard_map/ppermute | solution.py:25
  333.1 1.1 fusion.74
  334.2 0.9 copy.105
  335.1 0.6 pad_maximum_fusion
  (91 shorter events, 1.9 us)
Async XLA Ops:
  7.2 256.3 %copy-start = (bf16[384,3072]{1,0:T(8,128)(2,1)S(1)}, bf16[384,3072]{1,0:T(8,128)(2,1)}, u32[]{:S(2)}) copy-start(bf16[384,3072]{1,0:T(8,128)(2,1)} %param.34) | copy-start | bytes 7077892
  7.2 5.1 %copy-start.2 = (bf16[8,2,3072]{2,1,0:T(2,128)(2,1)S(1)}, bf16[8,2,3072]{2,1,0:T(2,128)(2,1)}, u32[]{:S(2)}) copy-start(bf16[8,2,3072]{2,1,0:T(2,128)(2,1)} %param.19) | copy-start | bytes 294916
  7.2 5.2 %copy-start.11 = (f32[8,3,3072]{2,0,1:T(8,128)S(1)}, f32[8,3,3072]{2,0,1:T(8,128)}, u32[]{:S(2)}) copy-start(f32[8,3,3072]{2,0,1:T(8,128)} %param.25) | copy-start | bytes 884740
  7.2 69.7 %all-gather.4.cloned.1.call-start = ((), (), s32[]{:S(2)}) async-start(), calls=%async_computation.4 | async-start | bytes 3342336 | tf_op jit(solution)/shard_map/all_gather | solution.py:128
  14.5 34.4 %all-to-all-start = ((bf16[16,2,8,3072]{3,2,1,0:T(8,128)(2,1)}), bf16[16,2,8,3072]{3,2,1,0:T(8,128)(2,1)}, u32[]{:S(2)}, u32[]{:S(2)}) async-start(bf16[16,2,8,3072]{3,2,1,0:T(8,128)(2,1)} %broadcast_in_dim.30), calls=%async_computation | async-start | bytes 3145728 | tf_op jit(solution)/shard_map/all_to_all | solution.py:131
  21.6 4.4 %copy-start.20 = (s32[8,2]{0,1:T(2,128)S(1)}, s32[8,2]{0,1:T(2,128)}, u32[]{:S(2)}) copy-start(s32[8,2]{0,1:T(2,128)} %param.22) | copy-start | bytes 196
  21.6 112.9 %all-gather.6.cloned.1.call-start = ((), (), s32[]{:S(2)}) async-start(), calls=%async_computation.5 | async-start | bytes 6684672 | tf_op jit(solution)/shard_map/all_gather | solution.py:174
  26.0 8.1 %copy-start.19 = (f32[2,2,128]{2,1,0:T(2,128)S(1)}, f32[2,2,128]{2,1,0:T(2,128)}, u32[]{:S(2)}) copy-start(f32[2,2,128]{2,1,0:T(2,128)} %param.32) | copy-start | bytes 6148
  85.2 1.4 copy-start.16
  85.2 1.5 copy-start.17
  86.4 2.4 copy-start.14
  86.4 2.4 copy-start.13
  86.4 3.3 copy-start.21
  140.3 1.1 copy-start.5
  141.4 2.7 copy-start.15
  144.1 7.1 %copy-start.12 = (f32[8,3,3072]{2,0,1:T(8,128)S(1)}, f32[8,3,3072]{2,0,1:T(8,128)}, u32[]{:S(2)}) copy-start(f32[8,3,3072]{2,0,1:T(8,128)} %param.26) | copy-start | bytes 884740
  144.1 55.7 %all-to-all-start.1 = ((bf16[16,4,8,3072]{3,2,1,0:T(8,128)(2,1)}), bf16[16,4,8,3072]{3,2,1,0:T(8,128)(2,1)}, u32[]{:S(2)}, u32[]{:S(2)}) async-start(bf16[16,4,8,3072]{3,2,1,0:T(8,128)(2,1)} %bitcast.189), calls=%async_computation.1 | async-start | bytes 6291456 | tf_op jit(solution)/shard_map/all_to_all | solution.py:87
  151.1 51.2 %copy-start.4 = (f32[8,3072]{1,0:T(8,128)S(1)}, f32[8,3072]{1,0:T(8,128)}, u32[]{:S(2)}) copy-start(f32[8,3072]{1,0:T(8,128)} %get-tuple-element.36) | copy-start | bytes 294916
  151.1 112.4 %all-gather.8.cloned.1.call-start = ((), (), s32[]{:S(2)}) async-start(), calls=%async_computation.6 | async-start | bytes 3342336 | tf_op jit(solution)/shard_map/all_gather | solution.py:210
  199.8 3.0 copy-start.6
  199.8 3.0 copy-start.7
  202.3 6.2 %copy-start.1 = (f32[4,8,3072]{2,1,0:T(8,128)}, f32[4,8,3072]{2,1,0:T(8,128)S(1)}, u32[]{:S(2)}) copy-start(f32[4,8,3072]{2,1,0:T(8,128)S(1)} %convert_reduce_fusion.1) | copy-start | bytes 1179652
  208.6 62.7 %all-to-all-start.3 = ((bf16[16,2,8,3072]{3,2,1,0:T(8,128)(2,1)}), bf16[16,2,8,3072]{3,2,1,0:T(8,128)(2,1)}, u32[]{:S(2)}, u32[]{:S(2)}) async-start(bf16[16,2,8,3072]{3,2,1,0:T(8,128)(2,1)} %bitcast.190), calls=%async_computation.3 | async-start | bytes 3145728 | tf_op jit(solution)/shard_map/all_to_all | solution.py:87
  271.3 4.7 %copy-start.22 = (s32[8]{0:T(128)S(1)}, s32[8]{0:T(128)}, u32[]{:S(2)}) copy-start(s32[8]{0:T(128)} %param.21) | copy-start | bytes 100
  271.3 8.3 %copy-start.3 = (bf16[8,2,3072]{2,1,0:T(2,128)(2,1)S(1)}, bf16[8,2,3072]{2,1,0:T(2,128)(2,1)}, u32[]{:S(2)}) copy-start(bf16[8,2,3072]{2,1,0:T(2,128)(2,1)} %param.19) | copy-start | bytes 294916
  271.3 8.3 %copy-start.10 = (f32[8,3072]{1,0:T(8,128)S(1)}, f32[8,3072]{1,0:T(8,128)}, u32[]{:S(2)}) copy-start(f32[8,3072]{1,0:T(8,128)} %get-tuple-element.30) | copy-start | bytes 294916
  271.3 51.9 %all-to-all-start.2 = ((bf16[16,4,8,3072]{3,2,1,0:T(8,128)(2,1)}), bf16[16,4,8,3072]{3,2,1,0:T(8,128)(2,1)}, u32[]{:S(2)}, u32[]{:S(2)}) async-start(bf16[16,4,8,3072]{3,2,1,0:T(8,128)(2,1)} %bitcast.191), calls=%async_computation.2 | async-start | bytes 6291456 | tf_op jit(solution)/shard_map/all_to_all | solution.py:87
  279.6 47.9 %copy-start.18 = (f32[8,2,128]{2,1,0:T(2,128)S(1)}, f32[8,2,128]{2,1,0:T(2,128)}, u32[]{:S(2)}) copy-start(f32[8,2,128]{2,1,0:T(2,128)} %param.20) | copy-start | bytes 24580
  323.2 2.9 copy-start.8
  323.2 2.9 copy-start.9
  327.6 7.5 %collective-permute-start = (f32[8,1,128]{2,1,0:T(1,128)S(1)}, f32[8,1,128]{2,1,0:T(1,128)S(1)}, u32[]{:S(2)}, u32[]{:S(2)}) collective-permute-start(f32[8,1,128]{2,1,0:T(1,128)S(1)} %get-tuple-element.51), channel_id=1, source_target_pairs={{0,16},{16,32},{32,48},{48,64},{64,80},{80,96},{96,112},{112,128},... | collective-permute-start | bytes 12296 | tf_op jit(solution)/shard_map/ppermute | solution.py:24
  329.5 5.6 %collective-permute-start.1 = (f32[8,1,128]{2,1,0:T(1,128)S(1)}, f32[8,1,128]{2,1,0:T(1,128)S(1)}, u32[]{:S(2)}, u32[]{:S(2)}) collective-permute-start(f32[8,1,128]{2,1,0:T(1,128)S(1)} %get-tuple-element.52), channel_id=1, source_target_pairs={{16,0},{32,16},{48,32},{64,48},{80,64},{96,80},{112,96},{128,112},... | collective-permute-start | bytes 12296 | tf_op jit(solution)/shard_map/ppermute | solution.py:25
Sparse Core Ops, SparseCore 0:
  11.3 65.5 all-gather.3
  89.8 44.6 all-gather.5
  203.7 59.7 all-gather.7

commit v5 on v4

--- a/solution.py
+++ b/solution.py
@@ -125,13 +125,25 @@
     image_count = owners * own_image
     text_tile = owners * own_text
     block_len = text_tile + image_count
-    image_mod = lax.all_gather(image_mod_own, "tensor", axis=0, tiled=True).reshape(
+    half = requests // 2
+    image_sc = lax.all_gather(image_mod_own[:, :half], "tensor", axis=0, tiled=True)
+    rest = jnp.concatenate(
+        [
+            image_mod_own[:, half:].reshape(-1, model_width),
+            text_mod_own.reshape(-1, model_width),
+        ],
+        0,
+    )
+    rest = lax.all_to_all(
+        jnp.broadcast_to(rest[None], (owners,) + rest.shape), "tensor", 0, 0, tiled=True
+    )
+    image_dma = rest[:, : own_image * (requests - half)].reshape(
+        image_count, requests - half, model_width
+    )
+    image_mod = jnp.concatenate([image_sc, image_dma], 1).reshape(
         image_count * requests, model_width
     )
-    text_mod = lax.all_to_all(
-        jnp.broadcast_to(text_mod_own[None], (owners,) + text_mod_own.shape), "tensor", 0, 0,
-        tiled=True,
-    ).reshape(text_tile * requests, model_width)
+    text_mod = rest[:, own_image * (requests - half) :].reshape(text_tile * requests, model_width)
     tile_index = lax.axis_index("tile")
     token_index = jnp.arange(image_count, dtype=jnp.int32)
     owner = token_index // own_image
@@ -207,7 +219,19 @@
         jnp.bfloat16
     )
     mlp_mod = modulate(image_mid, mod_mlp[None, :, 0, :], mod_mlp[None, :, 1, :])
-    piece = lax.all_gather(mlp_mod, "tensor", axis=0, tiled=True)
+    piece = jnp.concatenate(
+        [
+            lax.all_gather(mlp_mod[:, :half], "tensor", axis=0, tiled=True),
+            lax.all_to_all(
+                jnp.broadcast_to(mlp_mod[None, :, half:], (owners,) + mlp_mod[:, half:].shape),
+                "tensor",
+                0,
+                0,
+                tiled=True,
+            ).reshape(image_count, requests - half, model_width),
+        ],
+        1,
+    )
     grown = jnp.dot(piece.reshape(-1, model_width), mlp_expand, preferred_element_type=jnp.float32)
     activated = jax.nn.gelu(grown, approximate=True).astype(jnp.bfloat16)
     text_out = (text_own.astype(jnp.float32) + mod_text[None, :, 2, :] * text_sum).astype(

time: 346 us -> 369 us (1.066)
  local copies, waits for them, and re-layouts: 24 us -> 37.2 us
  waiting for transfers between devices: 223 us -> 234 us
  starting transfers between devices: 28.9 us -> 33.6 us
  other arithmetic: 26.9 us -> 22.6 us
    all_to_all x1 -> x2, waiting for transfers between devices: 14.9 us -> 54.5 us  [the longest x1 34.6 us: per_device(): lax.all_to_all(jnp.broadcast_to(rest[None], (owners,) + rest.shape), 'ten...]
    all_gather x2, waiting for transfers between devices: 73.7 us -> 43.3 us  [the longest x1 28.7 us: per_device(): lax.all_gather(mlp_mod[:, :half], 'tensor', axis=0, tiled=True)]
    slice x0 -> x3, local copies, waits for them, and re-layouts: none -> 5.34 us  [the longest x1 3.89 us: per_device(): rest[:, own_image * (requests - half):]]
    all_to_all x1 -> x2, starting transfers between devices: 7.08 us -> 11.5 us  [the longest x1 7.08 us: per_device(): lax.all_to_all(jnp.broadcast_to(rest[None], (owners,) + rest.shape), 'ten...]
    reshape x0 -> x2, local copies, waits for them, and re-layouts: none -> 3.89 us  [the longest x1 3.86 us: per_device(): rest[:, :own_image * (requests - half)]]
    unnamed x50 -> x66, local copies, waits for them, and re-layouts: 10.3 us -> 11 us
  transfers between devices with their start and end apart: 9 -> 10, of which waited for: 6 -> 7; matrix products, arithmetic and copies ran while one was open for 12% -> 12% of each run, Pallas kernels for 0% -> 0%
where the time goes in v5:
time: 369 us; the launch traced here: 365 us
  waiting for transfers between devices  234 us (63%)
  local copies, waits for them, and re-layouts  37.2 us (10%)
  starting transfers between devices  33.6 us (9%)
  other arithmetic  22.6 us (6%)
  matrix products  22.3 us (6%)
  between operations  15 us (4%)
    all_to_all x3, waiting for transfers between devices, sum_over_tensor(): parts = lax.all_to_all(parts, 'tensor', 0, 0, tiled=True)  90.5 us
    all_gather x1, waiting for transfers between devices, per_device(): lax.all_gather(jnp.stack([keys, values], 1), 'tile', axis=0, tiled=True)  45.1 us
    all_to_all x1, waiting for transfers between devices, per_device(): lax.all_to_all(jnp.broadcast_to(rest[None], (owners,) + rest.shape), 'ten...  34.6 us
    all_gather x1, waiting for transfers between devices, per_device(): lax.all_gather(mlp_mod[:, :half], 'tensor', axis=0, tiled=True)  28.7 us
    all_to_all x1, waiting for transfers between devices, per_device(): lax.all_to_all(jnp.broadcast_to(mlp_mod[None, :, half:], (owners,) + mlp_...  20 us
    all_to_all x3, starting transfers between devices, sum_over_tensor(): parts = lax.all_to_all(parts, 'tensor', 0, 0, tiled=True)  16.3 us
    all_gather x1, waiting for transfers between devices, per_device(): lax.all_gather(image_mod_own[:, :half], 'tensor', axis=0, tiled=True)  14.6 us
    unnamed x66, local copies, waits for them, and re-layouts  11 us
  transfers between devices with their start and end apart: 10, of which 7 were waited for; matrix products, arithmetic and copies ran while one was open for 12% of the time, Pallas kernels for 0%

profile of v5, /device:TPU:32, one launch (start us, length us, event | category | flops | bytes accessed | tf_op | source)
XLA Modules:
  0.0 365.0 jit_solution(17032802552939871688)
XLA Ops:
  7.2 1.1 copy.85
  8.7 1.7 slice_bitcast_fusion.12
  10.5 0.7 fusion.129
  11.2 0.7 slice_bitcast_fusion.7
  12.4 2.1 broadcast_in_dim.32
  14.4 7.1 %all-to-all-start = ((bf16[16,32,3072]{2,1,0:T(8,128)(2,1)}), bf16[16,32,3072]{2,1,0:T(8,128)(2,1)}, u32[]{:S(2)}, u32[]{:S(2)}) async-start(bf16[16,32,3072]{2,1,0:T(8,128)(2,1)} %broadcast_in_dim.32), calls=%async_computation | async-start | bytes 6291456 | tf_op jit(solution)/shard_map/all_to_all | solution.py:137
  21.6 0.7 all-gather.4.cloned.1.call-update
  22.3 4.3 %copy.88 = bf16[3072,3,128]{0,2,1:T(8,128)(2,1)} copy(bf16[3072,3,128]{2,0,1:T(8,128)(2,1)} %param.28) | data formatting | bytes 4718592 | tf_op args[10]
  26.7 0.7 copy.92
  27.4 0.7 copy.93
  28.1 4.3 %copy.87 = bf16[3072,3,128]{0,2,1:T(8,128)(2,1)} copy(bf16[3072,3,128]{2,0,1:T(8,128)(2,1)} %param.29) | data formatting | bytes 4718592 | tf_op args[11]
  32.4 0.5 and_select_fusion.2
  33.0 0.5 compare_and_fusion
  33.5 0.6 compare_select_fusion
  34.1 0.6 iota_and_fusion
  34.7 0.5 slice_bitcast_fusion.18
  35.2 34.6 %all-to-all-done = bf16[16,32,3072]{2,1,0:T(8,128)(2,1)} async-done(((bf16[16,32,3072]{2,1,0:T(8,128)(2,1)}), bf16[16,32,3072]{2,1,0:T(8,128)(2,1)}, u32[]{:S(2)}, u32[]{:S(2)}) %all-to-all-start) | async-done | bytes 3145760 | tf_op jit(solution)/shard_map/all_to_all | solution.py:137
  69.8 3.9 %fusion.122 = (bf16[16,16,3072]{2,1,0:T(8,128)(2,1)}, bf16[16,16,3072]{2,1,0:T(8,128)(2,1)}) fusion(bf16[16,32,3072]{2,1,0:T(8,128)(2,1)} %all-to-all-done), kind=kLoop, calls=%fused_computation.211 | loop fusion | bytes 6291456 | tf_op jit(solution)/shard_map/slice | solution.py:146
  73.7 3.9 %reshape.833 = bf16[64,4,3072]{2,1,0:T(4,128)(2,1)} reshape(bf16[16,16,3072]{2,1,0:T(8,128)(2,1)} %get-tuple-element.27) | data formatting | bytes 3145728 | tf_op jit(solution)/shard_map/reshape | solution.py:140
  77.6 14.6 %all-gather.4.cloned.1.call-done = bf16[64,4,3072]{2,1,0:T(4,128)(2,1)} async-done(((bf16[4,4,3072]{2,1,0:T(4,128)(2,1)}), bf16[64,4,3072]{2,1,0:T(4,128)(2,1)}) %all-gather.4.cloned.1.call-update) | async-done | bytes 1572880 | tf_op jit(solution)/shard_map/all_gather | solution.py:129
  92.2 4.4 %fusion.23 = f32[64,8,3,1,128]{4,1,2,0,3:T(8,128)S(1)} fusion(bf16[3072,3,128]{0,2,1:T(8,128)(2,1)} %copy.88, bf16[64,4,3072]{2,1,0:T(4,128)(2,1)} %reshape.833, bf16[64,4,3072]{2,1,0:T(4,128)(2,1)} %all-gather.4.cloned.1.call-done), kind=kOutput, calls=%fused_computation.33 | convolution fusion | flops 1214251008 | bytes 6291456 | tf_op jit(solution)/shard_map/dot_general | solution.py:160
  96.6 0.8 multiply_reduce_fusion.2
  97.4 0.8 copy.90
  98.3 0.7 copy.91
  99.0 0.8 copy.95
  99.8 0.7 copy.96
  100.5 1.1 multiply_multiply_fusion.2
  102.2 0.5 copy-done.3
  102.7 1.0 fusion.26
  104.2 1.4 fusion.76
  105.6 0.8 maximum_maximum_fusion
  106.5 45.1 %all-gather.6.cloned.1.call-done = bf16[1536,2,8,1,128]{4,2,0,3,1:T(8,128)(2,1)} async-done(((bf16[96,2,8,1,128]{4,2,0,3,1:T(8,128)(2,1)}), bf16[1536,2,8,1,128]{4,2,0,3,1:T(8,128)(2,1)}) %all-gather.6.cloned.1.call-update) | async-done | bytes 6291472 | tf_op jit(solution)/shard_map/all_gather | solution.py:186
  151.6 3.1 slice_bitcast_fusion.1
  154.7 1.2 fusion.14
  155.9 1.6 fusion.131
  157.5 1.1 fusion.39
  158.7 2.6 convolution_convert_fusion.1
  161.3 7.0 %all-to-all-start.1 = ((bf16[16,4,8,3072]{3,2,1,0:T(8,128)(2,1)}), bf16[16,4,8,3072]{3,2,1,0:T(8,128)(2,1)}, u32[]{:S(2)}, u32[]{:S(2)}) async-start(bf16[16,4,8,3072]{3,2,1,0:T(8,128)(2,1)} %bitcast.194), calls=%async_computation.1 | async-start | bytes 6291456 | tf_op jit(solution)/shard_map/all_to_all | solution.py:87
  168.5 0.7 slice_bitcast_fusion.9
  169.3 47.7 %all-to-all-done.1 = bf16[16,4,8,3072]{3,2,1,0:T(8,128)(2,1)} async-done(((bf16[16,4,8,3072]{3,2,1,0:T(8,128)(2,1)}), bf16[16,4,8,3072]{3,2,1,0:T(8,128)(2,1)}, u32[]{:S(2)}, u32[]{:S(2)}) %all-to-all-start.1) | async-done | bytes 3145760 | tf_op jit(solution)/shard_map/all_to_all | solution.py:87
  217.0 2.5 convert_reduce_fusion.1
  220.1 0.7 fusion.128
  220.8 2.7 broadcast_in_dim.42
  223.5 4.4 %all-to-all-start.2 = ((bf16[16,4,4,3072]{3,2,1,0:T(4,128)(2,1)}), bf16[16,4,4,3072]{3,2,1,0:T(4,128)(2,1)}, u32[]{:S(2)}, u32[]{:S(2)}) async-start(bf16[16,4,4,3072]{3,2,1,0:T(4,128)(2,1)} %broadcast_in_dim.42), calls=%async_computation.2 | async-start | bytes 3145728 | tf_op jit(solution)/shard_map/all_to_all | solution.py:225
  227.9 0.8 slice_bitcast_fusion.13
  228.8 0.5 slice.208
  230.0 3.0 fusion.5
  232.9 20.0 %all-to-all-done.2 = bf16[16,4,4,3072]{3,2,1,0:T(4,128)(2,1)} async-done(((bf16[16,4,4,3072]{3,2,1,0:T(4,128)(2,1)}), bf16[16,4,4,3072]{3,2,1,0:T(4,128)(2,1)}, u32[]{:S(2)}, u32[]{:S(2)}) %all-to-all-start.2) | async-done | bytes 1572896 | tf_op jit(solution)/shard_map/all_to_all | solution.py:225
  252.9 4.4 %all-to-all-start.4 = ((bf16[16,2,8,3072]{3,2,1,0:T(8,128)(2,1)}), bf16[16,2,8,3072]{3,2,1,0:T(8,128)(2,1)}, u32[]{:S(2)}, u32[]{:S(2)}) async-start(bf16[16,2,8,3072]{3,2,1,0:T(8,128)(2,1)} %bitcast.195), calls=%async_computation.4 | async-start | bytes 3145728 | tf_op jit(solution)/shard_map/all_to_all | solution.py:87
  257.3 28.7 %all-gather.8.cloned.1.call-done = bf16[64,4,3072]{2,1,0:T(4,128)(2,1)} async-done(((bf16[4,4,3072]{2,1,0:T(4,128)(2,1)}), bf16[64,4,3072]{2,1,0:T(4,128)(2,1)}) %all-gather.8.cloned.1.call-update) | async-done | bytes 1572880 | tf_op jit(solution)/shard_map/all_gather | solution.py:224
  286.0 7.8 %convolution_convert_fusion = bf16[512,3072]{1,0:T(8,128)(2,1)} fusion(bf16[384,3072]{1,0:T(8,128)(2,1)S(1)} %copy-done, bf16[3072,384]{1,0:T(8,128)(2,1)} %param.33, bf16[64,4,3072]{2,1,0:T(4,128)(2,1)} %bitcast.50, bf16[64,4,3072]{2,1,0:T(4,128)(2,1)} %all-gather.8.cloned.1.call-done), kind=kOutput, calls=%fused_computation.6 | convolution fusion | flops 2425552896 | bytes 11010048 | tf_op jit(solution)/shard_map/dot_general | solution.py:240
  293.8 4.9 %all-to-all-start.3 = ((bf16[16,4,8,3072]{3,2,1,0:T(8,128)(2,1)}), bf16[16,4,8,3072]{3,2,1,0:T(8,128)(2,1)}, u32[]{:S(2)}, u32[]{:S(2)}) async-start(bf16[16,4,8,3072]{3,2,1,0:T(8,128)(2,1)} %bitcast.196), calls=%async_computation.3 | async-start | bytes 6291456 | tf_op jit(solution)/shard_map/all_to_all | solution.py:87
  298.7 1.2 fusion.127
  299.9 0.7 copy_bitcast_fusion
  300.6 1.6 convert_reduce_fusion.2
  302.3 0.7 copy.106
  303.1 42.8 %all-to-all-done.3 = bf16[16,4,8,3072]{3,2,1,0:T(8,128)(2,1)} async-done(((bf16[16,4,8,3072]{3,2,1,0:T(8,128)(2,1)}), bf16[16,4,8,3072]{3,2,1,0:T(8,128)(2,1)}, u32[]{:S(2)}, u32[]{:S(2)}) %all-to-all-start.3) | async-done | bytes 3145760 | tf_op jit(solution)/shard_map/all_to_all | solution.py:87
  345.9 2.5 convert_reduce_fusion
  348.8 1.3 convolution_bitcast_fusion
  350.3 1.9 collective-permute-start
  352.3 3.6 collective-permute-start.1
  355.9 1.1 fusion.68
  357.0 0.9 copy.105
  357.9 0.6 pad_maximum_fusion.1
  (116 shorter events, 3.7 us)
Async XLA Ops:
  7.2 278.8 %copy-start = (bf16[384,3072]{1,0:T(8,128)(2,1)S(1)}, bf16[384,3072]{1,0:T(8,128)(2,1)}, u32[]{:S(2)}) copy-start(bf16[384,3072]{1,0:T(8,128)(2,1)} %param.34) | copy-start | bytes 7077892
  7.2 4.0 %copy-start.13 = (f32[8,3,3072]{2,0,1:T(8,128)S(1)}, f32[8,3,3072]{2,0,1:T(8,128)}, u32[]{:S(2)}) copy-start(f32[8,3,3072]{2,0,1:T(8,128)} %param.25) | copy-start | bytes 884740
  7.2 4.7 %copy-start.4 = (bf16[8,2,3072]{2,1,0:T(2,128)(2,1)S(1)}, bf16[8,2,3072]{2,1,0:T(2,128)(2,1)}, u32[]{:S(2)}) copy-start(bf16[8,2,3072]{2,1,0:T(2,128)(2,1)} %param.19) | copy-start | bytes 294916
  14.4 55.4 %all-to-all-start = ((bf16[16,32,3072]{2,1,0:T(8,128)(2,1)}), bf16[16,32,3072]{2,1,0:T(8,128)(2,1)}, u32[]{:S(2)}, u32[]{:S(2)}) async-start(bf16[16,32,3072]{2,1,0:T(8,128)(2,1)} %broadcast_in_dim.32), calls=%async_computation | async-start | bytes 6291456 | tf_op jit(solution)/shard_map/all_to_all | solution.py:137
  21.5 5.1 %copy-start.22 = (s32[8,2]{0,1:T(2,128)S(1)}, s32[8,2]{0,1:T(2,128)}, u32[]{:S(2)}) copy-start(s32[8,2]{0,1:T(2,128)} %param.22) | copy-start | bytes 196
  21.5 70.7 %all-gather.4.cloned.1.call-start = ((), (), s32[]{:S(2)}) async-start(), calls=%async_computation.5 | async-start | bytes 1671168 | tf_op jit(solution)/shard_map/all_gather | solution.py:129
  22.2 129.4 %all-gather.6.cloned.1.call-start = ((), (), s32[]{:S(2)}) async-start(), calls=%async_computation.6 | async-start | bytes 6684672 | tf_op jit(solution)/shard_map/all_gather | solution.py:186
  26.6 8.1 %copy-start.21 = (f32[2,2,128]{2,1,0:T(2,128)S(1)}, f32[2,2,128]{2,1,0:T(2,128)}, u32[]{:S(2)}) copy-start(f32[2,2,128]{2,1,0:T(2,128)} %param.32) | copy-start | bytes 6148
  100.5 1.7 copy-start.2
  100.5 2.1 copy-start.3
  102.7 1.3 copy-start.19
  102.7 1.3 copy-start.20
  102.7 1.4 copy-start.16
  102.7 1.4 copy-start.17
  102.7 1.4 copy-start.23
  102.7 1.4 copy-start.24
  102.7 1.4 copy-start.25
  102.7 1.4 copy-start.26
  102.7 1.4 copy-start.27
  102.7 1.4 copy-start.28
  103.7 2.7 copy-start.29
  157.5 1.1 copy-start.7
  158.6 2.7 copy-start.15
  161.3 7.2 %copy-start.14 = (f32[8,3,3072]{2,0,1:T(8,128)S(1)}, f32[8,3,3072]{2,0,1:T(8,128)}, u32[]{:S(2)}) copy-start(f32[8,3,3072]{2,0,1:T(8,128)} %param.26) | copy-start | bytes 884740
  161.3 55.7 %all-to-all-start.1 = ((bf16[16,4,8,3072]{3,2,1,0:T(8,128)(2,1)}), bf16[16,4,8,3072]{3,2,1,0:T(8,128)(2,1)}, u32[]{:S(2)}, u32[]{:S(2)}) async-start(bf16[16,4,8,3072]{3,2,1,0:T(8,128)(2,1)} %bitcast.194), calls=%async_computation.1 | async-start | bytes 6291456 | tf_op jit(solution)/shard_map/all_to_all | solution.py:87
  168.3 51.2 %copy-start.6 = (f32[8,3072]{1,0:T(8,128)S(1)}, f32[8,3072]{1,0:T(8,128)}, u32[]{:S(2)}) copy-start(f32[8,3072]{1,0:T(8,128)} %get-tuple-element.38) | copy-start | bytes 294916
  168.3 117.7 %all-gather.8.cloned.1.call-start = ((), (), s32[]{:S(2)}) async-start(), calls=%async_computation.7 | async-start | bytes 1671168 | tf_op jit(solution)/shard_map/all_gather | solution.py:224
  217.0 3.0 copy-start.8
  217.0 3.0 copy-start.9
  219.5 9.3 %copy-start.1 = (f32[4,8,3072]{2,1,0:T(8,128)}, f32[4,8,3072]{2,1,0:T(8,128)S(1)}, u32[]{:S(2)}) copy-start(f32[4,8,3072]{2,1,0:T(8,128)S(1)} %convert_reduce_fusion.1) | copy-start | bytes 1179652
  223.5 29.4 %all-to-all-start.2 = ((bf16[16,4,4,3072]{3,2,1,0:T(4,128)(2,1)}), bf16[16,4,4,3072]{3,2,1,0:T(4,128)(2,1)}, u32[]{:S(2)}, u32[]{:S(2)}) async-start(bf16[16,4,4,3072]{3,2,1,0:T(4,128)(2,1)} %broadcast_in_dim.42), calls=%async_computation.2 | async-start | bytes 3145728 | tf_op jit(solution)/shard_map/all_to_all | solution.py:225
  252.9 40.9 %all-to-all-start.4 = ((bf16[16,2,8,3072]{3,2,1,0:T(8,128)(2,1)}), bf16[16,2,8,3072]{3,2,1,0:T(8,128)(2,1)}, u32[]{:S(2)}, u32[]{:S(2)}) async-start(bf16[16,2,8,3072]{3,2,1,0:T(8,128)(2,1)} %bitcast.195), calls=%async_computation.4 | async-start | bytes 3145728 | tf_op jit(solution)/shard_map/all_to_all | solution.py:87
  293.8 4.9 %copy-start.30 = (s32[8]{0:T(128)S(1)}, s32[8]{0:T(128)}, u32[]{:S(2)}) copy-start(s32[8]{0:T(128)} %param.21) | copy-start | bytes 100
  293.8 8.5 %copy-start.5 = (bf16[8,2,3072]{2,1,0:T(2,128)(2,1)S(1)}, bf16[8,2,3072]{2,1,0:T(2,128)(2,1)}, u32[]{:S(2)}) copy-start(bf16[8,2,3072]{2,1,0:T(2,128)(2,1)} %param.19) | copy-start | bytes 294916
  293.8 8.5 %copy-start.12 = (f32[8,3072]{1,0:T(8,128)S(1)}, f32[8,3072]{1,0:T(8,128)}, u32[]{:S(2)}) copy-start(f32[8,3072]{1,0:T(8,128)} %get-tuple-element.32) | copy-start | bytes 294916
  293.8 52.1 %all-to-all-start.3 = ((bf16[16,4,8,3072]{3,2,1,0:T(8,128)(2,1)}), bf16[16,4,8,3072]{3,2,1,0:T(8,128)(2,1)}, u32[]{:S(2)}, u32[]{:S(2)}) async-start(bf16[16,4,8,3072]{3,2,1,0:T(8,128)(2,1)} %bitcast.196), calls=%async_computation.3 | async-start | bytes 6291456 | tf_op jit(solution)/shard_map/all_to_all | solution.py:87
  302.3 48.0 %copy-start.18 = (f32[8,2,128]{2,1,0:T(2,128)S(1)}, f32[8,2,128]{2,1,0:T(2,128)}, u32[]{:S(2)}) copy-start(f32[8,2,128]{2,1,0:T(2,128)} %param.20) | copy-start | bytes 24580
  345.9 2.9 copy-start.10
  345.9 2.9 copy-start.11
  350.3 7.5 %collective-permute-start = (f32[8,1,128]{2,1,0:T(1,128)S(1)}, f32[8,1,128]{2,1,0:T(1,128)S(1)}, u32[]{:S(2)}, u32[]{:S(2)}) collective-permute-start(f32[8,1,128]{2,1,0:T(1,128)S(1)} %get-tuple-element.57), channel_id=1, source_target_pairs={{0,16},{16,32},{32,48},{48,64},{64,80},{80,96},{96,112},{112,128},... | collective-permute-start | bytes 12296 | tf_op jit(solution)/shard_map/ppermute | solution.py:24
  352.3 5.6 %collective-permute-start.1 = (f32[8,1,128]{2,1,0:T(1,128)S(1)}, f32[8,1,128]{2,1,0:T(1,128)S(1)}, u32[]{:S(2)}, u32[]{:S(2)}) collective-permute-start(f32[8,1,128]{2,1,0:T(1,128)S(1)} %get-tuple-element.58), channel_id=1, source_target_pairs={{16,0},{32,16},{48,32},{64,48},{80,64},{96,80},{112,96},{128,112},... | collective-permute-start | bytes 12296 | tf_op jit(solution)/shard_map/ppermute | solution.py:25
Sparse Core Ops, SparseCore 0:
  25.3 66.7 all-gather.3
  106.5 45.0 all-gather.5
  221.0 64.9 all-gather.7

commit v6 on v4

--- a/solution.py
+++ b/solution.py
@@ -171,27 +171,43 @@
     )
     values = jnp.concatenate([text_qkv[:, :, 2], image_qkv[:, :, 2]], 0).astype(jnp.bfloat16)
     score_scale = 1.0 / math.sqrt(HEAD_DIM)
-    kv_all = lax.all_gather(jnp.stack([keys, values], 1), "tile", axis=0, tiled=True)
-    keys_all, values_all = kv_all[:, 0], kv_all[:, 1]
-    usable = key_usable(text_len, keys_all.shape[0], text_tile, block_len)[:, None, None, :]
+    tiles = lax.axis_size("tile")
+    parts = tiles // requests
+    part_len = block_len // parts
+    keys_r = jnp.repeat(keys.transpose(1, 0, 2, 3), parts, axis=0)
+    values_r = jnp.repeat(values.transpose(1, 0, 2, 3), parts, axis=0)
+    query_r = query.transpose(1, 0, 2, 3).reshape(tiles, part_len, local_heads, HEAD_DIM)
+    outgoing = jnp.concatenate([keys_r, values_r, query_r], 1)
+    incoming = lax.all_to_all(outgoing, "tile", 0, 0, tiled=True)
+    keys_all = incoming[:, :block_len].reshape(tiles * block_len, local_heads, HEAD_DIM)
+    values_all = incoming[:, block_len : 2 * block_len].reshape(
+        tiles * block_len, local_heads, HEAD_DIM
+    )
+    query_mine = incoming[:, 2 * block_len :].reshape(tiles * part_len, local_heads, HEAD_DIM)
+    my_request = tile_index // parts
+    usable = key_usable(text_len[my_request][None], keys_all.shape[0], text_tile, block_len)[
+        0
+    ][None, None, :]
     scores = (
-        jnp.einsum("qrhd,krhd->rhqk", query, keys_all, preferred_element_type=jnp.float32)
+        jnp.einsum("qhd,khd->hqk", query_mine, keys_all, preferred_element_type=jnp.float32)
         * score_scale
     )
     row_top = jnp.max(jnp.where(usable, scores, -jnp.inf), -1, keepdims=True)
     weights_raw = jnp.where(usable, jnp.exp(scores - row_top), 0.0)
     weight_sum = jnp.sum(weights_raw, -1, keepdims=True)
     accum = jnp.einsum(
-        "rhqk,krhd->rhqd",
+        "hqk,khd->hqd",
         weights_raw.astype(jnp.bfloat16),
         values_all,
         preferred_element_type=jnp.float32,
     )
-    attended = (
-        (accum / weight_sum).astype(jnp.bfloat16).transpose(2, 0, 1, 3).reshape(
-            block_len, requests, local_cols
+    attended_mine = (
+        (accum / weight_sum).astype(jnp.bfloat16).transpose(1, 0, 2).reshape(
+            tiles, part_len, local_heads * HEAD_DIM
         )
     )
+    returned = lax.all_to_all(attended_mine, "tile", 0, 0, tiled=True)
+    attended = returned.reshape(requests, block_len, local_cols).transpose(1, 0, 2)
     text_att = attended[:text_tile].reshape(text_tile * requests, local_cols)
     image_att = attended[text_tile:].reshape(image_count * requests, local_cols)
     image_term = jnp.dot(image_att, proj_image, preferred_element_type=jnp.float32).reshape(

time: 346 us -> 345 us (level)
  waiting for transfers between devices: 223 us -> 202 us
  blocking collectives: 0 us -> 15 us
  starting transfers between devices: 28.9 us -> 34.2 us
    all_gather x1 -> x0, waiting for transfers between devices: 43.8 us -> none  [per_device(): lax.all_gather(jnp.stack([keys, values], 1), 'tile', axis=0, tiled=True)]
    all_to_all x0 -> x1, waiting for transfers between devices: none -> 22.2 us  [per_device(): incoming = lax.all_to_all(outgoing, 'tile', 0, 0, tiled=True)]
    all_to_all x0 -> x1, blocking collectives: none -> 15 us  [per_device(): returned = lax.all_to_all(attended_mine, 'tile', 0, 0, tiled=True)]
    all_to_all x0 -> x1, starting transfers between devices: none -> 7.5 us  [per_device(): incoming = lax.all_to_all(outgoing, 'tile', 0, 0, tiled=True)]
    unnamed x50 -> x52, local copies, waits for them, and re-layouts: 10.3 us -> 11 us
where the time goes in v6:
time: 345 us; the launch traced here: 341 us
  waiting for transfers between devices  202 us (59%)
  starting transfers between devices  34.2 us (10%)
  other arithmetic  26.4 us (8%)
  matrix products  24.1 us (7%)
  local copies, waits for them, and re-layouts  23.6 us (7%)
  between operations  15.2 us (4%)
  blocking collectives  15 us (4%)
    all_to_all x3, waiting for transfers between devices, sum_over_tensor(): parts = lax.all_to_all(parts, 'tensor', 0, 0, tiled=True)  91.5 us
    all_gather x1, waiting for transfers between devices, per_device(): piece = lax.all_gather(mlp_mod, 'tensor', axis=0, tiled=True)  50.4 us
    all_gather x1, waiting for transfers between devices, per_device(): lax.all_gather(image_mod_own, 'tensor', axis=0, tiled=True)  23.3 us
    all_to_all x1, waiting for transfers between devices, per_device(): incoming = lax.all_to_all(outgoing, 'tile', 0, 0, tiled=True)  22.2 us
    all_to_all x1, blocking collectives, per_device(): returned = lax.all_to_all(attended_mine, 'tile', 0, 0, tiled=True)  15 us
    all_to_all x1, waiting for transfers between devices, per_device(): lax.all_to_all(jnp.broadcast_to(text_mod_own[None], (owners,) + text_mod_...  14.9 us
    all_to_all x3, starting transfers between devices, sum_over_tensor(): parts = lax.all_to_all(parts, 'tensor', 0, 0, tiled=True)  13.8 us
    unnamed x52, local copies, waits for them, and re-layouts  11 us
  transfers between devices with their start and end apart: 9, of which 6 were waited for; matrix products, arithmetic and copies ran while one was open for 12% of the time, Pallas kernels for 0%

profile of v6, /device:TPU:32, one launch (start us, length us, event | category | flops | bytes accessed | tf_op | source)
XLA Modules:
  0.0 340.8 jit_solution(9372551018860808209)
XLA Ops:
  7.2 1.1 copy.77
  8.7 1.7 slice_bitcast_fusion.9
  10.4 0.8 add_convert_fusion.1
  11.2 1.0 fusion.71
  12.4 0.6 slice_bitcast_fusion.4
  13.2 1.3 broadcast_in_dim.42
  14.5 7.1 %all-to-all-start = ((bf16[16,2,8,3072]{3,2,1,0:T(8,128)(2,1)}), bf16[16,2,8,3072]{3,2,1,0:T(8,128)(2,1)}, u32[]{:S(2)}, u32[]{:S(2)}) async-start(bf16[16,2,8,3072]{3,2,1,0:T(8,128)(2,1)} %broadcast_in_dim.42), calls=%async_computation | async-start | bytes 3145728 | tf_op jit(solution)/shard_map/all_to_all | solution.py:131
  21.6 4.3 %copy.80 = bf16[3072,3,128]{0,2,1:T(8,128)(2,1)} copy(bf16[3072,3,128]{2,0,1:T(8,128)(2,1)} %param.28) | data formatting | bytes 4718592 | tf_op args[10]
  26.0 0.7 copy.84
  26.7 0.7 copy.85
  27.4 4.3 %copy.79 = bf16[3072,3,128]{0,2,1:T(8,128)(2,1)} copy(bf16[3072,3,128]{2,0,1:T(8,128)(2,1)} %param.29) | data formatting | bytes 4718592 | tf_op args[11]
  31.7 0.6 and_select_fusion.2
  32.2 0.6 compare_and_fusion
  32.8 0.6 compare_select_fusion
  33.4 0.6 iota_and_fusion
  34.0 14.9 %all-to-all-done = bf16[16,2,8,3072]{3,2,1,0:T(8,128)(2,1)} async-done(((bf16[16,2,8,3072]{3,2,1,0:T(8,128)(2,1)}), bf16[16,2,8,3072]{3,2,1,0:T(8,128)(2,1)}, u32[]{:S(2)}, u32[]{:S(2)}) %all-to-all-start) | async-done | bytes 1572896 | tf_op jit(solution)/shard_map/all_to_all | solution.py:131
  48.9 3.1 fusion.18
  52.3 0.6 fusion.90
  52.9 0.8 multiply_convert_fusion.1
  53.7 23.3 %all-gather.3.cloned.1.call-done = bf16[64,8,3072]{2,1,0:T(8,128)(2,1)} async-done(((bf16[4,8,3072]{2,1,0:T(8,128)(2,1)}), bf16[64,8,3072]{2,1,0:T(8,128)(2,1)}) %all-gather.3.cloned.1.call-update) | async-done | bytes 3145744 | tf_op jit(solution)/shard_map/all_gather | solution.py:128
  76.9 4.4 %fusion.13 = f32[64,8,3,1,128]{4,1,2,0,3:T(8,128)S(1)} fusion(bf16[3072,3,128]{0,2,1:T(8,128)(2,1)} %copy.80, bf16[64,8,3072]{2,1,0:T(8,128)(2,1)} %all-gather.3.cloned.1.call-done), kind=kOutput, calls=%fused_computation.20 | convolution fusion | flops 1207959552 | bytes 6291456 | tf_op jit(solution)/shard_map/dot_general | solution.py:148
  81.3 0.8 multiply_reduce_fusion.2
  82.2 0.8 copy.82
  83.0 0.7 copy.83
  83.7 0.8 copy.88
  84.5 0.7 copy.89
  85.2 1.0 multiply_multiply_fusion.2
  86.7 2.1 fusion.65
  89.1 1.1 pad_maximum_fusion
  90.2 7.5 %all-to-all-start.1 = ((bf16[16,240,1,128]{3,1,2,0:T(8,128)(2,1)}), bf16[16,240,1,128]{3,1,2,0:T(8,128)(2,1)}, u32[]{:S(2)}, u32[]{:S(2)}) async-start(bf16[16,240,1,128]{3,1,2,0:T(8,128)(2,1)} %pad_maximum_fusion), calls=%async_computation.1 | async-start | bytes 1966080 | tf_op jit(solution)/shard_map/all_to_all | solution.py:181
  97.7 0.6 dynamic_slice.3
  98.3 0.7 fusion.100
  99.0 22.2 %all-to-all-done.1 = bf16[16,240,1,128]{3,1,2,0:T(8,128)(2,1)} async-done(((bf16[16,240,1,128]{3,1,2,0:T(8,128)(2,1)}), bf16[16,240,1,128]{3,1,2,0:T(8,128)(2,1)}, u32[]{:S(2)}, u32[]{:S(2)}) %all-to-all-start.1) | async-done | bytes 983072 | tf_op jit(solution)/shard_map/all_to_all | solution.py:181
  121.2 1.2 fusion.110
  122.3 0.9 slice.176
  123.3 0.9 select_reduce_fusion
  124.2 1.1 fusion.1
  125.2 0.9 fusion.24
  126.2 15.0 %all_to_all.30 = bf16[16,48,128]{2,1,0:T(8,128)(2,1)S(1)} all-to-all(bf16[16,48,128]{2,1,0:T(8,128)(2,1)S(1)} %bitcast.211), channel_id=1, replica_groups=mesh['tile'=16,'tensor'=16] {'tile'}, dimensions={0} | all-to-all | bytes 393216 | tf_op jit(solution)/shard_map/all_to_all | solution.py:209
  141.2 0.7 copy-done.5
  141.9 2.6 convolution_convert_fusion
  144.6 4.7 %all-to-all-start.3 = ((bf16[16,4,8,3072]{3,2,1,0:T(8,128)(2,1)}), bf16[16,4,8,3072]{3,2,1,0:T(8,128)(2,1)}, u32[]{:S(2)}, u32[]{:S(2)}) async-start(bf16[16,4,8,3072]{3,2,1,0:T(8,128)(2,1)} %bitcast.199), calls=%async_computation.3 | async-start | bytes 6291456 | tf_op jit(solution)/shard_map/all_to_all | solution.py:87
  149.5 0.7 slice_bitcast_fusion.6
  150.2 48.7 %all-to-all-done.3 = bf16[16,4,8,3072]{3,2,1,0:T(8,128)(2,1)} async-done(((bf16[16,4,8,3072]{3,2,1,0:T(8,128)(2,1)}), bf16[16,4,8,3072]{3,2,1,0:T(8,128)(2,1)}, u32[]{:S(2)}, u32[]{:S(2)}) %all-to-all-start.3) | async-done | bytes 3145760 | tf_op jit(solution)/shard_map/all_to_all | solution.py:87
  198.9 2.5 convert_reduce_fusion.1
  201.9 0.8 fusion.50
  202.7 0.5 slice.179
  203.9 3.0 fusion
  206.9 4.4 %all-to-all-start.5 = ((bf16[16,2,8,3072]{3,2,1,0:T(8,128)(2,1)}), bf16[16,2,8,3072]{3,2,1,0:T(8,128)(2,1)}, u32[]{:S(2)}, u32[]{:S(2)}) async-start(bf16[16,2,8,3072]{3,2,1,0:T(8,128)(2,1)} %bitcast.200), calls=%async_computation.5 | async-start | bytes 3145728 | tf_op jit(solution)/shard_map/all_to_all | solution.py:87
  211.3 50.4 %all-gather.5.cloned.1.call-done = bf16[64,8,3072]{2,1,0:T(8,128)(2,1)} async-done(((bf16[4,8,3072]{2,1,0:T(8,128)(2,1)}), bf16[64,8,3072]{2,1,0:T(8,128)(2,1)}) %all-gather.5.cloned.1.call-update) | async-done | bytes 3145744 | tf_op jit(solution)/shard_map/all_gather | solution.py:226
  261.7 7.8 %convolution_convert_fusion.1 = bf16[512,3072]{1,0:T(8,128)(2,1)} fusion(bf16[384,3072]{1,0:T(8,128)(2,1)S(1)} %copy-done, bf16[3072,384]{1,0:T(8,128)(2,1)} %param.33, bf16[64,8,3072]{2,1,0:T(8,128)(2,1)} %all-gather.5.cloned.1.call-done), kind=kOutput, calls=%fused_computation.5 | convolution fusion | flops 2419261440 | bytes 11010048 | tf_op jit(solution)/shard_map/dot_general | solution.py:232
  269.5 4.7 %all-to-all-start.4 = ((bf16[16,4,8,3072]{3,2,1,0:T(8,128)(2,1)}), bf16[16,4,8,3072]{3,2,1,0:T(8,128)(2,1)}, u32[]{:S(2)}, u32[]{:S(2)}) async-start(bf16[16,4,8,3072]{3,2,1,0:T(8,128)(2,1)} %bitcast.201), calls=%async_computation.4 | async-start | bytes 6291456 | tf_op jit(solution)/shard_map/all_to_all | solution.py:87
  274.2 1.2 fusion.115
  275.4 0.7 copy_bitcast_fusion
  276.1 1.6 convert_reduce_fusion.2
  277.8 0.7 copy.97
  278.6 42.8 %all-to-all-done.4 = bf16[16,4,8,3072]{3,2,1,0:T(8,128)(2,1)} async-done(((bf16[16,4,8,3072]{3,2,1,0:T(8,128)(2,1)}), bf16[16,4,8,3072]{3,2,1,0:T(8,128)(2,1)}, u32[]{:S(2)}, u32[]{:S(2)}) %all-to-all-start.4) | async-done | bytes 3145760 | tf_op jit(solution)/shard_map/all_to_all | solution.py:87
  321.4 2.5 convert_reduce_fusion
  324.3 1.3 convolution_bitcast_fusion
  325.8 1.9 collective-permute-start
  327.7 3.6 %collective-permute-start.1 = (f32[8,1,128]{2,1,0:T(1,128)S(1)}, f32[8,1,128]{2,1,0:T(1,128)S(1)}, u32[]{:S(2)}, u32[]{:S(2)}) collective-permute-start(f32[8,1,128]{2,1,0:T(1,128)S(1)} %get-tuple-element.52), channel_id=1, source_target_pairs={{16,0},{32,16},{48,32},{64,48},{80,64},{96,80},{112,96},{128,112},... | collective-permute-start | bytes 12296 | tf_op jit(solution)/shard_map/ppermute | solution.py:25
  331.3 1.1 fusion.57
  332.4 0.9 copy.96
  333.3 0.6 pad_maximum_fusion.1
  (97 shorter events, 3.0 us)
Async XLA Ops:
  7.2 254.5 %copy-start = (bf16[384,3072]{1,0:T(8,128)(2,1)S(1)}, bf16[384,3072]{1,0:T(8,128)(2,1)}, u32[]{:S(2)}) copy-start(bf16[384,3072]{1,0:T(8,128)(2,1)} %param.34) | copy-start | bytes 7077892
  7.2 5.1 %copy-start.2 = (bf16[8,2,3072]{2,1,0:T(2,128)(2,1)S(1)}, bf16[8,2,3072]{2,1,0:T(2,128)(2,1)}, u32[]{:S(2)}) copy-start(bf16[8,2,3072]{2,1,0:T(2,128)(2,1)} %param.19) | copy-start | bytes 294916
  7.2 5.2 %copy-start.12 = (f32[8,3,3072]{2,0,1:T(8,128)S(1)}, f32[8,3,3072]{2,0,1:T(8,128)}, u32[]{:S(2)}) copy-start(f32[8,3,3072]{2,0,1:T(8,128)} %param.25) | copy-start | bytes 884740
  7.2 69.7 %all-gather.3.cloned.1.call-start = ((), (), s32[]{:S(2)}) async-start(), calls=%async_computation.6 | async-start | bytes 3342336 | tf_op jit(solution)/shard_map/all_gather | solution.py:128
  14.5 34.4 %all-to-all-start = ((bf16[16,2,8,3072]{3,2,1,0:T(8,128)(2,1)}), bf16[16,2,8,3072]{3,2,1,0:T(8,128)(2,1)}, u32[]{:S(2)}, u32[]{:S(2)}) async-start(bf16[16,2,8,3072]{3,2,1,0:T(8,128)(2,1)} %broadcast_in_dim.42), calls=%async_computation | async-start | bytes 3145728 | tf_op jit(solution)/shard_map/all_to_all | solution.py:131
  21.6 4.3 %copy-start.21 = (s32[8,2]{0,1:T(2,128)S(1)}, s32[8,2]{0,1:T(2,128)}, u32[]{:S(2)}) copy-start(s32[8,2]{0,1:T(2,128)} %param.22) | copy-start | bytes 196
  25.9 8.1 %copy-start.20 = (f32[2,2,128]{2,1,0:T(2,128)S(1)}, f32[2,2,128]{2,1,0:T(2,128)}, u32[]{:S(2)}) copy-start(f32[2,2,128]{2,1,0:T(2,128)} %param.32) | copy-start | bytes 6148
  85.2 1.4 copy-start.17
  85.2 1.5 copy-start.18
  86.4 2.4 copy-start.16
  86.4 2.4 copy-start.15
  86.4 2.5 copy-start.14
  88.9 8.8 %copy-start.22 = (s32[8]{0:T(128)S(1)}, s32[8]{0:T(128)}, u32[]{:S(2)}) copy-start(s32[8]{0:T(128)} %param.23) | copy-start | bytes 100
  90.2 30.9 %all-to-all-start.1 = ((bf16[16,240,1,128]{3,1,2,0:T(8,128)(2,1)}), bf16[16,240,1,128]{3,1,2,0:T(8,128)(2,1)}, u32[]{:S(2)}, u32[]{:S(2)}) async-start(bf16[16,240,1,128]{3,1,2,0:T(8,128)(2,1)} %pad_maximum_fusion), calls=%async_computation.1 | async-start | bytes 1966080 | tf_op jit(solution)/shard_map/all_to_all | solution.py:181
  125.2 16.7 %copy-start.6 = (bf16[128,3072]{1,0:T(8,128)(2,1)S(1)}, bf16[128,3072]{1,0:T(8,128)(2,1)}, u32[]{:S(2)}) copy-start(bf16[128,3072]{1,0:T(8,128)(2,1)} %param.30) | copy-start | bytes 2359300
  141.2 0.7 copy-start.5
  144.6 4.9 %copy-start.13 = (f32[8,3,3072]{2,0,1:T(8,128)S(1)}, f32[8,3,3072]{2,0,1:T(8,128)}, u32[]{:S(2)}) copy-start(f32[8,3,3072]{2,0,1:T(8,128)} %param.26) | copy-start | bytes 884740
  144.6 54.4 %all-to-all-start.3 = ((bf16[16,4,8,3072]{3,2,1,0:T(8,128)(2,1)}), bf16[16,4,8,3072]{3,2,1,0:T(8,128)(2,1)}, u32[]{:S(2)}, u32[]{:S(2)}) async-start(bf16[16,4,8,3072]{3,2,1,0:T(8,128)(2,1)} %bitcast.199), calls=%async_computation.3 | async-start | bytes 6291456 | tf_op jit(solution)/shard_map/all_to_all | solution.py:87
  149.2 52.2 %copy-start.4 = (f32[8,3072]{1,0:T(8,128)S(1)}, f32[8,3072]{1,0:T(8,128)}, u32[]{:S(2)}) copy-start(f32[8,3072]{1,0:T(8,128)} %get-tuple-element.36) | copy-start | bytes 294916
  149.3 112.4 %all-gather.5.cloned.1.call-start = ((), (), s32[]{:S(2)}) async-start(), calls=%async_computation.7 | async-start | bytes 3342336 | tf_op jit(solution)/shard_map/all_gather | solution.py:226
  198.9 3.0 copy-start.7
  198.9 3.0 copy-start.8
  201.5 5.4 %copy-start.1 = (f32[4,8,3072]{2,1,0:T(8,128)}, f32[4,8,3072]{2,1,0:T(8,128)S(1)}, u32[]{:S(2)}) copy-start(f32[4,8,3072]{2,1,0:T(8,128)S(1)} %convert_reduce_fusion.1) | copy-start | bytes 1179652
  206.9 62.6 %all-to-all-start.5 = ((bf16[16,2,8,3072]{3,2,1,0:T(8,128)(2,1)}), bf16[16,2,8,3072]{3,2,1,0:T(8,128)(2,1)}, u32[]{:S(2)}, u32[]{:S(2)}) async-start(bf16[16,2,8,3072]{3,2,1,0:T(8,128)(2,1)} %bitcast.200), calls=%async_computation.5 | async-start | bytes 3145728 | tf_op jit(solution)/shard_map/all_to_all | solution.py:87
  269.5 4.7 %copy-start.23 = (s32[8]{0:T(128)S(1)}, s32[8]{0:T(128)}, u32[]{:S(2)}) copy-start(s32[8]{0:T(128)} %param.21) | copy-start | bytes 100
  269.5 8.3 %copy-start.3 = (bf16[8,2,3072]{2,1,0:T(2,128)(2,1)S(1)}, bf16[8,2,3072]{2,1,0:T(2,128)(2,1)}, u32[]{:S(2)}) copy-start(bf16[8,2,3072]{2,1,0:T(2,128)(2,1)} %param.19) | copy-start | bytes 294916
  269.5 8.3 %copy-start.11 = (f32[8,3072]{1,0:T(8,128)S(1)}, f32[8,3072]{1,0:T(8,128)}, u32[]{:S(2)}) copy-start(f32[8,3072]{1,0:T(8,128)} %get-tuple-element.30) | copy-start | bytes 294916
  269.5 51.9 %all-to-all-start.4 = ((bf16[16,4,8,3072]{3,2,1,0:T(8,128)(2,1)}), bf16[16,4,8,3072]{3,2,1,0:T(8,128)(2,1)}, u32[]{:S(2)}, u32[]{:S(2)}) async-start(bf16[16,4,8,3072]{3,2,1,0:T(8,128)(2,1)} %bitcast.201), calls=%async_computation.4 | async-start | bytes 6291456 | tf_op jit(solution)/shard_map/all_to_all | solution.py:87
  277.8 47.9 %copy-start.19 = (f32[8,2,128]{2,1,0:T(2,128)S(1)}, f32[8,2,128]{2,1,0:T(2,128)}, u32[]{:S(2)}) copy-start(f32[8,2,128]{2,1,0:T(2,128)} %param.20) | copy-start | bytes 24580
  321.4 2.9 copy-start.9
  321.4 2.9 copy-start.10
  325.8 7.5 %collective-permute-start = (f32[8,1,128]{2,1,0:T(1,128)S(1)}, f32[8,1,128]{2,1,0:T(1,128)S(1)}, u32[]{:S(2)}, u32[]{:S(2)}) collective-permute-start(f32[8,1,128]{2,1,0:T(1,128)S(1)} %get-tuple-element.51), channel_id=1, source_target_pairs={{0,16},{16,32},{32,48},{48,64},{64,80},{80,96},{96,112},{112,128},... | collective-permute-start | bytes 12296 | tf_op jit(solution)/shard_map/ppermute | solution.py:24
  327.7 5.6 %collective-permute-start.1 = (f32[8,1,128]{2,1,0:T(1,128)S(1)}, f32[8,1,128]{2,1,0:T(1,128)S(1)}, u32[]{:S(2)}, u32[]{:S(2)}) collective-permute-start(f32[8,1,128]{2,1,0:T(1,128)S(1)} %get-tuple-element.52), channel_id=1, source_target_pairs={{16,0},{32,16},{48,32},{64,48},{80,64},{96,80},{112,96},{128,112},... | collective-permute-start | bytes 12296 | tf_op jit(solution)/shard_map/ppermute | solution.py:25
Sparse Core Ops, SparseCore 0:
  11.3 65.5 all-gather.2
  202.8 58.8 all-gather.4

commit v7 on v6

--- a/solution.py
+++ b/solution.py
@@ -125,13 +125,12 @@
     image_count = owners * own_image
     text_tile = owners * own_text
     block_len = text_tile + image_count
-    image_mod = lax.all_gather(image_mod_own, "tensor", axis=0, tiled=True).reshape(
-        image_count * requests, model_width
-    )
-    text_mod = lax.all_to_all(
-        jnp.broadcast_to(text_mod_own[None], (owners,) + text_mod_own.shape), "tensor", 0, 0,
-        tiled=True,
-    ).reshape(text_tile * requests, model_width)
+    joined = jnp.concatenate([image_mod_own, text_mod_own], 0)
+    gathered = lax.all_to_all(
+        jnp.broadcast_to(joined[None], (owners,) + joined.shape), "tensor", 0, 0, tiled=True
+    )
+    image_mod = gathered[:, :own_image].reshape(image_count * requests, model_width)
+    text_mod = gathered[:, own_image:].reshape(text_tile * requests, model_width)
     tile_index = lax.axis_index("tile")
     token_index = jnp.arange(image_count, dtype=jnp.int32)
     owner = token_index // own_image
@@ -223,7 +222,9 @@
         jnp.bfloat16
     )
     mlp_mod = modulate(image_mid, mod_mlp[None, :, 0, :], mod_mlp[None, :, 1, :])
-    piece = lax.all_gather(mlp_mod, "tensor", axis=0, tiled=True)
+    piece = lax.all_to_all(
+        jnp.broadcast_to(mlp_mod[None], (owners,) + mlp_mod.shape), "tensor", 0, 0, tiled=True
+    ).reshape(image_count, requests, model_width)
     grown = jnp.dot(piece.reshape(-1, model_width), mlp_expand, preferred_element_type=jnp.float32)
     activated = jax.nn.gelu(grown, approximate=True).astype(jnp.bfloat16)
     text_out = (text_own.astype(jnp.float32) + mod_text[None, :, 2, :] * text_sum).astype(

time: 345 us -> 363 us (1.052)
  waiting for transfers between devices: 202 us -> 223 us
  between operations: 15.2 us -> 1.9 us
  local copies, waits for them, and re-layouts: 23.6 us -> 31.6 us
  starting transfers between devices: 34.2 us -> 41.3 us
  matrix products: 24.1 us -> 19.3 us
    all_to_all x1 -> x2, waiting for transfers between devices: 14.9 us -> 100 us  [the longest x1 57.9 us: per_device(): lax.all_to_all(jnp.broadcast_to(joined[None], (owners,) + joined.shape),...]
    all_gather x2 -> x0, waiting for transfers between devices: 73.6 us -> none  [the longest x1 50.4 us: per_device(): piece = lax.all_gather(mlp_mod, 'tensor', axis=0, tiled=True)]
    all_to_all x3, waiting for transfers between devices: 91.5 us -> 100 us  [sum_over_tensor(): parts = lax.all_to_all(parts, 'tensor', 0, 0, tiled=True)]
    all_to_all x1 -> x2, starting transfers between devices: 7.08 us -> 11.6 us  [the longest x1 7.08 us: per_device(): lax.all_to_all(jnp.broadcast_to(joined[None], (owners,) + joined.shape),...]
    slice x0 -> x2, local copies, waits for them, and re-layouts: none -> 3.95 us  [the longest x1 2.31 us: per_device(): gathered[:, :own_image].reshape(image_count * requests, model_width)]
    unnamed x52 -> x63, local copies, waits for them, and re-layouts: 11 us -> 10.6 us
  transfers between devices with their start and end apart: 9 -> 8, of which waited for: 6 -> 6; matrix products, arithmetic and copies ran while one was open for 12% -> 9% of each run, Pallas kernels for 0% -> 0%
where the time goes in v7:
time: 363 us; the launch traced here: 357 us
  waiting for transfers between devices  223 us (61%)
  starting transfers between devices  41.3 us (11%)
  local copies, waits for them, and re-layouts  31.6 us (9%)
  other arithmetic  25.4 us (7%)
  matrix products  19.3 us (5%)
  blocking collectives  15 us (4%)
    all_to_all x3, waiting for transfers between devices, sum_over_tensor(): parts = lax.all_to_all(parts, 'tensor', 0, 0, tiled=True)  100 us
    all_to_all x1, waiting for transfers between devices, per_device(): lax.all_to_all(jnp.broadcast_to(joined[None], (owners,) + joined.shape),...  57.9 us
    all_to_all x1, waiting for transfers between devices, per_device(): lax.all_to_all(jnp.broadcast_to(mlp_mod[None], (owners,) + mlp_mod.shape)...  42.6 us
    all_to_all x1, waiting for transfers between devices, per_device(): incoming = lax.all_to_all(outgoing, 'tile', 0, 0, tiled=True)  22.2 us
    all_to_all x1, blocking collectives, per_device(): returned = lax.all_to_all(attended_mine, 'tile', 0, 0, tiled=True)  15 us
    all_to_all x3, starting transfers between devices, sum_over_tensor(): parts = lax.all_to_all(parts, 'tensor', 0, 0, tiled=True)  14.3 us
    unnamed x63, local copies, waits for them, and re-layouts  10.6 us
    all_to_all x1, starting transfers between devices, per_device(): incoming = lax.all_to_all(outgoing, 'tile', 0, 0, tiled=True)  8.59 us
  transfers between devices with their start and end apart: 8, of which 6 were waited for; matrix products, arithmetic and copies ran while one was open for 9% of the time, Pallas kernels for 0%

profile of v7, /device:TPU:32, one launch (start us, length us, event | category | flops | bytes accessed | tf_op | source)
XLA Modules:
  0.0 357.4 jit_solution(6789910971055761588)
XLA Ops:
  0.7 1.2 copy.106
  2.2 1.6 slice_bitcast_fusion.9
  3.8 1.6 slice_bitcast_fusion.4
  5.4 1.0 fusion.61
  6.4 1.1 fusion.64
  7.8 2.8 broadcast_in_dim.44
  10.6 7.1 %all-to-all-start = ((bf16[16,6,8,3072]{3,2,1,0:T(8,128)(2,1)}), bf16[16,6,8,3072]{3,2,1,0:T(8,128)(2,1)}, u32[]{:S(2)}, u32[]{:S(2)}) async-start(bf16[16,6,8,3072]{3,2,1,0:T(8,128)(2,1)} %broadcast_in_dim.44), calls=%async_computation | async-start | bytes 9437184 | tf_op jit(solution)/shard_map/all_to_all | solution.py:129
  17.7 4.3 %copy.84 = bf16[3072,3,128]{0,2,1:T(8,128)(2,1)} copy(bf16[3072,3,128]{2,0,1:T(8,128)(2,1)} %param.28) | data formatting | bytes 4718592 | tf_op args[10]
  22.1 0.7 copy.88
  22.8 0.7 copy.89
  23.5 4.3 %copy.83 = bf16[3072,3,128]{0,2,1:T(8,128)(2,1)} copy(bf16[3072,3,128]{2,0,1:T(8,128)(2,1)} %param.29) | data formatting | bytes 4718592 | tf_op args[11]
  28.3 0.5 compare_and_fusion
  28.8 0.5 compare_select_fusion
  29.3 0.6 iota_and_fusion
  29.9 0.6 slice_bitcast_fusion.14
  30.5 57.9 %all-to-all-done = bf16[16,6,8,3072]{3,2,1,0:T(8,128)(2,1)} async-done(((bf16[16,6,8,3072]{3,2,1,0:T(8,128)(2,1)}), bf16[16,6,8,3072]{3,2,1,0:T(8,128)(2,1)}, u32[]{:S(2)}, u32[]{:S(2)}) %all-to-all-start) | async-done | bytes 4718624 | tf_op jit(solution)/shard_map/all_to_all | solution.py:129
  88.4 2.3 slice.172
  91.0 1.8 fusion.10
  92.8 0.8 multiply_reduce_fusion.2
  93.6 0.8 copy.86
  94.4 0.7 copy.87
  95.2 0.8 copy.92
  96.0 0.7 copy.93
  96.7 1.0 multiply_multiply_fusion.2
  98.1 1.6 slice.170
  100.1 1.0 fusion.13
  101.5 1.4 fusion.55
  103.2 1.1 pad_maximum_fusion
  104.3 8.6 %all-to-all-start.1 = ((bf16[16,240,1,128]{3,1,2,0:T(8,128)(2,1)}), bf16[16,240,1,128]{3,1,2,0:T(8,128)(2,1)}, u32[]{:S(2)}, u32[]{:S(2)}) async-start(bf16[16,240,1,128]{3,1,2,0:T(8,128)(2,1)} %pad_maximum_fusion), calls=%async_computation.1 | async-start | bytes 1966080 | tf_op jit(solution)/shard_map/all_to_all | solution.py:180
  112.9 0.6 dynamic_slice.3
  113.4 0.7 fusion.90
  114.1 22.2 %all-to-all-done.1 = bf16[16,240,1,128]{3,1,2,0:T(8,128)(2,1)} async-done(((bf16[16,240,1,128]{3,1,2,0:T(8,128)(2,1)}), bf16[16,240,1,128]{3,1,2,0:T(8,128)(2,1)}, u32[]{:S(2)}, u32[]{:S(2)}) %all-to-all-start.1) | async-done | bytes 983072 | tf_op jit(solution)/shard_map/all_to_all | solution.py:180
  136.3 1.2 fusion.100
  137.5 0.9 slice.186
  138.4 0.9 select_reduce_fusion
  139.3 1.1 fusion.1
  140.4 0.9 fusion.19
  141.3 15.0 %all_to_all.35 = bf16[16,48,128]{2,1,0:T(8,128)(2,1)S(1)} all-to-all(bf16[16,48,128]{2,1,0:T(8,128)(2,1)S(1)} %bitcast.205), channel_id=1, replica_groups=mesh['tile'=16,'tensor'=16] {'tile'}, dimensions={0} | all-to-all | bytes 393216 | tf_op jit(solution)/shard_map/all_to_all | solution.py:208
  156.4 0.7 copy-done.7
  157.1 2.7 convolution_convert_fusion
  159.7 5.3 %all-to-all-start.3 = ((bf16[16,4,8,3072]{3,2,1,0:T(8,128)(2,1)}), bf16[16,4,8,3072]{3,2,1,0:T(8,128)(2,1)}, u32[]{:S(2)}, u32[]{:S(2)}) async-start(bf16[16,4,8,3072]{3,2,1,0:T(8,128)(2,1)} %bitcast.191), calls=%async_computation.3 | async-start | bytes 6291456 | tf_op jit(solution)/shard_map/all_to_all | solution.py:87
  165.0 0.7 slice_bitcast_fusion.6
  165.7 48.5 %all-to-all-done.3 = bf16[16,4,8,3072]{3,2,1,0:T(8,128)(2,1)} async-done(((bf16[16,4,8,3072]{3,2,1,0:T(8,128)(2,1)}), bf16[16,4,8,3072]{3,2,1,0:T(8,128)(2,1)}, u32[]{:S(2)}, u32[]{:S(2)}) %all-to-all-start.3) | async-done | bytes 3145760 | tf_op jit(solution)/shard_map/all_to_all | solution.py:87
  214.2 2.5 convert_reduce_fusion.1
  217.3 2.0 broadcast_in_dim.90
  219.3 4.5 %all-to-all-start.4 = ((bf16[16,4,8,3072]{3,2,1,0:T(8,128)(2,1)}), bf16[16,4,8,3072]{3,2,1,0:T(8,128)(2,1)}, u32[]{:S(2)}, u32[]{:S(2)}) async-start(bf16[16,4,8,3072]{3,2,1,0:T(8,128)(2,1)} %broadcast_in_dim.90), calls=%async_computation.4 | async-start | bytes 6291456 | tf_op jit(solution)/shard_map/all_to_all | solution.py:225
  225.0 3.0 fusion
  228.0 42.6 %all-to-all-done.4 = bf16[16,4,8,3072]{3,2,1,0:T(8,128)(2,1)} async-done(((bf16[16,4,8,3072]{3,2,1,0:T(8,128)(2,1)}), bf16[16,4,8,3072]{3,2,1,0:T(8,128)(2,1)}, u32[]{:S(2)}, u32[]{:S(2)}) %all-to-all-start.4) | async-done | bytes 3145760 | tf_op jit(solution)/shard_map/all_to_all | solution.py:225
  270.6 4.4 %all-to-all-start.6 = ((bf16[16,2,8,3072]{3,2,1,0:T(8,128)(2,1)}), bf16[16,2,8,3072]{3,2,1,0:T(8,128)(2,1)}, u32[]{:S(2)}, u32[]{:S(2)}) async-start(bf16[16,2,8,3072]{3,2,1,0:T(8,128)(2,1)} %bitcast.192), calls=%async_computation.6 | async-start | bytes 3145728 | tf_op jit(solution)/shard_map/all_to_all | solution.py:87
  275.0 7.8 %convolution_convert_fusion.1 = bf16[512,3072]{1,0:T(8,128)(2,1)} fusion(bf16[384,3072]{1,0:T(8,128)(2,1)S(1)} %copy-done, bf16[512,3072]{1,0:T(8,128)(2,1)} %bitcast.57, bf16[3072,384]{1,0:T(8,128)(2,1)} %param.33), kind=kOutput, calls=%fused_computation.5 | convolution fusion | flops 2419261440 | bytes 11010048 | tf_op jit(solution)/shard_map/dot_general | solution.py:233
  282.8 14.6 %all-to-all-done.6 = bf16[16,2,8,3072]{3,2,1,0:T(8,128)(2,1)} async-done(((bf16[16,2,8,3072]{3,2,1,0:T(8,128)(2,1)}), bf16[16,2,8,3072]{3,2,1,0:T(8,128)(2,1)}, u32[]{:S(2)}, u32[]{:S(2)}) %all-to-all-start.6) | async-done | bytes 1572896 | tf_op jit(solution)/shard_map/all_to_all | solution.py:87
  297.4 4.6 %all-to-all-start.5 = ((bf16[16,4,8,3072]{3,2,1,0:T(8,128)(2,1)}), bf16[16,4,8,3072]{3,2,1,0:T(8,128)(2,1)}, u32[]{:S(2)}, u32[]{:S(2)}) async-start(bf16[16,4,8,3072]{3,2,1,0:T(8,128)(2,1)} %bitcast.193), calls=%async_computation.5 | async-start | bytes 6291456 | tf_op jit(solution)/shard_map/all_to_all | solution.py:87
  302.1 1.2 fusion.105
  303.2 0.7 copy_bitcast_fusion
  304.0 1.6 convert_reduce_fusion.2
  305.7 0.7 copy.102
  306.4 37.2 %all-to-all-done.5 = bf16[16,4,8,3072]{3,2,1,0:T(8,128)(2,1)} async-done(((bf16[16,4,8,3072]{3,2,1,0:T(8,128)(2,1)}), bf16[16,4,8,3072]{3,2,1,0:T(8,128)(2,1)}, u32[]{:S(2)}, u32[]{:S(2)}) %all-to-all-start.5) | async-done | bytes 3145760 | tf_op jit(solution)/shard_map/all_to_all | solution.py:87
  343.6 2.5 convert_reduce_fusion
  346.5 1.3 convolution_bitcast_fusion
  348.0 1.9 collective-permute-start
  349.9 4.9 %collective-permute-start.1 = (f32[8,1,128]{2,1,0:T(1,128)S(1)}, f32[8,1,128]{2,1,0:T(1,128)S(1)}, u32[]{:S(2)}, u32[]{:S(2)}) collective-permute-start(f32[8,1,128]{2,1,0:T(1,128)S(1)} %get-tuple-element.46), channel_id=1, source_target_pairs={{16,0},{32,16},{48,32},{64,48},{80,64},{96,80},{112,96},{128,112},... | collective-permute-start | bytes 12296 | tf_op jit(solution)/shard_map/ppermute | solution.py:25
  354.8 1.1 fusion.48
  355.9 0.9 copy.105
  356.8 0.6 pad_maximum_fusion.2
  (109 shorter events, 4.6 us)
Async XLA Ops:
  0.6 274.4 %copy-start = (bf16[384,3072]{1,0:T(8,128)(2,1)S(1)}, bf16[384,3072]{1,0:T(8,128)(2,1)}, u32[]{:S(2)}) copy-start(bf16[384,3072]{1,0:T(8,128)(2,1)} %param.34) | copy-start | bytes 7077892
  0.6 7.0 %copy-start.4 = (bf16[8,2,3072]{2,1,0:T(2,128)(2,1)S(1)}, bf16[8,2,3072]{2,1,0:T(2,128)(2,1)}, u32[]{:S(2)}) copy-start(bf16[8,2,3072]{2,1,0:T(2,128)(2,1)} %param.19) | copy-start | bytes 294916
  10.6 77.8 %all-to-all-start = ((bf16[16,6,8,3072]{3,2,1,0:T(8,128)(2,1)}), bf16[16,6,8,3072]{3,2,1,0:T(8,128)(2,1)}, u32[]{:S(2)}, u32[]{:S(2)}) async-start(bf16[16,6,8,3072]{3,2,1,0:T(8,128)(2,1)} %broadcast_in_dim.44), calls=%async_computation | async-start | bytes 9437184 | tf_op jit(solution)/shard_map/all_to_all | solution.py:129
  17.7 4.3 %copy-start.21 = (s32[8,2]{0,1:T(2,128)S(1)}, s32[8,2]{0,1:T(2,128)}, u32[]{:S(2)}) copy-start(s32[8,2]{0,1:T(2,128)} %param.22) | copy-start | bytes 196
  22.0 8.0 %copy-start.20 = (f32[2,2,128]{2,1,0:T(2,128)S(1)}, f32[2,2,128]{2,1,0:T(2,128)}, u32[]{:S(2)}) copy-start(f32[2,2,128]{2,1,0:T(2,128)} %param.32) | copy-start | bytes 6148
  88.4 2.6 copy-start.3
  97.9 2.1 copy-start.2
  100.0 1.3 copy-start.18
  100.0 1.3 copy-start.19
  100.0 1.4 copy-start.15
  100.0 1.4 copy-start.16
  100.0 1.4 copy-start.22
  100.0 1.4 copy-start.23
  100.0 1.4 copy-start.24
  100.1 1.4 copy-start.25
  100.1 1.4 copy-start.26
  100.1 1.4 copy-start.27
  103.0 9.9 %copy-start.28 = (s32[8]{0:T(128)S(1)}, s32[8]{0:T(128)}, u32[]{:S(2)}) copy-start(s32[8]{0:T(128)} %param.23) | copy-start | bytes 100
  104.3 32.0 %all-to-all-start.1 = ((bf16[16,240,1,128]{3,1,2,0:T(8,128)(2,1)}), bf16[16,240,1,128]{3,1,2,0:T(8,128)(2,1)}, u32[]{:S(2)}, u32[]{:S(2)}) async-start(bf16[16,240,1,128]{3,1,2,0:T(8,128)(2,1)} %pad_maximum_fusion), calls=%async_computation.1 | async-start | bytes 1966080 | tf_op jit(solution)/shard_map/all_to_all | solution.py:180
  140.4 16.7 %copy-start.8 = (bf16[128,3072]{1,0:T(8,128)(2,1)S(1)}, bf16[128,3072]{1,0:T(8,128)(2,1)}, u32[]{:S(2)}) copy-start(bf16[128,3072]{1,0:T(8,128)(2,1)} %param.30) | copy-start | bytes 2359300
  156.4 0.7 copy-start.7
  159.7 5.3 %copy-start.14 = (f32[8,3,3072]{2,0,1:T(8,128)S(1)}, f32[8,3,3072]{2,0,1:T(8,128)}, u32[]{:S(2)}) copy-start(f32[8,3,3072]{2,0,1:T(8,128)} %param.26) | copy-start | bytes 884740
  159.7 54.5 %all-to-all-start.3 = ((bf16[16,4,8,3072]{3,2,1,0:T(8,128)(2,1)}), bf16[16,4,8,3072]{3,2,1,0:T(8,128)(2,1)}, u32[]{:S(2)}, u32[]{:S(2)}) async-start(bf16[16,4,8,3072]{3,2,1,0:T(8,128)(2,1)} %bitcast.191), calls=%async_computation.3 | async-start | bytes 6291456 | tf_op jit(solution)/shard_map/all_to_all | solution.py:87
  165.0 51.8 %copy-start.6 = (f32[8,3072]{1,0:T(8,128)S(1)}, f32[8,3072]{1,0:T(8,128)}, u32[]{:S(2)}) copy-start(f32[8,3072]{1,0:T(8,128)} %get-tuple-element.30) | copy-start | bytes 294916
  214.2 3.0 copy-start.9
  214.2 3.0 copy-start.10
  216.7 7.1 %copy-start.1 = (f32[4,8,3072]{2,1,0:T(8,128)}, f32[4,8,3072]{2,1,0:T(8,128)S(1)}, u32[]{:S(2)}) copy-start(f32[4,8,3072]{2,1,0:T(8,128)S(1)} %convert_reduce_fusion.1) | copy-start | bytes 1179652
  219.3 51.3 %all-to-all-start.4 = ((bf16[16,4,8,3072]{3,2,1,0:T(8,128)(2,1)}), bf16[16,4,8,3072]{3,2,1,0:T(8,128)(2,1)}, u32[]{:S(2)}, u32[]{:S(2)}) async-start(bf16[16,4,8,3072]{3,2,1,0:T(8,128)(2,1)} %broadcast_in_dim.90), calls=%async_computation.4 | async-start | bytes 6291456 | tf_op jit(solution)/shard_map/all_to_all | solution.py:225
  270.6 26.8 %all-to-all-start.6 = ((bf16[16,2,8,3072]{3,2,1,0:T(8,128)(2,1)}), bf16[16,2,8,3072]{3,2,1,0:T(8,128)(2,1)}, u32[]{:S(2)}, u32[]{:S(2)}) async-start(bf16[16,2,8,3072]{3,2,1,0:T(8,128)(2,1)} %bitcast.192), calls=%async_computation.6 | async-start | bytes 3145728 | tf_op jit(solution)/shard_map/all_to_all | solution.py:87
  297.4 4.6 %copy-start.29 = (s32[8]{0:T(128)S(1)}, s32[8]{0:T(128)}, u32[]{:S(2)}) copy-start(s32[8]{0:T(128)} %param.21) | copy-start | bytes 100
  297.4 8.2 %copy-start.5 = (bf16[8,2,3072]{2,1,0:T(2,128)(2,1)S(1)}, bf16[8,2,3072]{2,1,0:T(2,128)(2,1)}, u32[]{:S(2)}) copy-start(bf16[8,2,3072]{2,1,0:T(2,128)(2,1)} %param.19) | copy-start | bytes 294916
  297.4 8.3 %copy-start.13 = (f32[8,3072]{1,0:T(8,128)S(1)}, f32[8,3072]{1,0:T(8,128)}, u32[]{:S(2)}) copy-start(f32[8,3072]{1,0:T(8,128)} %get-tuple-element.24) | copy-start | bytes 294916
  297.4 46.2 %all-to-all-start.5 = ((bf16[16,4,8,3072]{3,2,1,0:T(8,128)(2,1)}), bf16[16,4,8,3072]{3,2,1,0:T(8,128)(2,1)}, u32[]{:S(2)}, u32[]{:S(2)}) async-start(bf16[16,4,8,3072]{3,2,1,0:T(8,128)(2,1)} %bitcast.193), calls=%async_computation.5 | async-start | bytes 6291456 | tf_op jit(solution)/shard_map/all_to_all | solution.py:87
  305.6 42.3 %copy-start.17 = (f32[8,2,128]{2,1,0:T(2,128)S(1)}, f32[8,2,128]{2,1,0:T(2,128)}, u32[]{:S(2)}) copy-start(f32[8,2,128]{2,1,0:T(2,128)} %param.20) | copy-start | bytes 24580
  343.6 2.9 copy-start.11
  343.6 2.9 copy-start.12
  348.0 8.8 %collective-permute-start = (f32[8,1,128]{2,1,0:T(1,128)S(1)}, f32[8,1,128]{2,1,0:T(1,128)S(1)}, u32[]{:S(2)}, u32[]{:S(2)}) collective-permute-start(f32[8,1,128]{2,1,0:T(1,128)S(1)} %get-tuple-element.45), channel_id=1, source_target_pairs={{0,16},{16,32},{32,48},{48,64},{64,80},{80,96},{96,112},{112,128},... | collective-permute-start | bytes 12296 | tf_op jit(solution)/shard_map/ppermute | solution.py:24
  349.9 6.8 %collective-permute-start.1 = (f32[8,1,128]{2,1,0:T(1,128)S(1)}, f32[8,1,128]{2,1,0:T(1,128)S(1)}, u32[]{:S(2)}, u32[]{:S(2)}) collective-permute-start(f32[8,1,128]{2,1,0:T(1,128)S(1)} %get-tuple-element.46), channel_id=1, source_target_pairs={{16,0},{32,16},{48,32},{64,48},{80,64},{96,80},{112,96},{128,112},... | collective-permute-start | bytes 12296 | tf_op jit(solution)/shard_map/ppermute | solution.py:25

commit v8 on v6

--- a/solution.py
+++ b/solution.py
@@ -224,25 +224,33 @@
     )
     mlp_mod = modulate(image_mid, mod_mlp[None, :, 0, :], mod_mlp[None, :, 1, :])
     piece = lax.all_gather(mlp_mod, "tensor", axis=0, tiled=True)
-    grown = jnp.dot(piece.reshape(-1, model_width), mlp_expand, preferred_element_type=jnp.float32)
-    activated = jax.nn.gelu(grown, approximate=True).astype(jnp.bfloat16)
     text_out = (text_own.astype(jnp.float32) + mod_text[None, :, 2, :] * text_sum).astype(
         jnp.bfloat16
     )
-    mlp_term = jnp.dot(activated, mlp_reduce, preferred_element_type=jnp.float32).reshape(
-        image_count, requests, model_width
-    )
-    mlp_sum = sum_over_tensor(mlp_term, owners, NARROW_SUMS)
-    image_out = (image_mid.astype(jnp.float32) + mod_mlp[None, :, 2, :] * mlp_sum).astype(
-        jnp.bfloat16
-    )
-    final_in = modulate(image_out, mod_final[None, :, 0, :], mod_final[None, :, 1, :])
-    velocity = jnp.dot(
-        final_in.reshape(own_image * requests, model_width),
-        final_weight,
-        preferred_element_type=jnp.float32,
-    ).reshape(own_image, requests, final_weight.shape[1])
-    velocity = velocity.transpose(1, 0, 2).reshape(
+    half = requests // 2
+    image_outs, velocities = [], []
+    for lo, hi in ((0, half), (half, requests)):
+        grown = jnp.dot(
+            piece[:, lo:hi].reshape(-1, model_width), mlp_expand, preferred_element_type=jnp.float32
+        )
+        activated = jax.nn.gelu(grown, approximate=True).astype(jnp.bfloat16)
+        mlp_term = jnp.dot(activated, mlp_reduce, preferred_element_type=jnp.float32).reshape(
+            image_count, hi - lo, model_width
+        )
+        mlp_sum = sum_over_tensor(mlp_term, owners, NARROW_SUMS)
+        image_out = (
+            image_mid[:, lo:hi].astype(jnp.float32) + mod_mlp[None, lo:hi, 2, :] * mlp_sum
+        ).astype(jnp.bfloat16)
+        final_in = modulate(image_out, mod_final[None, lo:hi, 0, :], mod_final[None, lo:hi, 1, :])
+        velocity = jnp.dot(
+            final_in.reshape(own_image * (hi - lo), model_width),
+            final_weight,
+            preferred_element_type=jnp.float32,
+        ).reshape(own_image, hi - lo, final_weight.shape[1])
+        image_outs.append(image_out)
+        velocities.append(velocity)
+    image_out = jnp.concatenate(image_outs, 1)
+    velocity = jnp.concatenate(velocities, 1).transpose(1, 0, 2).reshape(
         requests, tile_rows, tile_cols * final_weight.shape[1]
     )
     step_float = step_index.astype(jnp.float32)

time: 345 us -> 360 us (1.043)
  local copies, waits for them, and re-layouts: 23.6 us -> 44.1 us
  waiting for transfers between devices: 202 us -> 188 us
  starting transfers between devices: 34.2 us -> 38.7 us
  matrix products: 24.1 us -> 28.2 us
    all_to_all x3 -> x4, waiting for transfers between devices: 91.5 us -> 76.4 us  [sum_over_tensor(): parts = lax.all_to_all(parts, 'tensor', 0, 0, tiled=True)]
    convert_element_type x0 -> x2, local copies, waits for them, and re-layouts: none -> 7.7 us  [sum_over_tensor(): parts = term.astype(jnp.bfloat16).reshape((owners, -1) + term.shape[1:])]
    reshape x1 -> x3, local copies, waits for them, and re-layouts: 0.09 us -> 7.53 us  [the longest x2 7.44 us: per_device(): piece[:, lo:hi].reshape(-1, model_width)]
    slice x1, local copies, waits for them, and re-layouts: 1.19 us -> 5.91 us  [per_device(): piece[:, lo:hi].reshape(-1, model_width)]
    all_to_all x3 -> x4, starting transfers between devices: 13.8 us -> 18.3 us  [sum_over_tensor(): parts = lax.all_to_all(parts, 'tensor', 0, 0, tiled=True)]
    dot_general x1 -> x2, matrix products: 7.78 us -> 10.6 us  [per_device(): jnp.dot(activated, mlp_reduce, preferred_element_type=jnp.float32)]
    reduce_sum x3 -> x4, other arithmetic: 6.7 us -> 8.36 us  [sum_over_tensor(): return jnp.sum(parts.astype(jnp.float32), 0)]
    unnamed x52 -> x58, local copies, waits for them, and re-layouts: 11 us -> 10.6 us
  transfers between devices with their start and end apart: 9 -> 10, of which waited for: 6 -> 8; matrix products, arithmetic and copies ran while one was open for 12% -> 18% of each run, Pallas kernels for 0% -> 0%
where the time goes in v8:
time: 360 us; the launch traced here: 355 us
  waiting for transfers between devices  188 us (52%)
  local copies, waits for them, and re-layouts  44.1 us (12%)
  starting transfers between devices  38.7 us (11%)
  matrix products  28.2 us (8%)
  other arithmetic  26.1 us (7%)
  between operations  15.3 us (4%)
  blocking collectives  15 us (4%)
    all_to_all x4, waiting for transfers between devices, sum_over_tensor(): parts = lax.all_to_all(parts, 'tensor', 0, 0, tiled=True)  76.4 us
    all_gather x1, waiting for transfers between devices, per_device(): piece = lax.all_gather(mlp_mod, 'tensor', axis=0, tiled=True)  50.2 us
    all_gather x1, waiting for transfers between devices, per_device(): lax.all_gather(image_mod_own, 'tensor', axis=0, tiled=True)  23.9 us
    all_to_all x1, waiting for transfers between devices, per_device(): incoming = lax.all_to_all(outgoing, 'tile', 0, 0, tiled=True)  22.2 us
    all_to_all x4, starting transfers between devices, sum_over_tensor(): parts = lax.all_to_all(parts, 'tensor', 0, 0, tiled=True)  18.3 us
    all_to_all x1, blocking collectives, per_device(): returned = lax.all_to_all(attended_mine, 'tile', 0, 0, tiled=True)  15 us
    all_to_all x1, waiting for transfers between devices, per_device(): lax.all_to_all(jnp.broadcast_to(text_mod_own[None], (owners,) + text_mod_...  15 us
    dot_general x2, matrix products, per_device(): jnp.dot(activated, mlp_reduce, preferred_element_type=jnp.float32)  10.6 us
  transfers between devices with their start and end apart: 10, of which 8 were waited for; matrix products, arithmetic and copies ran while one was open for 18% of the time, Pallas kernels for 0%

profile of v8, /device:TPU:32, one launch (start us, length us, event | category | flops | bytes accessed | tf_op | source)
XLA Modules:
  0.0 355.4 jit_solution(7799247402937604918)
XLA Ops:
  7.2 1.1 copy.68
  8.7 1.7 slice_bitcast_fusion.8
  10.4 0.8 add_convert_fusion.1
  11.5 0.7 slice_bitcast_fusion.4
  12.3 1.3 broadcast_in_dim.42
  13.6 7.1 %all-to-all-start = ((bf16[16,2,8,3072]{3,2,1,0:T(8,128)(2,1)}), bf16[16,2,8,3072]{3,2,1,0:T(8,128)(2,1)}, u32[]{:S(2)}, u32[]{:S(2)}) async-start(bf16[16,2,8,3072]{3,2,1,0:T(8,128)(2,1)} %broadcast_in_dim.42), calls=%async_computation | async-start | bytes 3145728 | tf_op jit(solution)/shard_map/all_to_all | solution.py:131
  20.7 4.3 %copy.71 = bf16[3072,3,128]{0,2,1:T(8,128)(2,1)} copy(bf16[3072,3,128]{2,0,1:T(8,128)(2,1)} %param.28) | data formatting | bytes 4718592 | tf_op args[10]
  25.2 0.7 copy.75
  25.8 0.7 copy.76
  26.5 4.3 %copy.70 = bf16[3072,3,128]{0,2,1:T(8,128)(2,1)} copy(bf16[3072,3,128]{2,0,1:T(8,128)(2,1)} %param.29) | data formatting | bytes 4718592 | tf_op args[11]
  33.1 15.0 %all-to-all-done = bf16[16,2,8,3072]{3,2,1,0:T(8,128)(2,1)} async-done(((bf16[16,2,8,3072]{3,2,1,0:T(8,128)(2,1)}), bf16[16,2,8,3072]{3,2,1,0:T(8,128)(2,1)}, u32[]{:S(2)}, u32[]{:S(2)}) %all-to-all-start) | async-done | bytes 1572896 | tf_op jit(solution)/shard_map/all_to_all | solution.py:131
  48.1 3.1 fusion.16
  51.4 0.6 fusion.106
  52.0 0.8 multiply_convert_fusion.1
  52.8 23.9 %all-gather.3.cloned.1.call-done = bf16[64,8,3072]{2,1,0:T(8,128)(2,1)} async-done(((bf16[4,8,3072]{2,1,0:T(8,128)(2,1)}), bf16[64,8,3072]{2,1,0:T(8,128)(2,1)}) %all-gather.3.cloned.1.call-update) | async-done | bytes 3145744 | tf_op jit(solution)/shard_map/all_gather | solution.py:128
  76.8 4.4 %fusion.11 = f32[64,8,3,1,128]{4,1,2,0,3:T(8,128)S(1)} fusion(bf16[3072,3,128]{0,2,1:T(8,128)(2,1)} %copy.71, bf16[64,8,3072]{2,1,0:T(8,128)(2,1)} %all-gather.3.cloned.1.call-done), kind=kOutput, calls=%fused_computation.20 | convolution fusion | flops 1207959552 | bytes 6291456 | tf_op jit(solution)/shard_map/dot_general | solution.py:148
  81.2 0.8 multiply_reduce_fusion.2
  82.0 0.8 copy.73
  82.8 0.7 copy.74
  83.5 0.8 copy.79
  84.4 0.7 copy.80
  85.1 1.0 multiply_multiply_fusion.3
  86.9 1.3 fusion.55
  88.6 1.1 pad_maximum_fusion
  89.6 7.5 %all-to-all-start.1 = ((bf16[16,240,1,128]{3,1,2,0:T(8,128)(2,1)}), bf16[16,240,1,128]{3,1,2,0:T(8,128)(2,1)}, u32[]{:S(2)}, u32[]{:S(2)}) async-start(bf16[16,240,1,128]{3,1,2,0:T(8,128)(2,1)} %pad_maximum_fusion), calls=%async_computation.1 | async-start | bytes 1966080 | tf_op jit(solution)/shard_map/all_to_all | solution.py:181
  97.7 0.7 fusion.116
  98.4 22.2 %all-to-all-done.1 = bf16[16,240,1,128]{3,1,2,0:T(8,128)(2,1)} async-done(((bf16[16,240,1,128]{3,1,2,0:T(8,128)(2,1)}), bf16[16,240,1,128]{3,1,2,0:T(8,128)(2,1)}, u32[]{:S(2)}, u32[]{:S(2)}) %all-to-all-start.1) | async-done | bytes 983072 | tf_op jit(solution)/shard_map/all_to_all | solution.py:181
  120.6 1.2 fusion.130
  121.7 0.9 slice.204
  122.7 0.9 select_reduce_fusion
  123.6 1.1 fusion.1
  124.7 0.9 fusion.22
  125.6 15.0 %all_to_all.35 = bf16[16,48,128]{2,1,0:T(8,128)(2,1)S(1)} all-to-all(bf16[16,48,128]{2,1,0:T(8,128)(2,1)S(1)} %bitcast.201), channel_id=1, replica_groups=mesh['tile'=16,'tensor'=16] {'tile'}, dimensions={0} | all-to-all | bytes 393216 | tf_op jit(solution)/shard_map/all_to_all | solution.py:209
  140.6 2.7 convolution_convert_fusion
  143.3 4.7 %all-to-all-start.3 = ((bf16[16,4,8,3072]{3,2,1,0:T(8,128)(2,1)}), bf16[16,4,8,3072]{3,2,1,0:T(8,128)(2,1)}, u32[]{:S(2)}, u32[]{:S(2)}) async-start(bf16[16,4,8,3072]{3,2,1,0:T(8,128)(2,1)} %bitcast.188), calls=%async_computation.3 | async-start | bytes 6291456 | tf_op jit(solution)/shard_map/all_to_all | solution.py:87
  148.2 0.7 add_bitcast_fusion
  148.9 48.8 %all-to-all-done.3 = bf16[16,4,8,3072]{3,2,1,0:T(8,128)(2,1)} async-done(((bf16[16,4,8,3072]{3,2,1,0:T(8,128)(2,1)}), bf16[16,4,8,3072]{3,2,1,0:T(8,128)(2,1)}, u32[]{:S(2)}, u32[]{:S(2)}) %all-to-all-start.3) | async-done | bytes 3145760 | tf_op jit(solution)/shard_map/all_to_all | solution.py:87
  197.7 2.5 convert_reduce_fusion
  200.2 0.9 add_convert_fusion
  201.5 0.8 fusion.32
  203.5 2.9 fusion
  206.4 4.4 %all-to-all-start.6 = ((bf16[16,2,8,3072]{3,2,1,0:T(8,128)(2,1)}), bf16[16,2,8,3072]{3,2,1,0:T(8,128)(2,1)}, u32[]{:S(2)}, u32[]{:S(2)}) async-start(bf16[16,2,8,3072]{3,2,1,0:T(8,128)(2,1)} %bitcast.191), calls=%async_computation.6 | async-start | bytes 3145728 | tf_op jit(solution)/shard_map/all_to_all | solution.py:87
  211.0 50.2 %all-gather.5.cloned.1.call-done = bf16[64,8,3072]{2,1,0:T(8,128)(2,1)} async-done(((bf16[4,8,3072]{2,1,0:T(8,128)(2,1)}), bf16[64,8,3072]{2,1,0:T(8,128)(2,1)}) %all-gather.5.cloned.1.call-update) | async-done | bytes 3145744 | tf_op jit(solution)/shard_map/all_gather | solution.py:226
  261.2 5.9 %fusion.129 = (bf16[64,4,3072]{2,1,0:T(4,128)(2,1)}, bf16[64,4,3072]{2,1,0:T(4,128)(2,1)}) fusion(bf16[64,8,3072]{2,1,0:T(8,128)(2,1)} %all-gather.5.cloned.1.call-done), kind=kLoop, calls=%fused_computation.229 | loop fusion | bytes 6291456 | tf_op jit(solution)/shard_map/slice | solution.py:234
  267.1 3.7 %reshape.841 = bf16[256,3072]{1,0:T(8,128)(2,1)} reshape(bf16[64,4,3072]{2,1,0:T(4,128)(2,1)} %get-tuple-element.27) | data formatting | bytes 3145728 | tf_op jit(solution)/shard_map/reshape | solution.py:234
  270.8 5.3 %convolution_convert_fusion.1 = bf16[256,3072]{1,0:T(8,128)(2,1)} fusion(bf16[384,3072]{1,0:T(8,128)(2,1)S(1)} %copy-done, bf16[256,3072]{1,0:T(8,128)(2,1)} %reshape.841, bf16[3072,384]{1,0:T(8,128)(2,1)} %param.33), kind=kOutput, calls=%fused_computation.6 | convolution fusion | flops 1209630720 | bytes 7864320 | tf_op jit(solution)/shard_map/dot_general | solution.py:237
  276.1 3.9 %convert_element_type.224 = bf16[16,4,4,3072]{3,2,1,0:T(4,128)(2,1)} reshape(bf16[256,3072]{1,0:T(8,128)(2,1)} %convolution_convert_fusion.1) | data formatting | bytes 3145728 | tf_op jit(solution)/shard_map/convert_element_type | solution.py:86
  280.0 4.5 %all-to-all-start.5 = ((bf16[16,4,4,3072]{3,2,1,0:T(4,128)(2,1)}), bf16[16,4,4,3072]{3,2,1,0:T(4,128)(2,1)}, u32[]{:S(2)}, u32[]{:S(2)}) async-start(bf16[16,4,4,3072]{3,2,1,0:T(4,128)(2,1)} %convert_element_type.224), calls=%async_computation.5 | async-start | bytes 3145728 | tf_op jit(solution)/shard_map/all_to_all | solution.py:87
  284.6 1.0 slice_bitcast_fusion.10
  285.6 3.7 %reshape.840 = bf16[256,3072]{1,0:T(8,128)(2,1)} reshape(bf16[64,4,3072]{2,1,0:T(4,128)(2,1)} %get-tuple-element.26) | data formatting | bytes 3145728 | tf_op jit(solution)/shard_map/reshape | solution.py:234
  289.3 5.3 %convolution_convert_fusion.2 = bf16[256,3072]{1,0:T(8,128)(2,1)} fusion(bf16[384,3072]{1,0:T(8,128)(2,1)S(1)} %copy-done, bf16[256,3072]{1,0:T(8,128)(2,1)} %reshape.840, bf16[3072,384]{1,0:T(8,128)(2,1)} %param.33), kind=kOutput, calls=%fused_computation.7 | convolution fusion | flops 1209630720 | bytes 7864320 | tf_op jit(solution)/shard_map/dot_general | solution.py:237
  294.6 3.8 %convert_element_type.218 = bf16[16,4,4,3072]{3,2,1,0:T(4,128)(2,1)} reshape(bf16[256,3072]{1,0:T(8,128)(2,1)} %convolution_convert_fusion.2) | data formatting | bytes 3145728 | tf_op jit(solution)/shard_map/convert_element_type | solution.py:86
  298.5 10.3 %all-to-all-done.5 = bf16[16,4,4,3072]{3,2,1,0:T(4,128)(2,1)} async-done(((bf16[16,4,4,3072]{3,2,1,0:T(4,128)(2,1)}), bf16[16,4,4,3072]{3,2,1,0:T(4,128)(2,1)}, u32[]{:S(2)}, u32[]{:S(2)}) %all-to-all-start.5) | async-done | bytes 1572896 | tf_op jit(solution)/shard_map/all_to_all | solution.py:87
  308.8 4.6 %all-to-all-start.4 = ((bf16[16,4,4,3072]{3,2,1,0:T(4,128)(2,1)}), bf16[16,4,4,3072]{3,2,1,0:T(4,128)(2,1)}, u32[]{:S(2)}, u32[]{:S(2)}) async-start(bf16[16,4,4,3072]{3,2,1,0:T(4,128)(2,1)} %convert_element_type.218), calls=%async_computation.4 | async-start | bytes 3145728 | tf_op jit(solution)/shard_map/all_to_all | solution.py:87
  313.5 1.6 convert_reduce_fusion.1
  315.2 0.7 copy.86
  315.9 2.1 convert_reduce_fusion.2
  318.0 17.4 %all-to-all-done.4 = bf16[16,4,4,3072]{3,2,1,0:T(4,128)(2,1)} async-done(((bf16[16,4,4,3072]{3,2,1,0:T(4,128)(2,1)}), bf16[16,4,4,3072]{3,2,1,0:T(4,128)(2,1)}, u32[]{:S(2)}, u32[]{:S(2)}) %all-to-all-start.4) | async-done | bytes 1572896 | tf_op jit(solution)/shard_map/all_to_all | solution.py:87
  335.4 2.1 convert_reduce_fusion.3
  338.2 1.3 fusion.51
  339.5 1.3 fusion.49
  341.0 1.9 collective-permute-start
  343.0 3.6 %collective-permute-start.1 = (f32[8,1,128]{2,1,0:T(1,128)S(1)}, f32[8,1,128]{2,1,0:T(1,128)S(1)}, u32[]{:S(2)}, u32[]{:S(2)}) collective-permute-start(f32[8,1,128]{2,1,0:T(1,128)S(1)} %get-tuple-element.61), channel_id=1, source_target_pairs={{16,0},{32,16},{48,32},{64,48},{80,64},{96,80},{112,96},{128,112},... | collective-permute-start | bytes 12296 | tf_op jit(solution)/shard_map/ppermute | solution.py:25
  346.7 0.9 copy.85
  (117 shorter events, 8.3 us)
Async XLA Ops:
  7.2 263.7 %copy-start = (bf16[384,3072]{1,0:T(8,128)(2,1)S(1)}, bf16[384,3072]{1,0:T(8,128)(2,1)}, u32[]{:S(2)}) copy-start(bf16[384,3072]{1,0:T(8,128)(2,1)} %param.34) | copy-start | bytes 7077892
  7.2 4.0 %copy-start.1 = (bf16[8,2,3072]{2,1,0:T(2,128)(2,1)S(1)}, bf16[8,2,3072]{2,1,0:T(2,128)(2,1)}, u32[]{:S(2)}) copy-start(bf16[8,2,3072]{2,1,0:T(2,128)(2,1)} %param.19) | copy-start | bytes 294916
  7.2 4.4 %copy-start.8 = (f32[8,3,3072]{2,0,1:T(8,128)S(1)}, f32[8,3,3072]{2,0,1:T(8,128)}, u32[]{:S(2)}) copy-start(f32[8,3,3072]{2,0,1:T(8,128)} %param.25) | copy-start | bytes 884740
  7.2 69.6 %all-gather.3.cloned.1.call-start = ((), (), s32[]{:S(2)}) async-start(), calls=%async_computation.7 | async-start | bytes 3342336 | tf_op jit(solution)/shard_map/all_gather | solution.py:128
  13.6 34.4 %all-to-all-start = ((bf16[16,2,8,3072]{3,2,1,0:T(8,128)(2,1)}), bf16[16,2,8,3072]{3,2,1,0:T(8,128)(2,1)}, u32[]{:S(2)}, u32[]{:S(2)}) async-start(bf16[16,2,8,3072]{3,2,1,0:T(8,128)(2,1)} %broadcast_in_dim.42), calls=%async_computation | async-start | bytes 3145728 | tf_op jit(solution)/shard_map/all_to_all | solution.py:131
  20.7 4.3 %copy-start.17 = (s32[8,2]{0,1:T(2,128)S(1)}, s32[8,2]{0,1:T(2,128)}, u32[]{:S(2)}) copy-start(s32[8,2]{0,1:T(2,128)} %param.22) | copy-start | bytes 196
  26.5 6.6 %copy-start.16 = (f32[2,2,128]{2,1,0:T(2,128)S(1)}, f32[2,2,128]{2,1,0:T(2,128)}, u32[]{:S(2)}) copy-start(f32[2,2,128]{2,1,0:T(2,128)} %param.32) | copy-start | bytes 6148
  86.0 0.8 copy-start.13
  86.0 0.8 copy-start.14
  86.1 0.8 copy-start.18
  86.1 0.8 copy-start.19
  86.1 0.7 copy-start.20
  86.1 0.7 copy-start.21
  86.1 0.7 copy-start.22
  86.1 0.7 copy-start.23
  86.3 1.9 copy-start.11
  86.5 1.7 copy-start.10
  86.5 1.8 copy-start.9
  88.5 8.6 %copy-start.24 = (s32[8]{0:T(128)S(1)}, s32[8]{0:T(128)}, u32[]{:S(2)}) copy-start(s32[8]{0:T(128)} %param.23) | copy-start | bytes 100
  89.6 30.9 %all-to-all-start.1 = ((bf16[16,240,1,128]{3,1,2,0:T(8,128)(2,1)}), bf16[16,240,1,128]{3,1,2,0:T(8,128)(2,1)}, u32[]{:S(2)}, u32[]{:S(2)}) async-start(bf16[16,240,1,128]{3,1,2,0:T(8,128)(2,1)} %pad_maximum_fusion), calls=%async_computation.1 | async-start | bytes 1966080 | tf_op jit(solution)/shard_map/all_to_all | solution.py:181
  124.7 16.0 %copy-start.3 = (bf16[128,3072]{1,0:T(8,128)(2,1)S(1)}, bf16[128,3072]{1,0:T(8,128)(2,1)}, u32[]{:S(2)}) copy-start(bf16[128,3072]{1,0:T(8,128)(2,1)} %param.30) | copy-start | bytes 2359300
  143.3 4.9 %copy-start.7 = (f32[8,3,3072]{2,0,1:T(8,128)S(1)}, f32[8,3,3072]{2,0,1:T(8,128)}, u32[]{:S(2)}) copy-start(f32[8,3,3072]{2,0,1:T(8,128)} %param.26) | copy-start | bytes 884740
  143.3 54.4 %all-to-all-start.3 = ((bf16[16,4,8,3072]{3,2,1,0:T(8,128)(2,1)}), bf16[16,4,8,3072]{3,2,1,0:T(8,128)(2,1)}, u32[]{:S(2)}, u32[]{:S(2)}) async-start(bf16[16,4,8,3072]{3,2,1,0:T(8,128)(2,1)} %bitcast.188), calls=%async_computation.3 | async-start | bytes 6291456 | tf_op jit(solution)/shard_map/all_to_all | solution.py:87
  148.0 113.2 %all-gather.5.cloned.1.call-start = ((), (), s32[]{:S(2)}) async-start(), calls=%async_computation.8 | async-start | bytes 3342336 | tf_op jit(solution)/shard_map/all_gather | solution.py:226
  197.7 3.8 %copy-start.4 = (f32[8,3072]{1,0:T(8,128)S(1)}, f32[8,3072]{1,0:T(8,128)}, u32[]{:S(2)}) copy-start(f32[8,3072]{1,0:T(8,128)} %get-tuple-element.39) | copy-start | bytes 294916
  197.7 3.8 %copy-start.5 = (f32[8,3072]{1,0:T(8,128)S(1)}, f32[8,3072]{1,0:T(8,128)}, u32[]{:S(2)}) copy-start(f32[8,3072]{1,0:T(8,128)} %get-tuple-element.40) | copy-start | bytes 294916
  203.5 7.3 %copy-start.12 = (f32[8,2,3072]{2,1,0:T(2,128)S(1)}, f32[8,2,3072]{2,1,0:T(2,128)}, u32[]{:S(2)}) copy-start(f32[8,2,3072]{2,1,0:T(2,128)} %param.27) | copy-start | bytes 589828
  206.4 73.6 %all-to-all-start.6 = ((bf16[16,2,8,3072]{3,2,1,0:T(8,128)(2,1)}), bf16[16,2,8,3072]{3,2,1,0:T(8,128)(2,1)}, u32[]{:S(2)}, u32[]{:S(2)}) async-start(bf16[16,2,8,3072]{3,2,1,0:T(8,128)(2,1)} %bitcast.191), calls=%async_computation.6 | async-start | bytes 3145728 | tf_op jit(solution)/shard_map/all_to_all | solution.py:87
  280.0 28.7 %all-to-all-start.5 = ((bf16[16,4,4,3072]{3,2,1,0:T(4,128)(2,1)}), bf16[16,4,4,3072]{3,2,1,0:T(4,128)(2,1)}, u32[]{:S(2)}, u32[]{:S(2)}) async-start(bf16[16,4,4,3072]{3,2,1,0:T(4,128)(2,1)} %convert_element_type.224), calls=%async_computation.5 | async-start | bytes 3145728 | tf_op jit(solution)/shard_map/all_to_all | solution.py:87
  298.5 15.0 %copy-start.25 = (s32[8]{0:T(128)S(1)}, s32[8]{0:T(128)}, u32[]{:S(2)}) copy-start(s32[8]{0:T(128)} %param.21) | copy-start | bytes 100
  298.5 16.6 %copy-start.2 = (bf16[8,2,3072]{2,1,0:T(2,128)(2,1)S(1)}, bf16[8,2,3072]{2,1,0:T(2,128)(2,1)}, u32[]{:S(2)}) copy-start(bf16[8,2,3072]{2,1,0:T(2,128)(2,1)} %param.19) | copy-start | bytes 294916
  298.5 16.6 %copy-start.6 = (f32[8,3072]{1,0:T(8,128)S(1)}, f32[8,3072]{1,0:T(8,128)}, u32[]{:S(2)}) copy-start(f32[8,3072]{1,0:T(8,128)} %get-tuple-element.34) | copy-start | bytes 294916
  308.8 26.6 %all-to-all-start.4 = ((bf16[16,4,4,3072]{3,2,1,0:T(4,128)(2,1)}), bf16[16,4,4,3072]{3,2,1,0:T(4,128)(2,1)}, u32[]{:S(2)}, u32[]{:S(2)}) async-start(bf16[16,4,4,3072]{3,2,1,0:T(4,128)(2,1)} %convert_element_type.218), calls=%async_computation.4 | async-start | bytes 3145728 | tf_op jit(solution)/shard_map/all_to_all | solution.py:87
  318.0 23.0 %copy-start.15 = (f32[8,2,128]{2,1,0:T(2,128)S(1)}, f32[8,2,128]{2,1,0:T(2,128)}, u32[]{:S(2)}) copy-start(f32[8,2,128]{2,1,0:T(2,128)} %param.20) | copy-start | bytes 24580
  341.0 6.6 %collective-permute-start = (f32[8,1,128]{2,1,0:T(1,128)S(1)}, f32[8,1,128]{2,1,0:T(1,128)S(1)}, u32[]{:S(2)}, u32[]{:S(2)}) collective-permute-start(f32[8,1,128]{2,1,0:T(1,128)S(1)} %get-tuple-element.60), channel_id=1, source_target_pairs={{0,16},{16,32},{32,48},{48,64},{64,80},{80,96},{96,112},{112,128},... | collective-permute-start | bytes 12296 | tf_op jit(solution)/shard_map/ppermute | solution.py:24
  343.0 5.0 %collective-permute-start.1 = (f32[8,1,128]{2,1,0:T(1,128)S(1)}, f32[8,1,128]{2,1,0:T(1,128)S(1)}, u32[]{:S(2)}, u32[]{:S(2)}) collective-permute-start(f32[8,1,128]{2,1,0:T(1,128)S(1)} %get-tuple-element.61), channel_id=1, source_target_pairs={{16,0},{32,16},{48,32},{64,48},{80,64},{96,80},{112,96},{128,112},... | collective-permute-start | bytes 12296 | tf_op jit(solution)/shard_map/ppermute | solution.py:25
Sparse Core Ops, SparseCore 0:
  11.3 65.3 all-gather.2
  202.5 58.6 all-gather.4

commit v9 on v7

--- a/solution.py
+++ b/solution.py
@@ -126,8 +126,8 @@
     text_tile = owners * own_text
     block_len = text_tile + image_count
     joined = jnp.concatenate([image_mod_own, text_mod_own], 0)
-    gathered = lax.all_to_all(
-        jnp.broadcast_to(joined[None], (owners,) + joined.shape), "tensor", 0, 0, tiled=True
+    gathered = lax.all_gather(joined, "tensor", axis=0, tiled=True).reshape(
+        owners, slots, requests, model_width
     )
     image_mod = gathered[:, :own_image].reshape(image_count * requests, model_width)
     text_mod = gathered[:, own_image:].reshape(text_tile * requests, model_width)
@@ -222,9 +222,7 @@
         jnp.bfloat16
     )
     mlp_mod = modulate(image_mid, mod_mlp[None, :, 0, :], mod_mlp[None, :, 1, :])
-    piece = lax.all_to_all(
-        jnp.broadcast_to(mlp_mod[None], (owners,) + mlp_mod.shape), "tensor", 0, 0, tiled=True
-    ).reshape(image_count, requests, model_width)
+    piece = lax.all_gather(mlp_mod, "tensor", axis=0, tiled=True)
     grown = jnp.dot(piece.reshape(-1, model_width), mlp_expand, preferred_element_type=jnp.float32)
     activated = jax.nn.gelu(grown, approximate=True).astype(jnp.bfloat16)
     text_out = (text_own.astype(jnp.float32) + mod_text[None, :, 2, :] * text_sum).astype(

time: 363 us -> 351 us (0.967)
  between operations: 1.9 us -> 15.3 us
  starting transfers between devices: 41.3 us -> 27.9 us
  waiting for transfers between devices: 223 us -> 212 us
    all_to_all x2 -> x0, waiting for transfers between devices: 100 us -> none  [the longest x1 57.9 us: per_device(): lax.all_to_all(jnp.broadcast_to(joined[None], (owners,) + joined.shape),...]
    all_gather x0 -> x2, waiting for transfers between devices: none -> 98.9 us  [the longest x1 50.1 us: per_device(): piece = lax.all_gather(mlp_mod, 'tensor', axis=0, tiled=True)]
    all_to_all x2 -> x0, starting transfers between devices: 11.6 us -> none  [the longest x1 7.08 us: per_device(): lax.all_to_all(jnp.broadcast_to(joined[None], (owners,) + joined.shape),...]
    all_to_all x3, waiting for transfers between devices: 100 us -> 91 us  [sum_over_tensor(): parts = lax.all_to_all(parts, 'tensor', 0, 0, tiled=True)]
    broadcast_in_dim x2 -> x0, local copies, waits for them, and re-layouts: 4.79 us -> none  [the longest x1 2.77 us: per_device(): jnp.broadcast_to(joined[None], (owners,) + joined.shape)]
    unnamed x63 -> x66, local copies, waits for them, and re-layouts: 10.6 us -> 11.9 us
  transfers between devices with their start and end apart: 8 -> 8, of which waited for: 6 -> 5; matrix products, arithmetic and copies ran while one was open for 9% -> 9% of each run, Pallas kernels for 0% -> 0%
where the time goes in v9:
time: 351 us; the launch traced here: 347 us
  waiting for transfers between devices  212 us (60%)
  local copies, waits for them, and re-layouts  28.8 us (8%)
  other arithmetic  28 us (8%)
  starting transfers between devices  27.9 us (8%)
  matrix products  19.3 us (5%)
  between operations  15.3 us (4%)
  blocking collectives  15 us (4%)
    all_to_all x3, waiting for transfers between devices, sum_over_tensor(): parts = lax.all_to_all(parts, 'tensor', 0, 0, tiled=True)  91 us
    all_gather x1, waiting for transfers between devices, per_device(): piece = lax.all_gather(mlp_mod, 'tensor', axis=0, tiled=True)  50.1 us
    all_gather x1, waiting for transfers between devices, per_device(): lax.all_gather(joined, 'tensor', axis=0, tiled=True)  48.8 us
    all_to_all x1, waiting for transfers between devices, per_device(): incoming = lax.all_to_all(outgoing, 'tile', 0, 0, tiled=True)  22.2 us
    all_to_all x1, blocking collectives, per_device(): returned = lax.all_to_all(attended_mine, 'tile', 0, 0, tiled=True)  15 us
    all_to_all x3, starting transfers between devices, sum_over_tensor(): parts = lax.all_to_all(parts, 'tensor', 0, 0, tiled=True)  14.6 us
    unnamed x66, local copies, waits for them, and re-layouts  11.9 us
    dot_general x1, matrix products, per_device(): jnp.dot(activated, mlp_reduce, preferred_element_type=jnp.float32)  7.79 us
  transfers between devices with their start and end apart: 8, of which 5 were waited for; matrix products, arithmetic and copies ran while one was open for 9% of the time, Pallas kernels for 0%

profile of v9, /device:TPU:32, one launch (start us, length us, event | category | flops | bytes accessed | tf_op | source)
XLA Modules:
  0.0 346.6 jit_solution(9819320041231795306)
XLA Ops:
  7.2 1.2 fusion.68
  8.4 1.1 fusion.71
  9.5 1.6 slice_bitcast_fusion.9
  11.1 1.6 slice_bitcast_fusion.4
  12.8 1.0 copy.79
  14.1 1.0 fusion.74
  15.2 0.7 pad_maximum_fusion.1
  16.1 0.7 copy.87
  16.8 0.7 copy.86
  17.5 4.3 %copy.82 = bf16[3072,3,128]{0,2,1:T(8,128)(2,1)} copy(bf16[3072,3,128]{2,0,1:T(8,128)(2,1)} %param.28) | data formatting | bytes 4718592 | tf_op args[10]
  21.8 4.3 %copy.81 = bf16[3072,3,128]{0,2,1:T(8,128)(2,1)} copy(bf16[3072,3,128]{2,0,1:T(8,128)(2,1)} %param.29) | data formatting | bytes 4718592 | tf_op args[11]
  26.1 0.6 and_select_fusion.2
  26.7 0.5 compare_and_fusion
  27.3 0.5 iota_and_fusion
  27.8 0.6 compare_select_fusion
  28.4 0.6 slice_bitcast_fusion.14
  29.0 48.8 %all-gather.3.cloned.1.call-done = bf16[96,8,3072]{2,1,0:T(8,128)(2,1)} async-done(((bf16[6,8,3072]{2,1,0:T(8,128)(2,1)}), bf16[96,8,3072]{2,1,0:T(8,128)(2,1)}) %all-gather.3.cloned.1.call-update) | async-done | bytes 4718608 | tf_op jit(solution)/shard_map/all_gather | solution.py:129
  77.8 2.7 slice.170
  80.5 2.3 slice.172
  83.1 1.8 fusion.12
  84.9 0.8 multiply_reduce_fusion.2
  85.7 0.7 fusion.85
  86.4 0.8 copy.84
  87.2 0.8 copy.90
  88.1 0.7 copy.91
  88.8 0.7 copy.85
  89.5 1.1 multiply_multiply_fusion.2
  91.7 1.0 fusion.15
  93.1 1.4 fusion.62
  94.8 1.0 pad_maximum_fusion
  95.9 7.5 %all-to-all-start = ((bf16[16,240,1,128]{3,1,2,0:T(8,128)(2,1)}), bf16[16,240,1,128]{3,1,2,0:T(8,128)(2,1)}, u32[]{:S(2)}, u32[]{:S(2)}) async-start(bf16[16,240,1,128]{3,1,2,0:T(8,128)(2,1)} %pad_maximum_fusion), calls=%async_computation | async-start | bytes 1966080 | tf_op jit(solution)/shard_map/all_to_all | solution.py:180
  103.4 0.6 dynamic_slice.3
  104.0 0.7 fusion.97
  104.6 22.2 %all-to-all-done = bf16[16,240,1,128]{3,1,2,0:T(8,128)(2,1)} async-done(((bf16[16,240,1,128]{3,1,2,0:T(8,128)(2,1)}), bf16[16,240,1,128]{3,1,2,0:T(8,128)(2,1)}, u32[]{:S(2)}, u32[]{:S(2)}) %all-to-all-start) | async-done | bytes 983072 | tf_op jit(solution)/shard_map/all_to_all | solution.py:180
  126.8 0.9 slice.186
  127.8 1.2 fusion.107
  129.0 0.9 select_reduce_fusion
  129.8 1.1 fusion.1
  130.9 0.9 fusion.21
  131.9 15.0 %all_to_all.25 = bf16[16,48,128]{2,1,0:T(8,128)(2,1)S(1)} all-to-all(bf16[16,48,128]{2,1,0:T(8,128)(2,1)S(1)} %bitcast.215), channel_id=1, replica_groups=mesh['tile'=16,'tensor'=16] {'tile'}, dimensions={0} | all-to-all | bytes 393216 | tf_op jit(solution)/shard_map/all_to_all | solution.py:208
  146.9 0.7 copy-done.7
  147.6 2.7 convolution_convert_fusion
  150.2 5.4 %all-to-all-start.2 = ((bf16[16,4,8,3072]{3,2,1,0:T(8,128)(2,1)}), bf16[16,4,8,3072]{3,2,1,0:T(8,128)(2,1)}, u32[]{:S(2)}, u32[]{:S(2)}) async-start(bf16[16,4,8,3072]{3,2,1,0:T(8,128)(2,1)} %bitcast.199), calls=%async_computation.2 | async-start | bytes 6291456 | tf_op jit(solution)/shard_map/all_to_all | solution.py:87
  155.9 0.7 slice_bitcast_fusion.6
  156.6 48.3 %all-to-all-done.2 = bf16[16,4,8,3072]{3,2,1,0:T(8,128)(2,1)} async-done(((bf16[16,4,8,3072]{3,2,1,0:T(8,128)(2,1)}), bf16[16,4,8,3072]{3,2,1,0:T(8,128)(2,1)}, u32[]{:S(2)}, u32[]{:S(2)}) %all-to-all-start.2) | async-done | bytes 3145760 | tf_op jit(solution)/shard_map/all_to_all | solution.py:87
  204.9 2.5 convert_reduce_fusion.1
  207.9 0.8 fusion.47
  209.9 3.0 fusion
  212.9 4.5 %all-to-all-start.4 = ((bf16[16,2,8,3072]{3,2,1,0:T(8,128)(2,1)}), bf16[16,2,8,3072]{3,2,1,0:T(8,128)(2,1)}, u32[]{:S(2)}, u32[]{:S(2)}) async-start(bf16[16,2,8,3072]{3,2,1,0:T(8,128)(2,1)} %bitcast.200), calls=%async_computation.4 | async-start | bytes 3145728 | tf_op jit(solution)/shard_map/all_to_all | solution.py:87
  217.4 50.1 %all-gather.5.cloned.1.call-done = bf16[64,8,3072]{2,1,0:T(8,128)(2,1)} async-done(((bf16[4,8,3072]{2,1,0:T(8,128)(2,1)}), bf16[64,8,3072]{2,1,0:T(8,128)(2,1)}) %all-gather.5.cloned.1.call-update) | async-done | bytes 3145744 | tf_op jit(solution)/shard_map/all_gather | solution.py:225
  267.5 7.8 %convolution_convert_fusion.1 = bf16[512,3072]{1,0:T(8,128)(2,1)} fusion(bf16[384,3072]{1,0:T(8,128)(2,1)S(1)} %copy-done, bf16[3072,384]{1,0:T(8,128)(2,1)} %param.33, bf16[64,8,3072]{2,1,0:T(8,128)(2,1)} %all-gather.5.cloned.1.call-done), kind=kOutput, calls=%fused_computation.5 | convolution fusion | flops 2419261440 | bytes 11010048 | tf_op jit(solution)/shard_map/dot_general | solution.py:231
  275.3 4.7 %all-to-all-start.3 = ((bf16[16,4,8,3072]{3,2,1,0:T(8,128)(2,1)}), bf16[16,4,8,3072]{3,2,1,0:T(8,128)(2,1)}, u32[]{:S(2)}, u32[]{:S(2)}) async-start(bf16[16,4,8,3072]{3,2,1,0:T(8,128)(2,1)} %bitcast.203), calls=%async_computation.3 | async-start | bytes 6291456 | tf_op jit(solution)/shard_map/all_to_all | solution.py:87
  280.0 1.2 fusion.112
  281.2 0.7 copy_bitcast_fusion
  282.0 1.6 convert_reduce_fusion.2
  283.7 0.7 copy.99
  284.4 42.8 %all-to-all-done.3 = bf16[16,4,8,3072]{3,2,1,0:T(8,128)(2,1)} async-done(((bf16[16,4,8,3072]{3,2,1,0:T(8,128)(2,1)}), bf16[16,4,8,3072]{3,2,1,0:T(8,128)(2,1)}, u32[]{:S(2)}, u32[]{:S(2)}) %all-to-all-start.3) | async-done | bytes 3145760 | tf_op jit(solution)/shard_map/all_to_all | solution.py:87
  327.2 2.5 convert_reduce_fusion
  330.1 1.3 convolution_bitcast_fusion
  331.6 1.9 collective-permute-start
  333.5 3.6 %collective-permute-start.1 = (f32[8,1,128]{2,1,0:T(1,128)S(1)}, f32[8,1,128]{2,1,0:T(1,128)S(1)}, u32[]{:S(2)}, u32[]{:S(2)}) collective-permute-start(f32[8,1,128]{2,1,0:T(1,128)S(1)} %get-tuple-element.46), channel_id=1, source_target_pairs={{16,0},{32,16},{48,32},{64,48},{80,64},{96,80},{112,96},{128,112},... | collective-permute-start | bytes 12296 | tf_op jit(solution)/shard_map/ppermute | solution.py:25
  337.2 1.1 fusion.54
  338.2 0.9 copy.98
  339.1 0.6 pad_maximum_fusion.2
  (111 shorter events, 4.4 us)
Async XLA Ops:
  7.2 260.3 %copy-start = (bf16[384,3072]{1,0:T(8,128)(2,1)S(1)}, bf16[384,3072]{1,0:T(8,128)(2,1)}, u32[]{:S(2)}) copy-start(bf16[384,3072]{1,0:T(8,128)(2,1)} %param.34) | copy-start | bytes 7077892
  7.2 8.8 %copy-start.22 = (s32[8,2]{0,1:T(2,128)S(1)}, s32[8,2]{0,1:T(2,128)}, u32[]{:S(2)}) copy-start(s32[8,2]{0,1:T(2,128)} %param.22) | copy-start | bytes 196
  7.2 70.6 %all-gather.3.cloned.1.call-start = ((), (), s32[]{:S(2)}) async-start(), calls=%async_computation.5 | async-start | bytes 5013504 | tf_op jit(solution)/shard_map/all_gather | solution.py:129
  21.8 6.6 %copy-start.21 = (f32[2,2,128]{2,1,0:T(2,128)S(1)}, f32[2,2,128]{2,1,0:T(2,128)}, u32[]{:S(2)}) copy-start(f32[2,2,128]{2,1,0:T(2,128)} %param.32) | copy-start | bytes 6148
  80.5 2.6 copy-start.3
  89.5 1.7 copy-start.2
  89.5 2.2 copy-start.4
  91.6 1.3 copy-start.19
  91.6 1.3 copy-start.20
  91.6 1.4 copy-start.16
  91.6 1.4 copy-start.17
  91.6 1.4 copy-start.23
  91.7 1.4 copy-start.24
  91.7 1.4 copy-start.25
  91.7 1.4 copy-start.26
  91.7 1.4 copy-start.27
  91.7 1.4 copy-start.28
  92.7 1.9 copy-start.9
  94.6 8.8 %copy-start.29 = (s32[8]{0:T(128)S(1)}, s32[8]{0:T(128)}, u32[]{:S(2)}) copy-start(s32[8]{0:T(128)} %param.23) | copy-start | bytes 100
  95.9 31.0 %all-to-all-start = ((bf16[16,240,1,128]{3,1,2,0:T(8,128)(2,1)}), bf16[16,240,1,128]{3,1,2,0:T(8,128)(2,1)}, u32[]{:S(2)}, u32[]{:S(2)}) async-start(bf16[16,240,1,128]{3,1,2,0:T(8,128)(2,1)} %pad_maximum_fusion), calls=%async_computation | async-start | bytes 1966080 | tf_op jit(solution)/shard_map/all_to_all | solution.py:180
  130.9 16.7 %copy-start.8 = (bf16[128,3072]{1,0:T(8,128)(2,1)S(1)}, bf16[128,3072]{1,0:T(8,128)(2,1)}, u32[]{:S(2)}) copy-start(bf16[128,3072]{1,0:T(8,128)(2,1)} %param.30) | copy-start | bytes 2359300
  146.9 0.7 copy-start.7
  150.2 5.7 %copy-start.15 = (f32[8,3,3072]{2,0,1:T(8,128)S(1)}, f32[8,3,3072]{2,0,1:T(8,128)}, u32[]{:S(2)}) copy-start(f32[8,3,3072]{2,0,1:T(8,128)} %param.26) | copy-start | bytes 884740
  150.2 54.7 %all-to-all-start.2 = ((bf16[16,4,8,3072]{3,2,1,0:T(8,128)(2,1)}), bf16[16,4,8,3072]{3,2,1,0:T(8,128)(2,1)}, u32[]{:S(2)}, u32[]{:S(2)}) async-start(bf16[16,4,8,3072]{3,2,1,0:T(8,128)(2,1)} %bitcast.199), calls=%async_computation.2 | async-start | bytes 6291456 | tf_op jit(solution)/shard_map/all_to_all | solution.py:87
  155.7 51.8 %copy-start.6 = (f32[8,3072]{1,0:T(8,128)S(1)}, f32[8,3072]{1,0:T(8,128)}, u32[]{:S(2)}) copy-start(f32[8,3072]{1,0:T(8,128)} %get-tuple-element.30) | copy-start | bytes 294916
  155.7 111.8 %all-gather.5.cloned.1.call-start = ((), (), s32[]{:S(2)}) async-start(), calls=%async_computation.6 | async-start | bytes 3342336 | tf_op jit(solution)/shard_map/all_gather | solution.py:225
  204.9 3.0 copy-start.10
  204.9 3.0 copy-start.11
  207.4 5.4 %copy-start.1 = (f32[4,8,3072]{2,1,0:T(8,128)}, f32[4,8,3072]{2,1,0:T(8,128)S(1)}, u32[]{:S(2)}) copy-start(f32[4,8,3072]{2,1,0:T(8,128)S(1)} %convert_reduce_fusion.1) | copy-start | bytes 1179652
  212.9 62.4 %all-to-all-start.4 = ((bf16[16,2,8,3072]{3,2,1,0:T(8,128)(2,1)}), bf16[16,2,8,3072]{3,2,1,0:T(8,128)(2,1)}, u32[]{:S(2)}, u32[]{:S(2)}) async-start(bf16[16,2,8,3072]{3,2,1,0:T(8,128)(2,1)} %bitcast.200), calls=%async_computation.4 | async-start | bytes 3145728 | tf_op jit(solution)/shard_map/all_to_all | solution.py:87
  275.3 4.7 %copy-start.30 = (s32[8]{0:T(128)S(1)}, s32[8]{0:T(128)}, u32[]{:S(2)}) copy-start(s32[8]{0:T(128)} %param.21) | copy-start | bytes 100
  275.3 8.3 %copy-start.5 = (bf16[8,2,3072]{2,1,0:T(2,128)(2,1)S(1)}, bf16[8,2,3072]{2,1,0:T(2,128)(2,1)}, u32[]{:S(2)}) copy-start(bf16[8,2,3072]{2,1,0:T(2,128)(2,1)} %param.19) | copy-start | bytes 294916
  275.3 8.3 %copy-start.14 = (f32[8,3072]{1,0:T(8,128)S(1)}, f32[8,3072]{1,0:T(8,128)}, u32[]{:S(2)}) copy-start(f32[8,3072]{1,0:T(8,128)} %get-tuple-element.24) | copy-start | bytes 294916
  275.3 51.8 %all-to-all-start.3 = ((bf16[16,4,8,3072]{3,2,1,0:T(8,128)(2,1)}), bf16[16,4,8,3072]{3,2,1,0:T(8,128)(2,1)}, u32[]{:S(2)}, u32[]{:S(2)}) async-start(bf16[16,4,8,3072]{3,2,1,0:T(8,128)(2,1)} %bitcast.203), calls=%async_computation.3 | async-start | bytes 6291456 | tf_op jit(solution)/shard_map/all_to_all | solution.py:87
  283.6 47.9 %copy-start.18 = (f32[8,2,128]{2,1,0:T(2,128)S(1)}, f32[8,2,128]{2,1,0:T(2,128)}, u32[]{:S(2)}) copy-start(f32[8,2,128]{2,1,0:T(2,128)} %param.20) | copy-start | bytes 24580
  327.2 2.9 copy-start.12
  327.2 2.9 copy-start.13
  331.6 7.5 %collective-permute-start = (f32[8,1,128]{2,1,0:T(1,128)S(1)}, f32[8,1,128]{2,1,0:T(1,128)S(1)}, u32[]{:S(2)}, u32[]{:S(2)}) collective-permute-start(f32[8,1,128]{2,1,0:T(1,128)S(1)} %get-tuple-element.45), channel_id=1, source_target_pairs={{0,16},{16,32},{32,48},{48,64},{64,80},{80,96},{96,112},{112,128},... | collective-permute-start | bytes 12296 | tf_op jit(solution)/shard_map/ppermute | solution.py:24
  333.5 5.6 %collective-permute-start.1 = (f32[8,1,128]{2,1,0:T(1,128)S(1)}, f32[8,1,128]{2,1,0:T(1,128)S(1)}, u32[]{:S(2)}, u32[]{:S(2)}) collective-permute-start(f32[8,1,128]{2,1,0:T(1,128)S(1)} %get-tuple-element.46), channel_id=1, source_target_pairs={{16,0},{32,16},{48,32},{64,48},{80,64},{96,80},{112,96},{128,112},... | collective-permute-start | bytes 12296 | tf_op jit(solution)/shard_map/ppermute | solution.py:25
Sparse Core Ops, SparseCore 0:
  16.1 61.6 all-gather.2
  208.8 58.6 all-gather.4

commit v10 on v6

--- a/solution.py
+++ b/solution.py
@@ -217,8 +217,6 @@
     text_term = jnp.dot(text_att, proj_text, preferred_element_type=jnp.float32).reshape(
         text_tile, requests, model_width
     )
-    after_image = (image_sum[0, 0, 0] * 0.0).astype(text_term.dtype)
-    text_sum = sum_over_tensor(text_term + after_image, owners, NARROW_SUMS)
     image_mid = (image_own.astype(jnp.float32) + mod_image[None, :, 2, :] * image_sum).astype(
         jnp.bfloat16
     )
@@ -226,13 +224,15 @@
     piece = lax.all_gather(mlp_mod, "tensor", axis=0, tiled=True)
     grown = jnp.dot(piece.reshape(-1, model_width), mlp_expand, preferred_element_type=jnp.float32)
     activated = jax.nn.gelu(grown, approximate=True).astype(jnp.bfloat16)
+    mlp_term = jnp.dot(activated, mlp_reduce, preferred_element_type=jnp.float32).reshape(
+        image_count, requests, model_width
+    )
+    mlp_sum = sum_over_tensor(mlp_term, owners, NARROW_SUMS)
+    after_mlp = (mlp_sum[0, 0, 0] * 0.0).astype(text_term.dtype)
+    text_sum = sum_over_tensor(text_term + after_mlp, owners, NARROW_SUMS)
     text_out = (text_own.astype(jnp.float32) + mod_text[None, :, 2, :] * text_sum).astype(
         jnp.bfloat16
     )
-    mlp_term = jnp.dot(activated, mlp_reduce, preferred_element_type=jnp.float32).reshape(
-        image_count, requests, model_width
-    )
-    mlp_sum = sum_over_tensor(mlp_term, owners, NARROW_SUMS)
     image_out = (image_mid.astype(jnp.float32) + mod_mlp[None, :, 2, :] * mlp_sum).astype(
         jnp.bfloat16
     )

time: 345 us -> 357 us (1.035)
  waiting for transfers between devices: 202 us -> 216 us
    all_to_all x3, waiting for transfers between devices: 91.5 us -> 107 us  [sum_over_tensor(): parts = lax.all_to_all(parts, 'tensor', 0, 0, tiled=True)]
    unnamed x52 -> x50, local copies, waits for them, and re-layouts: 11 us -> 11.8 us
  transfers between devices with their start and end apart: 9 -> 9, of which waited for: 6 -> 7; matrix products, arithmetic and copies ran while one was open for 12% -> 8% of each run, Pallas kernels for 0% -> 0%
where the time goes in v10:
time: 357 us; the launch traced here: 356 us
  waiting for transfers between devices  216 us (61%)
  starting transfers between devices  34.3 us (10%)
  other arithmetic  28.5 us (8%)
  matrix products  23.8 us (7%)
  local copies, waits for them, and re-layouts  23.4 us (7%)
  between operations  15.2 us (4%)
  blocking collectives  15 us (4%)
    all_to_all x3, waiting for transfers between devices, sum_over_tensor(): parts = lax.all_to_all(parts, 'tensor', 0, 0, tiled=True)  107 us
    all_gather x1, waiting for transfers between devices, per_device(): piece = lax.all_gather(mlp_mod, 'tensor', axis=0, tiled=True)  48.5 us
    all_gather x1, waiting for transfers between devices, per_device(): lax.all_gather(image_mod_own, 'tensor', axis=0, tiled=True)  23.2 us
    all_to_all x1, waiting for transfers between devices, per_device(): incoming = lax.all_to_all(outgoing, 'tile', 0, 0, tiled=True)  22.2 us
    all_to_all x1, blocking collectives, per_device(): returned = lax.all_to_all(attended_mine, 'tile', 0, 0, tiled=True)  15 us
    all_to_all x1, waiting for transfers between devices, per_device(): lax.all_to_all(jnp.broadcast_to(text_mod_own[None], (owners,) + text_mod_...  14.9 us
    all_to_all x3, starting transfers between devices, sum_over_tensor(): parts = lax.all_to_all(parts, 'tensor', 0, 0, tiled=True)  13.9 us
    unnamed x50, local copies, waits for them, and re-layouts  11.8 us
  transfers between devices with their start and end apart: 9, of which 7 were waited for; matrix products, arithmetic and copies ran while one was open for 8% of the time, Pallas kernels for 0%

profile of v10, /device:TPU:32, one launch (start us, length us, event | category | flops | bytes accessed | tf_op | source)
XLA Modules:
  0.0 355.8 jit_solution(9018295076503622408)
XLA Ops:
  7.2 1.1 copy.77
  8.7 1.7 slice_bitcast_fusion.9
  10.4 0.8 add_convert_fusion.1
  11.2 1.0 fusion.71
  12.4 0.7 slice_bitcast_fusion.4
  13.2 1.3 broadcast_in_dim.42
  14.5 7.1 %all-to-all-start = ((bf16[16,2,8,3072]{3,2,1,0:T(8,128)(2,1)}), bf16[16,2,8,3072]{3,2,1,0:T(8,128)(2,1)}, u32[]{:S(2)}, u32[]{:S(2)}) async-start(bf16[16,2,8,3072]{3,2,1,0:T(8,128)(2,1)} %broadcast_in_dim.42), calls=%async_computation | async-start | bytes 3145728 | tf_op jit(solution)/shard_map/all_to_all | solution.py:131
  21.6 4.3 %copy.80 = bf16[3072,3,128]{0,2,1:T(8,128)(2,1)} copy(bf16[3072,3,128]{2,0,1:T(8,128)(2,1)} %param.28) | data formatting | bytes 4718592 | tf_op args[10]
  26.1 0.7 copy.84
  26.8 0.7 copy.85
  27.5 4.3 %copy.79 = bf16[3072,3,128]{0,2,1:T(8,128)(2,1)} copy(bf16[3072,3,128]{2,0,1:T(8,128)(2,1)} %param.29) | data formatting | bytes 4718592 | tf_op args[11]
  31.7 0.6 and_select_fusion.2
  33.5 0.6 iota_and_fusion
  34.1 14.9 %all-to-all-done = bf16[16,2,8,3072]{3,2,1,0:T(8,128)(2,1)} async-done(((bf16[16,2,8,3072]{3,2,1,0:T(8,128)(2,1)}), bf16[16,2,8,3072]{3,2,1,0:T(8,128)(2,1)}, u32[]{:S(2)}, u32[]{:S(2)}) %all-to-all-start) | async-done | bytes 1572896 | tf_op jit(solution)/shard_map/all_to_all | solution.py:131
  49.0 3.1 fusion.18
  52.3 0.6 fusion.90
  52.9 0.8 multiply_convert_fusion.1
  53.7 23.2 %all-gather.3.cloned.1.call-done = bf16[64,8,3072]{2,1,0:T(8,128)(2,1)} async-done(((bf16[4,8,3072]{2,1,0:T(8,128)(2,1)}), bf16[64,8,3072]{2,1,0:T(8,128)(2,1)}) %all-gather.3.cloned.1.call-update) | async-done | bytes 3145744 | tf_op jit(solution)/shard_map/all_gather | solution.py:128
  76.9 4.4 %fusion.13 = f32[64,8,3,1,128]{4,1,2,0,3:T(8,128)S(1)} fusion(bf16[3072,3,128]{0,2,1:T(8,128)(2,1)} %copy.80, bf16[64,8,3072]{2,1,0:T(8,128)(2,1)} %all-gather.3.cloned.1.call-done), kind=kOutput, calls=%fused_computation.20 | convolution fusion | flops 1207959552 | bytes 6291456 | tf_op jit(solution)/shard_map/dot_general | solution.py:148
  81.4 0.8 multiply_reduce_fusion.2
  82.2 0.8 copy.82
  83.0 0.7 copy.83
  83.7 0.8 copy.88
  84.6 0.7 copy.89
  85.3 1.0 multiply_multiply_fusion.2
  86.7 2.1 fusion.65
  89.2 1.1 pad_maximum_fusion
  90.2 7.5 %all-to-all-start.1 = ((bf16[16,240,1,128]{3,1,2,0:T(8,128)(2,1)}), bf16[16,240,1,128]{3,1,2,0:T(8,128)(2,1)}, u32[]{:S(2)}, u32[]{:S(2)}) async-start(bf16[16,240,1,128]{3,1,2,0:T(8,128)(2,1)} %pad_maximum_fusion), calls=%async_computation.1 | async-start | bytes 1966080 | tf_op jit(solution)/shard_map/all_to_all | solution.py:181
  98.3 0.7 fusion.100
  99.0 22.2 %all-to-all-done.1 = bf16[16,240,1,128]{3,1,2,0:T(8,128)(2,1)} async-done(((bf16[16,240,1,128]{3,1,2,0:T(8,128)(2,1)}), bf16[16,240,1,128]{3,1,2,0:T(8,128)(2,1)}, u32[]{:S(2)}, u32[]{:S(2)}) %all-to-all-start.1) | async-done | bytes 983072 | tf_op jit(solution)/shard_map/all_to_all | solution.py:181
  121.2 1.2 fusion.110
  122.3 0.9 slice.176
  123.3 0.9 select_reduce_fusion
  124.2 1.1 fusion.1
  125.3 0.9 fusion.24
  126.2 15.0 %all_to_all.30 = bf16[16,48,128]{2,1,0:T(8,128)(2,1)S(1)} all-to-all(bf16[16,48,128]{2,1,0:T(8,128)(2,1)S(1)} %bitcast.211), channel_id=1, replica_groups=mesh['tile'=16,'tensor'=16] {'tile'}, dimensions={0} | all-to-all | bytes 393216 | tf_op jit(solution)/shard_map/all_to_all | solution.py:209
  141.2 0.7 copy-done.6
  142.0 2.7 convolution_convert_fusion
  144.6 4.7 %all-to-all-start.3 = ((bf16[16,4,8,3072]{3,2,1,0:T(8,128)(2,1)}), bf16[16,4,8,3072]{3,2,1,0:T(8,128)(2,1)}, u32[]{:S(2)}, u32[]{:S(2)}) async-start(bf16[16,4,8,3072]{3,2,1,0:T(8,128)(2,1)} %bitcast.199), calls=%async_computation.3 | async-start | bytes 6291456 | tf_op jit(solution)/shard_map/all_to_all | solution.py:87
  149.5 0.7 slice_bitcast_fusion.6
  150.2 48.8 %all-to-all-done.3 = bf16[16,4,8,3072]{3,2,1,0:T(8,128)(2,1)} async-done(((bf16[16,4,8,3072]{3,2,1,0:T(8,128)(2,1)}), bf16[16,4,8,3072]{3,2,1,0:T(8,128)(2,1)}, u32[]{:S(2)}, u32[]{:S(2)}) %all-to-all-start.3) | async-done | bytes 3145760 | tf_op jit(solution)/shard_map/all_to_all | solution.py:87
  199.0 2.5 convert_reduce_fusion.1
  201.5 0.8 copy-done.1
  202.7 0.8 fusion.50
  203.5 48.5 %all-gather.5.cloned.1.call-done = bf16[64,8,3072]{2,1,0:T(8,128)(2,1)} async-done(((bf16[4,8,3072]{2,1,0:T(8,128)(2,1)}), bf16[64,8,3072]{2,1,0:T(8,128)(2,1)}) %all-gather.5.cloned.1.call-update) | async-done | bytes 3145744 | tf_op jit(solution)/shard_map/all_gather | solution.py:224
  252.1 7.8 %convolution_convert_fusion.1 = bf16[512,3072]{1,0:T(8,128)(2,1)} fusion(bf16[384,3072]{1,0:T(8,128)(2,1)S(1)} %copy-done, bf16[3072,384]{1,0:T(8,128)(2,1)} %param.33, bf16[64,8,3072]{2,1,0:T(8,128)(2,1)} %all-gather.5.cloned.1.call-done), kind=kOutput, calls=%fused_computation.5 | convolution fusion | flops 2419261440 | bytes 11010048 | tf_op jit(solution)/shard_map/dot_general | solution.py:227
  259.8 4.7 %all-to-all-start.4 = ((bf16[16,4,8,3072]{3,2,1,0:T(8,128)(2,1)}), bf16[16,4,8,3072]{3,2,1,0:T(8,128)(2,1)}, u32[]{:S(2)}, u32[]{:S(2)}) async-start(bf16[16,4,8,3072]{3,2,1,0:T(8,128)(2,1)} %bitcast.201), calls=%async_computation.4 | async-start | bytes 6291456 | tf_op jit(solution)/shard_map/all_to_all | solution.py:87
  264.5 0.6 divide_subtract_fusion
  265.3 0.7 copy_bitcast_fusion
  266.0 45.7 %all-to-all-done.4 = bf16[16,4,8,3072]{3,2,1,0:T(8,128)(2,1)} async-done(((bf16[16,4,8,3072]{3,2,1,0:T(8,128)(2,1)}), bf16[16,4,8,3072]{3,2,1,0:T(8,128)(2,1)}, u32[]{:S(2)}, u32[]{:S(2)}) %all-to-all-start.4) | async-done | bytes 3145760 | tf_op jit(solution)/shard_map/all_to_all | solution.py:87
  311.7 2.6 convert_reduce_fusion
  314.8 1.0 convert_reduce_fusion.4
  316.7 2.7 fusion
  319.4 4.5 %all-to-all-start.5 = ((bf16[16,2,8,3072]{3,2,1,0:T(8,128)(2,1)}), bf16[16,2,8,3072]{3,2,1,0:T(8,128)(2,1)}, u32[]{:S(2)}, u32[]{:S(2)}) async-start(bf16[16,2,8,3072]{3,2,1,0:T(8,128)(2,1)} %bitcast.200), calls=%async_computation.5 | async-start | bytes 3145728 | tf_op jit(solution)/shard_map/all_to_all | solution.py:87
  323.9 1.4 convolution_bitcast_fusion
  325.4 0.8 multiply_add_fusion.1
  326.2 1.9 collective-permute-start
  328.1 3.6 %collective-permute-start.1 = (f32[8,1,128]{2,1,0:T(1,128)S(1)}, f32[8,1,128]{2,1,0:T(1,128)S(1)}, u32[]{:S(2)}, u32[]{:S(2)}) collective-permute-start(f32[8,1,128]{2,1,0:T(1,128)S(1)} %get-tuple-element.52), channel_id=1, source_target_pairs={{16,0},{32,16},{48,32},{64,48},{80,64},{96,80},{112,96},{128,112},... | collective-permute-start | bytes 12296 | tf_op jit(solution)/shard_map/ppermute | solution.py:25
  331.8 1.1 fusion.57
  332.9 0.9 copy.96
  333.8 0.6 pad_maximum_fusion.1
  334.4 12.1 %all-to-all-done.5 = bf16[16,2,8,3072]{3,2,1,0:T(8,128)(2,1)} async-done(((bf16[16,2,8,3072]{3,2,1,0:T(8,128)(2,1)}), bf16[16,2,8,3072]{3,2,1,0:T(8,128)(2,1)}, u32[]{:S(2)}, u32[]{:S(2)}) %all-to-all-start.5) | async-done | bytes 1572896 | tf_op jit(solution)/shard_map/all_to_all | solution.py:87
  346.5 1.6 convert_reduce_fusion.2
  348.2 0.7 copy.97
  (95 shorter events, 5.1 us)
Async XLA Ops:
  7.2 244.9 %copy-start = (bf16[384,3072]{1,0:T(8,128)(2,1)S(1)}, bf16[384,3072]{1,0:T(8,128)(2,1)}, u32[]{:S(2)}) copy-start(bf16[384,3072]{1,0:T(8,128)(2,1)} %param.34) | copy-start | bytes 7077892
  7.2 5.1 %copy-start.2 = (bf16[8,2,3072]{2,1,0:T(2,128)(2,1)S(1)}, bf16[8,2,3072]{2,1,0:T(2,128)(2,1)}, u32[]{:S(2)}) copy-start(bf16[8,2,3072]{2,1,0:T(2,128)(2,1)} %param.19) | copy-start | bytes 294916
  7.2 5.2 %copy-start.10 = (f32[8,3,3072]{2,0,1:T(8,128)S(1)}, f32[8,3,3072]{2,0,1:T(8,128)}, u32[]{:S(2)}) copy-start(f32[8,3,3072]{2,0,1:T(8,128)} %param.25) | copy-start | bytes 884740
  7.2 69.7 %all-gather.3.cloned.1.call-start = ((), (), s32[]{:S(2)}) async-start(), calls=%async_computation.6 | async-start | bytes 3342336 | tf_op jit(solution)/shard_map/all_gather | solution.py:128
  14.5 34.4 %all-to-all-start = ((bf16[16,2,8,3072]{3,2,1,0:T(8,128)(2,1)}), bf16[16,2,8,3072]{3,2,1,0:T(8,128)(2,1)}, u32[]{:S(2)}, u32[]{:S(2)}) async-start(bf16[16,2,8,3072]{3,2,1,0:T(8,128)(2,1)} %broadcast_in_dim.42), calls=%async_computation | async-start | bytes 3145728 | tf_op jit(solution)/shard_map/all_to_all | solution.py:131
  21.6 4.4 %copy-start.20 = (s32[8,2]{0,1:T(2,128)S(1)}, s32[8,2]{0,1:T(2,128)}, u32[]{:S(2)}) copy-start(s32[8,2]{0,1:T(2,128)} %param.22) | copy-start | bytes 196
  25.9 8.1 %copy-start.19 = (f32[2,2,128]{2,1,0:T(2,128)S(1)}, f32[2,2,128]{2,1,0:T(2,128)}, u32[]{:S(2)}) copy-start(f32[2,2,128]{2,1,0:T(2,128)} %param.32) | copy-start | bytes 6148
  85.3 1.4 copy-start.16
  85.3 1.5 copy-start.17
  86.5 2.4 copy-start.14
  86.5 2.4 copy-start.13
  86.5 2.5 copy-start.12
  88.9 8.8 %copy-start.21 = (s32[8]{0:T(128)S(1)}, s32[8]{0:T(128)}, u32[]{:S(2)}) copy-start(s32[8]{0:T(128)} %param.23) | copy-start | bytes 100
  90.2 30.9 %all-to-all-start.1 = ((bf16[16,240,1,128]{3,1,2,0:T(8,128)(2,1)}), bf16[16,240,1,128]{3,1,2,0:T(8,128)(2,1)}, u32[]{:S(2)}, u32[]{:S(2)}) async-start(bf16[16,240,1,128]{3,1,2,0:T(8,128)(2,1)} %pad_maximum_fusion), calls=%async_computation.1 | async-start | bytes 1966080 | tf_op jit(solution)/shard_map/all_to_all | solution.py:181
  125.3 16.7 %copy-start.7 = (bf16[128,3072]{1,0:T(8,128)(2,1)S(1)}, bf16[128,3072]{1,0:T(8,128)(2,1)}, u32[]{:S(2)}) copy-start(bf16[128,3072]{1,0:T(8,128)(2,1)} %param.30) | copy-start | bytes 2359300
  141.2 0.7 copy-start.6
  144.6 4.9 %copy-start.11 = (f32[8,3,3072]{2,0,1:T(8,128)S(1)}, f32[8,3,3072]{2,0,1:T(8,128)}, u32[]{:S(2)}) copy-start(f32[8,3,3072]{2,0,1:T(8,128)} %param.26) | copy-start | bytes 884740
  144.6 54.4 %all-to-all-start.3 = ((bf16[16,4,8,3072]{3,2,1,0:T(8,128)(2,1)}), bf16[16,4,8,3072]{3,2,1,0:T(8,128)(2,1)}, u32[]{:S(2)}, u32[]{:S(2)}) async-start(bf16[16,4,8,3072]{3,2,1,0:T(8,128)(2,1)} %bitcast.199), calls=%async_computation.3 | async-start | bytes 6291456 | tf_op jit(solution)/shard_map/all_to_all | solution.py:87
  149.3 53.0 %copy-start.4 = (f32[8,3072]{1,0:T(8,128)S(1)}, f32[8,3072]{1,0:T(8,128)}, u32[]{:S(2)}) copy-start(f32[8,3072]{1,0:T(8,128)} %get-tuple-element.36) | copy-start | bytes 294916
  149.3 102.7 %all-gather.5.cloned.1.call-start = ((), (), s32[]{:S(2)}) async-start(), calls=%async_computation.7 | async-start | bytes 3342336 | tf_op jit(solution)/shard_map/all_gather | solution.py:224
  201.5 0.8 copy-start.1
  259.8 4.7 %copy-start.22 = (s32[8]{0:T(128)S(1)}, s32[8]{0:T(128)}, u32[]{:S(2)}) copy-start(s32[8]{0:T(128)} %param.21) | copy-start | bytes 100
  259.8 5.3 %copy-start.15 = (f32[8,2,3072]{2,1,0:T(2,128)S(1)}, f32[8,2,3072]{2,1,0:T(2,128)}, u32[]{:S(2)}) copy-start(f32[8,2,3072]{2,1,0:T(2,128)} %param.27) | copy-start | bytes 589828
  259.8 51.9 %all-to-all-start.4 = ((bf16[16,4,8,3072]{3,2,1,0:T(8,128)(2,1)}), bf16[16,4,8,3072]{3,2,1,0:T(8,128)(2,1)}, u32[]{:S(2)}, u32[]{:S(2)}) async-start(bf16[16,4,8,3072]{3,2,1,0:T(8,128)(2,1)} %bitcast.201), calls=%async_computation.4 | async-start | bytes 6291456 | tf_op jit(solution)/shard_map/all_to_all | solution.py:87
  311.7 5.0 %copy-start.8 = (bf16[128,3072]{1,0:T(8,128)(2,1)S(1)}, bf16[128,3072]{1,0:T(8,128)(2,1)}, u32[]{:S(2)}) copy-start(bf16[128,3072]{1,0:T(8,128)(2,1)} %param.31) | copy-start | bytes 2359300
  316.7 8.7 %copy-start.18 = (f32[8,2,128]{2,1,0:T(2,128)S(1)}, f32[8,2,128]{2,1,0:T(2,128)}, u32[]{:S(2)}) copy-start(f32[8,2,128]{2,1,0:T(2,128)} %param.20) | copy-start | bytes 24580
  316.7 15.1 %copy-start.5 = (f32[8,3072]{1,0:T(8,128)S(1)}, f32[8,3072]{1,0:T(8,128)}, u32[]{:S(2)}) copy-start(f32[8,3072]{1,0:T(8,128)} %get-tuple-element.36) | copy-start | bytes 294916
  319.4 28.8 %copy-start.3 = (bf16[8,2,3072]{2,1,0:T(2,128)(2,1)S(1)}, bf16[8,2,3072]{2,1,0:T(2,128)(2,1)}, u32[]{:S(2)}) copy-start(bf16[8,2,3072]{2,1,0:T(2,128)(2,1)} %param.19) | copy-start | bytes 294916
  319.4 27.1 %all-to-all-start.5 = ((bf16[16,2,8,3072]{3,2,1,0:T(8,128)(2,1)}), bf16[16,2,8,3072]{3,2,1,0:T(8,128)(2,1)}, u32[]{:S(2)}, u32[]{:S(2)}) async-start(bf16[16,2,8,3072]{3,2,1,0:T(8,128)(2,1)} %bitcast.200), calls=%async_computation.5 | async-start | bytes 3145728 | tf_op jit(solution)/shard_map/all_to_all | solution.py:87
  325.3 22.9 %copy-start.9 = (f32[8,3072]{1,0:T(8,128)S(1)}, f32[8,3072]{1,0:T(8,128)}, u32[]{:S(2)}) copy-start(f32[8,3072]{1,0:T(8,128)} %get-tuple-element.30) | copy-start | bytes 294916
  326.2 7.6 %collective-permute-start = (f32[8,1,128]{2,1,0:T(1,128)S(1)}, f32[8,1,128]{2,1,0:T(1,128)S(1)}, u32[]{:S(2)}, u32[]{:S(2)}) collective-permute-start(f32[8,1,128]{2,1,0:T(1,128)S(1)} %get-tuple-element.51), channel_id=1, source_target_pairs={{0,16},{16,32},{32,48},{48,64},{64,80},{80,96},{96,112},{112,128},... | collective-permute-start | bytes 12296 | tf_op jit(solution)/shard_map/ppermute | solution.py:24
  328.1 5.6 %collective-permute-start.1 = (f32[8,1,128]{2,1,0:T(1,128)S(1)}, f32[8,1,128]{2,1,0:T(1,128)S(1)}, u32[]{:S(2)}, u32[]{:S(2)}) collective-permute-start(f32[8,1,128]{2,1,0:T(1,128)S(1)} %get-tuple-element.52), channel_id=1, source_target_pairs={{16,0},{32,16},{48,32},{64,48},{80,64},{96,80},{112,96},{128,112},... | collective-permute-start | bytes 12296 | tf_op jit(solution)/shard_map/ppermute | solution.py:25
Sparse Core Ops, SparseCore 0:
  11.3 65.5 all-gather.2
  203.6 48.3 all-gather.4

commit v11 on v6

--- a/solution.py
+++ b/solution.py
@@ -142,34 +142,37 @@
     col_ids = (anchor[None, :, 1] + (owner * tile_cols + within % tile_cols)[:, None]).astype(
         jnp.float32
     )
-    cos_table, sin_table = rope_tables(row_ids, col_ids)
-    cos_table = cos_table[:, :, None, :]
-    sin_table = sin_table[:, :, None, :]
+    cos_table, sin_table = rope_tables(row_ids.reshape(-1), col_ids.reshape(-1))
+    cos_table = cos_table[:, None, :]
+    sin_table = sin_table[:, None, :]
     image_qkv = jnp.dot(
         image_mod, qkv_image.reshape(model_width, 3 * local_cols), preferred_element_type=jnp.float32
-    ).reshape(image_count, requests, 3, local_heads, HEAD_DIM)
+    ).reshape(image_count * requests, 3, local_heads, HEAD_DIM)
     text_qkv = jnp.dot(
         text_mod, qkv_text.reshape(model_width, 3 * local_cols), preferred_element_type=jnp.float32
-    ).reshape(text_tile, requests, 3, local_heads, HEAD_DIM)
+    ).reshape(text_tile * requests, 3, local_heads, HEAD_DIM)
+    token_shape = (block_len, requests, local_heads, HEAD_DIM)
     query = jnp.concatenate(
         [
-            head_norm(text_qkv[:, :, 0], qk_gain[1, 0]).astype(jnp.bfloat16),
-            rotate(head_norm(image_qkv[:, :, 0], qk_gain[0, 0]), cos_table, sin_table).astype(
+            head_norm(text_qkv[:, 0], qk_gain[1, 0]).astype(jnp.bfloat16),
+            rotate(head_norm(image_qkv[:, 0], qk_gain[0, 0]), cos_table, sin_table).astype(
                 jnp.bfloat16
             ),
         ],
         0,
-    )
+    ).reshape(token_shape)
     keys = jnp.concatenate(
         [
-            head_norm(text_qkv[:, :, 1], qk_gain[1, 1]).astype(jnp.bfloat16),
-            rotate(head_norm(image_qkv[:, :, 1], qk_gain[0, 1]), cos_table, sin_table).astype(
+            head_norm(text_qkv[:, 1], qk_gain[1, 1]).astype(jnp.bfloat16),
+            rotate(head_norm(image_qkv[:, 1], qk_gain[0, 1]), cos_table, sin_table).astype(
                 jnp.bfloat16
             ),
         ],
         0,
-    )
-    values = jnp.concatenate([text_qkv[:, :, 2], image_qkv[:, :, 2]], 0).astype(jnp.bfloat16)
+    ).reshape(token_shape)
+    values = (
+        jnp.concatenate([text_qkv[:, 2], image_qkv[:, 2]], 0).astype(jnp.bfloat16).reshape(token_shape)
+    )
     score_scale = 1.0 / math.sqrt(HEAD_DIM)
     tiles = lax.axis_size("tile")
     parts = tiles // requests

time: 345 us -> 345 us (level)
    unnamed x52 -> x50, local copies, waits for them, and re-layouts: 11 us -> 11 us
  transfers between devices with their start and end apart: 9 -> 9, of which waited for: 6 -> 6; matrix products, arithmetic and copies ran while one was open for 12% -> 11% of each run, Pallas kernels for 0% -> 0%
where the time goes in v11:
time: 345 us; the launch traced here: 341 us
  waiting for transfers between devices  204 us (59%)
  starting transfers between devices  34.2 us (10%)
  other arithmetic  27.1 us (8%)
  matrix products  23.7 us (7%)
  local copies, waits for them, and re-layouts  21.9 us (6%)
  between operations  15.2 us (4%)
  blocking collectives  15 us (4%)
    all_to_all x3, waiting for transfers between devices, sum_over_tensor(): parts = lax.all_to_all(parts, 'tensor', 0, 0, tiled=True)  91.5 us
    all_gather x1, waiting for transfers between devices, per_device(): piece = lax.all_gather(mlp_mod, 'tensor', axis=0, tiled=True)  50.4 us
    all_gather x1, waiting for transfers between devices, per_device(): lax.all_gather(image_mod_own, 'tensor', axis=0, tiled=True)  23.3 us
    all_to_all x1, waiting for transfers between devices, per_device(): incoming = lax.all_to_all(outgoing, 'tile', 0, 0, tiled=True)  22.2 us
    all_to_all x1, waiting for transfers between devices, per_device(): lax.all_to_all(jnp.broadcast_to(text_mod_own[None], (owners,) + text_mod_...  16.2 us
    all_to_all x1, blocking collectives, per_device(): returned = lax.all_to_all(attended_mine, 'tile', 0, 0, tiled=True)  15 us
    all_to_all x3, starting transfers between devices, sum_over_tensor(): parts = lax.all_to_all(parts, 'tensor', 0, 0, tiled=True)  13.8 us
    unnamed x50, local copies, waits for them, and re-layouts  11 us
  transfers between devices with their start and end apart: 9, of which 6 were waited for; matrix products, arithmetic and copies ran while one was open for 11% of the time, Pallas kernels for 0%

profile of v11, /device:TPU:32, one launch (start us, length us, event | category | flops | bytes accessed | tf_op | source)
XLA Modules:
  0.0 340.7 jit_solution(16405498130412113823)
XLA Ops:
  7.2 1.1 copy.54
  8.7 1.0 slice_bitcast_fusion.9
  9.7 0.8 add_convert_fusion.1
  10.6 1.0 fusion.66
  11.8 0.7 slice_bitcast_fusion.4
  12.6 1.3 broadcast_in_dim.42
  13.9 7.1 %all-to-all-start = ((bf16[16,2,8,3072]{3,2,1,0:T(8,128)(2,1)}), bf16[16,2,8,3072]{3,2,1,0:T(8,128)(2,1)}, u32[]{:S(2)}, u32[]{:S(2)}) async-start(bf16[16,2,8,3072]{3,2,1,0:T(8,128)(2,1)} %broadcast_in_dim.42), calls=%async_computation | async-start | bytes 3145728 | tf_op jit(solution)/shard_map/all_to_all | solution.py:131
  21.0 4.3 %copy.57 = bf16[3072,3,128]{0,2,1:T(8,128)(2,1)} copy(bf16[3072,3,128]{2,0,1:T(8,128)(2,1)} %param.28) | data formatting | bytes 4718592 | tf_op args[10]
  25.6 4.3 %copy.56 = bf16[3072,3,128]{0,2,1:T(8,128)(2,1)} copy(bf16[3072,3,128]{2,0,1:T(8,128)(2,1)} %param.29) | data formatting | bytes 4718592 | tf_op args[11]
  29.9 0.6 and_select_fusion.2
  30.5 0.5 compare_and_fusion
  31.0 0.6 compare_select_fusion
  31.6 0.6 iota_and_fusion
  32.2 16.2 %all-to-all-done = bf16[16,2,8,3072]{3,2,1,0:T(8,128)(2,1)} async-done(((bf16[16,2,8,3072]{3,2,1,0:T(8,128)(2,1)}), bf16[16,2,8,3072]{3,2,1,0:T(8,128)(2,1)}, u32[]{:S(2)}, u32[]{:S(2)}) %all-to-all-start) | async-done | bytes 1572896 | tf_op jit(solution)/shard_map/all_to_all | solution.py:131
  48.4 3.1 fusion.13
  51.9 0.7 copy.65
  52.7 0.7 copy.62
  53.4 23.3 %all-gather.3.cloned.1.call-done = bf16[64,8,3072]{2,1,0:T(8,128)(2,1)} async-done(((bf16[4,8,3072]{2,1,0:T(8,128)(2,1)}), bf16[64,8,3072]{2,1,0:T(8,128)(2,1)}) %all-gather.3.cloned.1.call-update) | async-done | bytes 3145744 | tf_op jit(solution)/shard_map/all_gather | solution.py:128
  76.7 4.0 %fusion.3 = f32[512,3,128]{0,2,1:T(8,128)S(1)} fusion(bf16[64,8,3072]{2,1,0:T(8,128)(2,1)} %all-gather.3.cloned.1.call-done, bf16[3072,3,128]{0,2,1:T(8,128)(2,1)} %copy.57), kind=kOutput, calls=%fused_computation.10 | convolution fusion | flops 1207959552 | bytes 6291456 | tf_op jit(solution)/shard_map/dot_general | solution.py:148
  81.2 0.7 fusion.83
  81.9 2.1 fusion.60
  84.2 0.9 pad_maximum_fusion.3
  85.3 0.7 copy.67
  86.0 0.9 pad_maximum_fusion.2
  87.3 2.0 pad_maximum_fusion
  89.3 7.5 %all-to-all-start.1 = ((bf16[16,240,1,128]{3,1,2,0:T(8,128)(2,1)}), bf16[16,240,1,128]{3,1,2,0:T(8,128)(2,1)}, u32[]{:S(2)}, u32[]{:S(2)}) async-start(bf16[16,240,1,128]{3,1,2,0:T(8,128)(2,1)} %pad_maximum_fusion), calls=%async_computation.1 | async-start | bytes 1966080 | tf_op jit(solution)/shard_map/all_to_all | solution.py:184
  96.8 0.6 dynamic_slice.3
  97.4 0.7 fusion.95
  98.1 22.2 %all-to-all-done.1 = bf16[16,240,1,128]{3,1,2,0:T(8,128)(2,1)} async-done(((bf16[16,240,1,128]{3,1,2,0:T(8,128)(2,1)}), bf16[16,240,1,128]{3,1,2,0:T(8,128)(2,1)}, u32[]{:S(2)}, u32[]{:S(2)}) %all-to-all-start.1) | async-done | bytes 983072 | tf_op jit(solution)/shard_map/all_to_all | solution.py:184
  120.2 1.2 fusion.105
  121.4 0.9 slice.176
  122.4 0.9 select_reduce_fusion
  123.2 1.1 fusion.1
  124.3 0.9 fusion.19
  125.3 15.0 %all_to_all.30 = bf16[16,48,128]{2,1,0:T(8,128)(2,1)S(1)} all-to-all(bf16[16,48,128]{2,1,0:T(8,128)(2,1)S(1)} %bitcast.211), channel_id=1, replica_groups=mesh['tile'=16,'tensor'=16] {'tile'}, dimensions={0} | all-to-all | bytes 393216 | tf_op jit(solution)/shard_map/all_to_all | solution.py:212
  140.3 0.7 copy-done.3
  141.0 2.6 convolution_convert_fusion
  143.6 4.7 %all-to-all-start.3 = ((bf16[16,4,8,3072]{3,2,1,0:T(8,128)(2,1)}), bf16[16,4,8,3072]{3,2,1,0:T(8,128)(2,1)}, u32[]{:S(2)}, u32[]{:S(2)}) async-start(bf16[16,4,8,3072]{3,2,1,0:T(8,128)(2,1)} %bitcast.191), calls=%async_computation.3 | async-start | bytes 6291456 | tf_op jit(solution)/shard_map/all_to_all | solution.py:87
  148.3 0.2 all-gather.5.cloned.1.call-start
  148.6 0.7 slice_bitcast_fusion.6
  149.3 48.7 %all-to-all-done.3 = bf16[16,4,8,3072]{3,2,1,0:T(8,128)(2,1)} async-done(((bf16[16,4,8,3072]{3,2,1,0:T(8,128)(2,1)}), bf16[16,4,8,3072]{3,2,1,0:T(8,128)(2,1)}, u32[]{:S(2)}, u32[]{:S(2)}) %all-to-all-start.3) | async-done | bytes 3145760 | tf_op jit(solution)/shard_map/all_to_all | solution.py:87
  198.0 2.5 convert_reduce_fusion.1
  200.7 0.2 fusion.42
  201.0 0.8 fusion.45
  201.8 0.5 slice.179
  203.0 3.0 fusion
  206.0 4.4 %all-to-all-start.5 = ((bf16[16,2,8,3072]{3,2,1,0:T(8,128)(2,1)}), bf16[16,2,8,3072]{3,2,1,0:T(8,128)(2,1)}, u32[]{:S(2)}, u32[]{:S(2)}) async-start(bf16[16,2,8,3072]{3,2,1,0:T(8,128)(2,1)} %bitcast.192), calls=%async_computation.5 | async-start | bytes 3145728 | tf_op jit(solution)/shard_map/all_to_all | solution.py:87
  210.4 50.4 %all-gather.5.cloned.1.call-done = bf16[64,8,3072]{2,1,0:T(8,128)(2,1)} async-done(((bf16[4,8,3072]{2,1,0:T(8,128)(2,1)}), bf16[64,8,3072]{2,1,0:T(8,128)(2,1)}) %all-gather.5.cloned.1.call-update) | async-done | bytes 3145744 | tf_op jit(solution)/shard_map/all_gather | solution.py:229
  260.8 7.8 %convolution_convert_fusion.1 = bf16[512,3072]{1,0:T(8,128)(2,1)} fusion(bf16[384,3072]{1,0:T(8,128)(2,1)S(1)} %copy-done, bf16[3072,384]{1,0:T(8,128)(2,1)} %param.33, bf16[64,8,3072]{2,1,0:T(8,128)(2,1)} %all-gather.5.cloned.1.call-done), kind=kOutput, calls=%fused_computation.5 | convolution fusion | flops 2419261440 | bytes 11010048 | tf_op jit(solution)/shard_map/dot_general | solution.py:235
  268.6 4.7 %all-to-all-start.4 = ((bf16[16,4,8,3072]{3,2,1,0:T(8,128)(2,1)}), bf16[16,4,8,3072]{3,2,1,0:T(8,128)(2,1)}, u32[]{:S(2)}, u32[]{:S(2)}) async-start(bf16[16,4,8,3072]{3,2,1,0:T(8,128)(2,1)} %bitcast.193), calls=%async_computation.4 | async-start | bytes 6291456 | tf_op jit(solution)/shard_map/all_to_all | solution.py:87
  273.3 1.2 fusion.110
  274.5 0.7 copy_bitcast_fusion
  275.2 1.6 convert_reduce_fusion.2
  276.9 0.7 copy.74
  277.6 42.8 %all-to-all-done.4 = bf16[16,4,8,3072]{3,2,1,0:T(8,128)(2,1)} async-done(((bf16[16,4,8,3072]{3,2,1,0:T(8,128)(2,1)}), bf16[16,4,8,3072]{3,2,1,0:T(8,128)(2,1)}, u32[]{:S(2)}, u32[]{:S(2)}) %all-to-all-start.4) | async-done | bytes 3145760 | tf_op jit(solution)/shard_map/all_to_all | solution.py:87
  320.4 2.5 convert_reduce_fusion
  322.9 1.0 convert_reduce_fusion.4
  324.0 0.2 fusion.46
  324.2 1.3 convolution_bitcast_fusion
  325.7 1.9 collective-permute-start
  327.6 3.6 %collective-permute-start.1 = (f32[8,1,128]{2,1,0:T(1,128)S(1)}, f32[8,1,128]{2,1,0:T(1,128)S(1)}, u32[]{:S(2)}, u32[]{:S(2)}) collective-permute-start(f32[8,1,128]{2,1,0:T(1,128)S(1)} %get-tuple-element.34), channel_id=1, source_target_pairs={{16,0},{32,16},{48,32},{64,48},{80,64},{96,80},{112,96},{128,112},... | collective-permute-start | bytes 12296 | tf_op jit(solution)/shard_map/ppermute | solution.py:25
  331.3 1.1 fusion.52
  332.4 0.9 copy.73
  333.2 0.6 pad_maximum_fusion.4
  (100 shorter events, 2.9 us)
Async XLA Ops:
  7.2 253.6 %copy-start = (bf16[384,3072]{1,0:T(8,128)(2,1)S(1)}, bf16[384,3072]{1,0:T(8,128)(2,1)}, u32[]{:S(2)}) copy-start(bf16[384,3072]{1,0:T(8,128)(2,1)} %param.34) | copy-start | bytes 7077892
  7.2 4.4 %copy-start.2 = (bf16[8,2,3072]{2,1,0:T(2,128)(2,1)S(1)}, bf16[8,2,3072]{2,1,0:T(2,128)(2,1)}, u32[]{:S(2)}) copy-start(bf16[8,2,3072]{2,1,0:T(2,128)(2,1)} %param.19) | copy-start | bytes 294916
  7.2 4.6 %copy-start.10 = (f32[8,3,3072]{2,0,1:T(8,128)S(1)}, f32[8,3,3072]{2,0,1:T(8,128)}, u32[]{:S(2)}) copy-start(f32[8,3,3072]{2,0,1:T(8,128)} %param.25) | copy-start | bytes 884740
  7.2 69.5 %all-gather.3.cloned.1.call-start = ((), (), s32[]{:S(2)}) async-start(), calls=%async_computation.6 | async-start | bytes 3342336 | tf_op jit(solution)/shard_map/all_gather | solution.py:128
  13.9 34.5 %all-to-all-start = ((bf16[16,2,8,3072]{3,2,1,0:T(8,128)(2,1)}), bf16[16,2,8,3072]{3,2,1,0:T(8,128)(2,1)}, u32[]{:S(2)}, u32[]{:S(2)}) async-start(bf16[16,2,8,3072]{3,2,1,0:T(8,128)(2,1)} %broadcast_in_dim.42), calls=%async_computation | async-start | bytes 3145728 | tf_op jit(solution)/shard_map/all_to_all | solution.py:131
  21.0 4.3 %copy-start.14 = (s32[8,2]{0,1:T(2,128)S(1)}, s32[8,2]{0,1:T(2,128)}, u32[]{:S(2)}) copy-start(s32[8,2]{0,1:T(2,128)} %param.22) | copy-start | bytes 196
  25.3 6.9 %copy-start.13 = (f32[2,2,128]{2,1,0:T(2,128)S(1)}, f32[2,2,128]{2,1,0:T(2,128)}, u32[]{:S(2)}) copy-start(f32[2,2,128]{2,1,0:T(2,128)} %param.32) | copy-start | bytes 6148
  80.8 1.1 copy-start.15
  80.8 1.1 copy-start.16
  80.8 1.1 copy-start.17
  80.8 1.1 copy-start.18
  80.8 1.0 copy-start.19
  80.8 1.0 copy-start.20
  86.0 10.8 %copy-start.21 = (s32[8]{0:T(128)S(1)}, s32[8]{0:T(128)}, u32[]{:S(2)}) copy-start(s32[8]{0:T(128)} %param.23) | copy-start | bytes 100
  89.3 31.0 %all-to-all-start.1 = ((bf16[16,240,1,128]{3,1,2,0:T(8,128)(2,1)}), bf16[16,240,1,128]{3,1,2,0:T(8,128)(2,1)}, u32[]{:S(2)}, u32[]{:S(2)}) async-start(bf16[16,240,1,128]{3,1,2,0:T(8,128)(2,1)} %pad_maximum_fusion), calls=%async_computation.1 | async-start | bytes 1966080 | tf_op jit(solution)/shard_map/all_to_all | solution.py:184
  124.3 16.7 %copy-start.4 = (bf16[128,3072]{1,0:T(8,128)(2,1)S(1)}, bf16[128,3072]{1,0:T(8,128)(2,1)}, u32[]{:S(2)}) copy-start(bf16[128,3072]{1,0:T(8,128)(2,1)} %param.30) | copy-start | bytes 2359300
  140.3 0.7 copy-start.3
  143.6 4.9 %copy-start.11 = (f32[8,3,3072]{2,0,1:T(8,128)S(1)}, f32[8,3,3072]{2,0,1:T(8,128)}, u32[]{:S(2)}) copy-start(f32[8,3,3072]{2,0,1:T(8,128)} %param.26) | copy-start | bytes 884740
  143.6 54.4 %all-to-all-start.3 = ((bf16[16,4,8,3072]{3,2,1,0:T(8,128)(2,1)}), bf16[16,4,8,3072]{3,2,1,0:T(8,128)(2,1)}, u32[]{:S(2)}, u32[]{:S(2)}) async-start(bf16[16,4,8,3072]{3,2,1,0:T(8,128)(2,1)} %bitcast.191), calls=%async_computation.3 | async-start | bytes 6291456 | tf_op jit(solution)/shard_map/all_to_all | solution.py:87
  148.3 112.4 %all-gather.5.cloned.1.call-start = ((), (), s32[]{:S(2)}) async-start(), calls=%async_computation.7 | async-start | bytes 3342336 | tf_op jit(solution)/shard_map/all_gather | solution.py:229
  198.0 3.0 copy-start.5
  198.0 3.0 copy-start.6
  200.5 5.4 %copy-start.1 = (f32[4,8,3072]{2,1,0:T(8,128)}, f32[4,8,3072]{2,1,0:T(8,128)S(1)}, u32[]{:S(2)}) copy-start(f32[4,8,3072]{2,1,0:T(8,128)S(1)} %convert_reduce_fusion.1) | copy-start | bytes 1179652
  206.0 62.6 %all-to-all-start.5 = ((bf16[16,2,8,3072]{3,2,1,0:T(8,128)(2,1)}), bf16[16,2,8,3072]{3,2,1,0:T(8,128)(2,1)}, u32[]{:S(2)}, u32[]{:S(2)}) async-start(bf16[16,2,8,3072]{3,2,1,0:T(8,128)(2,1)} %bitcast.192), calls=%async_computation.5 | async-start | bytes 3145728 | tf_op jit(solution)/shard_map/all_to_all | solution.py:87
  268.5 4.7 %copy-start.22 = (s32[8]{0:T(128)S(1)}, s32[8]{0:T(128)}, u32[]{:S(2)}) copy-start(s32[8]{0:T(128)} %param.21) | copy-start | bytes 100
  268.5 8.3 %copy-start.9 = (f32[8,3072]{1,0:T(8,128)S(1)}, f32[8,3072]{1,0:T(8,128)}, u32[]{:S(2)}) copy-start(f32[8,3072]{1,0:T(8,128)} %get-tuple-element.14) | copy-start | bytes 294916
  268.6 51.9 %all-to-all-start.4 = ((bf16[16,4,8,3072]{3,2,1,0:T(8,128)(2,1)}), bf16[16,4,8,3072]{3,2,1,0:T(8,128)(2,1)}, u32[]{:S(2)}, u32[]{:S(2)}) async-start(bf16[16,4,8,3072]{3,2,1,0:T(8,128)(2,1)} %bitcast.193), calls=%async_computation.4 | async-start | bytes 6291456 | tf_op jit(solution)/shard_map/all_to_all | solution.py:87
  276.8 48.8 %copy-start.12 = (f32[8,2,128]{2,1,0:T(2,128)S(1)}, f32[8,2,128]{2,1,0:T(2,128)}, u32[]{:S(2)}) copy-start(f32[8,2,128]{2,1,0:T(2,128)} %param.20) | copy-start | bytes 24580
  276.9 47.3 %copy-start.7 = (f32[8,3072]{1,0:T(8,128)S(1)}, f32[8,3072]{1,0:T(8,128)}, u32[]{:S(2)}) copy-start(f32[8,3072]{1,0:T(8,128)} %get-tuple-element.55) | copy-start | bytes 294916
  320.4 3.8 %copy-start.8 = (f32[8,3072]{1,0:T(8,128)S(1)}, f32[8,3072]{1,0:T(8,128)}, u32[]{:S(2)}) copy-start(f32[8,3072]{1,0:T(8,128)} %get-tuple-element.56) | copy-start | bytes 294916
  325.7 7.5 %collective-permute-start = (f32[8,1,128]{2,1,0:T(1,128)S(1)}, f32[8,1,128]{2,1,0:T(1,128)S(1)}, u32[]{:S(2)}, u32[]{:S(2)}) collective-permute-start(f32[8,1,128]{2,1,0:T(1,128)S(1)} %get-tuple-element.33), channel_id=1, source_target_pairs={{0,16},{16,32},{32,48},{48,64},{64,80},{80,96},{96,112},{112,128},... | collective-permute-start | bytes 12296 | tf_op jit(solution)/shard_map/ppermute | solution.py:24
  327.6 5.6 %collective-permute-start.1 = (f32[8,1,128]{2,1,0:T(1,128)S(1)}, f32[8,1,128]{2,1,0:T(1,128)S(1)}, u32[]{:S(2)}, u32[]{:S(2)}) collective-permute-start(f32[8,1,128]{2,1,0:T(1,128)S(1)} %get-tuple-element.34), channel_id=1, source_target_pairs={{16,0},{32,16},{48,32},{64,48},{80,64},{96,80},{112,96},{128,112},... | collective-permute-start | bytes 12296 | tf_op jit(solution)/shard_map/ppermute | solution.py:25
Sparse Core Ops, SparseCore 0:
  11.0 65.6 all-gather.2
  201.9 58.7 all-gather.4
